TPU v7x, 256 devices: a whole 4x4x8 slice. The times are simulated.
256 devices in a mesh: dp: 16 (over y, x), section: 2 (over core), tensor: 8 (over z).
Axes of the slice: x: 4, y: 4, z: 8, core: 2. Of those that a mesh axis runs over, the one named last changes fastest.
Arguments:
- tokens: bfloat16 [2048, 16384], P('dp'), may hold values from -9 to 9
- order: int32 [2048], replicated, may hold values from 0 to 2047, as said below
- segments: int32 [2048], replicated, may hold values from 0 to 1, as said below
- gain: float32 [2, 16384], P('section', 'dp'), may hold values from 0.1 to 1.9
- w_query: bfloat16 [2, 16384, 8192], P('section', 'dp', 'tensor'), may hold values from -0.046875 to 0.046875
- key_value_weight: bfloat16 [2, 16384, 8, 256], P('section', 'dp', 'tensor'), may hold values from -0.046875 to 0.046875
- w_out: bfloat16 [2, 8192, 16384], P('section', 'tensor', 'dp'), may hold values from -0.0625 to 0.0625
Outputs:
- layer_out: bfloat16 [2048, 16384], P('section', 'dp')
Inputs may be any that keep to these rules, and one draw needn't show every extreme that they name: A permutation that moves whole sentences: the rows of one sentence (a run of equal segments within a block of 32 rows) come from consecutive entry rows in order. `segments`: within each block of 32 rows the sentence numbers do not fall and each of 0 to 1 appears.
All inputs are finite; a program needn't handle non-finite values.
Results may differ from a plain program's by a relative error of at most 0.022.
Values may be sent and summed in bfloat16 or wider, within the bound.
No kernel may reach another device: no remote copies, remote signals or barrier semaphores. Data moves between devices by JAX's collectives and lax.ppermute only.
A program may use at most 64 MiB of HBM per device.

v0:
```python
import math

import jax
import jax.numpy as jnp
from jax import lax
from jax.sharding import PartitionSpec as P

MODEL_WIDTH = 16384
KEYVALUE_HEADS = 8
QUERY_HEADS = 64
MICRO_TOKENS = 32
M = 4


norm_epsilon = 1e-05


def passed_along(array, axis, by):
    count = lax.axis_size(axis)
    return lax.ppermute(array, axis, [(i, (i + by) % count) for i in range(count)])


def causal_block_attend(query_rows, key_value_rows, sentence_segment_rows, query_group_width):
    row_count = query_rows.shape[0]
    kv_heads = key_value_rows.shape[1]
    head_size = key_value_rows.shape[2] // 2
    query_head_rows = query_rows.reshape(row_count, kv_heads, query_group_width, head_size)
    key_heads = key_value_rows[:, :, :head_size]
    value_heads = key_value_rows[:, :, head_size:]
    scores = jnp.einsum(
        "qkgd,skd->kgqs", query_head_rows, key_heads, preferred_element_type=jnp.float32
    ) / math.sqrt(head_size)
    position = jnp.arange(row_count)
    allowed = (sentence_segment_rows[:, None] == sentence_segment_rows[None, :]) & (
        position[None, :] <= position[:, None]
    )
    raw_weights = jnp.where(allowed[None, None], jnp.exp(scores), 0.0)
    totals = jnp.sum(raw_weights, axis=-1, keepdims=True)
    probs = (raw_weights / totals).astype(jnp.bfloat16)
    attended_rows = jnp.einsum(
        "kgqs,skd->qkgd", probs, value_heads, preferred_element_type=jnp.float32
    )
    return attended_rows.astype(jnp.bfloat16).reshape(
        row_count, kv_heads * query_group_width * head_size
    )


def section_layer(
    hidden, sentence_segment_rows, gain_row, query_weight, key_value_matrix, out_weight
):
    slice_width = hidden.shape[1]
    own_rows = sentence_segment_rows.shape[0]
    own_start = lax.axis_index("dp") * own_rows
    widened = hidden.astype(jnp.float32)
    normed_rows = (widened * gain_row[None, :]).astype(jnp.bfloat16)
    query_terms = jnp.dot(normed_rows, query_weight, preferred_element_type=jnp.float32)
    keyval_terms = jnp.dot(
        normed_rows, key_value_matrix.reshape(slice_width, -1), preferred_element_type=jnp.float32
    )
    square_terms = jnp.sum(widened * widened, axis=1)
    all_squares = lax.psum(square_terms, "dp")
    own_squares = lax.dynamic_slice_in_dim(all_squares, own_start, own_rows)
    query_sums, keyval_sums = (
        lax.psum_scatter(
            query_terms.astype(jnp.bfloat16), "dp", scatter_dimension=0, tiled=True
        ).astype(jnp.float32),
        lax.psum_scatter(
            keyval_terms.astype(jnp.bfloat16), "dp", scatter_dimension=0, tiled=True
        ).astype(jnp.float32),
    )
    root_mean_square = jnp.sqrt(own_squares / MODEL_WIDTH + norm_epsilon)
    query_rows = (query_sums / root_mean_square[:, None]).astype(jnp.bfloat16)
    kv_heads = key_value_matrix.shape[1]
    key_value_rows = (
        (keyval_sums / root_mean_square[:, None])
        .astype(jnp.bfloat16)
        .reshape(own_rows, kv_heads, key_value_matrix.shape[2])
    )
    attended_rows = causal_block_attend(
        query_rows, key_value_rows, sentence_segment_rows, QUERY_HEADS // KEYVALUE_HEADS
    )
    head_terms = jnp.dot(
        lax.all_gather(attended_rows, "dp", axis=0, tiled=True),
        out_weight,
        preferred_element_type=jnp.float32,
    )
    head_total = lax.psum(head_terms.astype(jnp.bfloat16), "tensor").astype(jnp.float32)
    return (widened + head_total).astype(jnp.bfloat16)


def on_device(tokens, order, segments, gain, w_query, key_value_weight, w_out):
    spread = lax.all_to_all(tokens, "dp", split_axis=1, concat_axis=0, tiled=True)
    arranged = jnp.take(spread, order, axis=0)
    group_count = lax.axis_size("dp")
    rows_all = group_count * MICRO_TOKENS
    section_index = lax.axis_index("section")
    group_index = lax.axis_index("dp")
    gain_row = gain[0]
    query_weight = w_query[0]
    key_value_matrix = key_value_weight[0]
    out_weight = w_out[0]
    received = jnp.zeros((rows_all, arranged.shape[1]), jnp.bfloat16)
    inbox = []
    results = []
    for turn_index in range(M + 1):
        if turn_index < M:
            fresh = arranged[turn_index * rows_all : (turn_index + 1) * rows_all]
        else:
            fresh = jnp.zeros_like(received)
        micro_index = jnp.where(
            section_index == 0, min(turn_index, M - 1), max(turn_index - 1, 0)
        ).astype(jnp.int32)
        sentence_segment_rows = lax.dynamic_slice_in_dim(
            segments, micro_index * rows_all + group_index * MICRO_TOKENS, MICRO_TOKENS
        )
        layer_input = jnp.where(section_index == 0, fresh, received)
        layer_output = section_layer(
            layer_input, sentence_segment_rows, gain_row, query_weight, key_value_matrix, out_weight
        )
        inbox.append(received)
        results.append(layer_output)
        if turn_index < M:
            received = passed_along(layer_output, "section", 1)
    half_count = M // 2
    from_back = jnp.concatenate(
        [inbox[index_value + 2] for index_value in range(half_count)], axis=0
    )
    kept_here = jnp.concatenate(
        [results[index_value + 1] for index_value in range(half_count, M)], axis=0
    )
    return jnp.where(section_index == 0, from_back, kept_here)


def solution(mesh):
    placed = (
        P("dp", None),
        P(),
        P(),
        P("section", "dp"),
        P("section", "dp", "tensor"),
        P("section", "dp", "tensor", None),
        P("section", "tensor", "dp"),
    )
    return jax.shard_map(
        on_device, mesh=mesh, in_specs=placed, out_specs=P("section", "dp"), check_vma=False
    )
```

profile of v0, /device:TPU:2, one launch (start us, length us, event | category | flops | bytes accessed | tf_op | source)
XLA Modules:
  0.0 1587.2 jit_solution(1069376487911914419)
XLA Ops:
  6.5 4.9 copy.87
  11.5 7.6 all-to-all-start
  19.2 59.1 %all-to-all-done = bf16[128,16,1024]{2,0,1:T(8,128)(2,1)} async-done(((bf16[128,16,1024]{2,0,1:T(8,128)(2,1)}), bf16[128,16,1024]{2,0,1:T(8,128)(2,1)}, u32[]{:S(2)}, u32[]{:S(2)}) %all-to-all-start) | async-done | bytes 4194336 | tf_op jit(solution)/shard_map/all_to_all | solution.py:92
  78.3 13.7 gather_fusion
  103.8 39.7 %psum.70 = f32[512]{0:T(512)S(1)} all-reduce(f32[512]{0:T(512)S(1)} %fusion.1), channel_id=1, replica_groups=mesh['dp'=16,'section'=2,'tensor'=8] {'dp'}, use_global_device_ids=true, to_apply=%region_2.3 | all-reduce | flops 512 | bytes 4096 | tf_op jit(solution)/shard_map/psum | solution.py:61
  143.6 36.6 %reduce-scatter.11.cloned.1.call-done = bf16[32,256]{1,0:T(8,128)(2,1)} async-done(((bf16[512,256]{1,0:T(8,128)(2,1)}), bf16[32,256]{1,0:T(8,128)(2,1)}) %reduce-scatter.11.cloned.1.call-update) | async-done | bytes 16400 | tf_op jit(solution)/shard_map/reduce_scatter | solution.py:67
  181.0 81.3 %reduce-scatter.13.cloned.1.call-done = bf16[32,1024]{1,0:T(8,128)(2,1)} async-done(((bf16[512,1024]{1,0:T(8,128)(2,1)}), bf16[32,1024]{1,0:T(8,128)(2,1)}) %reduce-scatter.13.cloned.1.call-update) | async-done | bytes 65552 | tf_op jit(solution)/shard_map/reduce_scatter | solution.py:64
  264.4 47.2 %all-gather.6.cloned.1.call-done = bf16[512,1024]{1,0:T(8,128)(2,1)} async-done(((bf16[32,1024]{1,0:T(8,128)(2,1)}), bf16[512,1024]{1,0:T(8,128)(2,1)}) %all-gather.6.cloned.1.call-update) | async-done | bytes 1048592 | tf_op jit(solution)/shard_map/all_gather | solution.py:83
  315.8 75.8 %all-reduce.6.cloned.1.call-done = bf16[512,1024]{1,0:T(8,128)(2,1)} async-done(((bf16[512,1024]{1,0:T(8,128)(2,1)}), bf16[512,1024]{1,0:T(8,128)(2,1)}) %all-reduce.6.cloned.1.call-update) | async-done | bytes 1048592 | tf_op jit(solution)/shard_map/psum | solution.py:87
  401.6 36.4 %psum.72 = f32[512]{0:T(512)S(1)} all-reduce(f32[512]{0:T(512)S(1)} %get-tuple-element.9), channel_id=1, replica_groups=mesh['dp'=16,'section'=2,'tensor'=8] {'dp'}, use_global_device_ids=true, to_apply=%region_8.9 | all-reduce | flops 512 | bytes 4096 | tf_op jit(solution)/shard_map/psum | solution.py:61
  438.1 37.8 %reduce-scatter.15.cloned.1.call-done = bf16[32,256]{1,0:T(8,128)(2,1)} async-done(((bf16[512,256]{1,0:T(8,128)(2,1)}), bf16[32,256]{1,0:T(8,128)(2,1)}) %reduce-scatter.15.cloned.1.call-update) | async-done | bytes 16400 | tf_op jit(solution)/shard_map/reduce_scatter | solution.py:67
  476.6 80.9 %reduce-scatter.17.cloned.1.call-done = bf16[32,1024]{1,0:T(8,128)(2,1)} async-done(((bf16[512,1024]{1,0:T(8,128)(2,1)}), bf16[32,1024]{1,0:T(8,128)(2,1)}) %reduce-scatter.17.cloned.1.call-update) | async-done | bytes 65552 | tf_op jit(solution)/shard_map/reduce_scatter | solution.py:64
  559.7 47.2 %all-gather.8.cloned.1.call-done = bf16[512,1024]{1,0:T(8,128)(2,1)} async-done(((bf16[32,1024]{1,0:T(8,128)(2,1)}), bf16[512,1024]{1,0:T(8,128)(2,1)}) %all-gather.8.cloned.1.call-update) | async-done | bytes 1048592 | tf_op jit(solution)/shard_map/all_gather | solution.py:83
  611.1 75.8 %all-reduce.8.cloned.1.call-done = bf16[512,1024]{1,0:T(8,128)(2,1)} async-done(((bf16[512,1024]{1,0:T(8,128)(2,1)}), bf16[512,1024]{1,0:T(8,128)(2,1)}) %all-reduce.8.cloned.1.call-update) | async-done | bytes 1048592 | tf_op jit(solution)/shard_map/psum | solution.py:87
  699.0 36.4 %psum.74 = f32[512]{0:T(512)S(1)} all-reduce(f32[512]{0:T(512)S(1)} %get-tuple-element.7), channel_id=1, replica_groups=mesh['dp'=16,'section'=2,'tensor'=8] {'dp'}, use_global_device_ids=true, to_apply=%region_14.15 | all-reduce | flops 512 | bytes 4096 | tf_op jit(solution)/shard_map/psum | solution.py:61
  735.5 36.5 %reduce-scatter.19.cloned.1.call-done = bf16[32,256]{1,0:T(8,128)(2,1)} async-done(((bf16[512,256]{1,0:T(8,128)(2,1)}), bf16[32,256]{1,0:T(8,128)(2,1)}) %reduce-scatter.19.cloned.1.call-update) | async-done | bytes 16400 | tf_op jit(solution)/shard_map/reduce_scatter | solution.py:67
  772.7 81.0 %reduce-scatter.21.cloned.1.call-done = bf16[32,1024]{1,0:T(8,128)(2,1)} async-done(((bf16[512,1024]{1,0:T(8,128)(2,1)}), bf16[32,1024]{1,0:T(8,128)(2,1)}) %reduce-scatter.21.cloned.1.call-update) | async-done | bytes 65552 | tf_op jit(solution)/shard_map/reduce_scatter | solution.py:64
  855.9 47.2 %all-gather.10.cloned.1.call-done = bf16[512,1024]{1,0:T(8,128)(2,1)} async-done(((bf16[32,1024]{1,0:T(8,128)(2,1)}), bf16[512,1024]{1,0:T(8,128)(2,1)}) %all-gather.10.cloned.1.call-update) | async-done | bytes 1048592 | tf_op jit(solution)/shard_map/all_gather | solution.py:83
  903.1 4.2 fusion.56
  907.4 75.8 %all-reduce.10.cloned.1.call-done = bf16[512,1024]{1,0:T(8,128)(2,1)} async-done(((bf16[512,1024]{1,0:T(8,128)(2,1)}), bf16[512,1024]{1,0:T(8,128)(2,1)}) %all-reduce.10.cloned.1.call-update) | async-done | bytes 1048592 | tf_op jit(solution)/shard_map/psum | solution.py:87
  996.5 36.4 %psum.76 = f32[512]{0:T(512)S(1)} all-reduce(f32[512]{0:T(512)S(1)} %get-tuple-element.5), channel_id=1, replica_groups=mesh['dp'=16,'section'=2,'tensor'=8] {'dp'}, use_global_device_ids=true, to_apply=%region_20.21 | all-reduce | flops 512 | bytes 4096 | tf_op jit(solution)/shard_map/psum | solution.py:61
  1032.9 36.5 %reduce-scatter.23.cloned.1.call-done = bf16[32,256]{1,0:T(8,128)(2,1)} async-done(((bf16[512,256]{1,0:T(8,128)(2,1)}), bf16[32,256]{1,0:T(8,128)(2,1)}) %reduce-scatter.23.cloned.1.call-update) | async-done | bytes 16400 | tf_op jit(solution)/shard_map/reduce_scatter | solution.py:67
  1070.2 80.9 %reduce-scatter.25.cloned.1.call-done = bf16[32,1024]{1,0:T(8,128)(2,1)} async-done(((bf16[512,1024]{1,0:T(8,128)(2,1)}), bf16[32,1024]{1,0:T(8,128)(2,1)}) %reduce-scatter.25.cloned.1.call-update) | async-done | bytes 65552 | tf_op jit(solution)/shard_map/reduce_scatter | solution.py:64
  1153.2 47.1 %all-gather.12.cloned.1.call-done = bf16[512,1024]{1,0:T(8,128)(2,1)} async-done(((bf16[32,1024]{1,0:T(8,128)(2,1)}), bf16[512,1024]{1,0:T(8,128)(2,1)}) %all-gather.12.cloned.1.call-update) | async-done | bytes 1048592 | tf_op jit(solution)/shard_map/all_gather | solution.py:83
  1200.3 4.2 fusion.59
  1204.5 75.8 %all-reduce.12.cloned.1.call-done = bf16[512,1024]{1,0:T(8,128)(2,1)} async-done(((bf16[512,1024]{1,0:T(8,128)(2,1)}), bf16[512,1024]{1,0:T(8,128)(2,1)}) %all-reduce.12.cloned.1.call-update) | async-done | bytes 1048592 | tf_op jit(solution)/shard_map/psum | solution.py:87
  1291.0 36.4 %psum.78 = f32[512]{0:T(512)S(1)} all-reduce(f32[512]{0:T(512)S(1)} %fusion.13), channel_id=1, replica_groups=mesh['dp'=16,'section'=2,'tensor'=8] {'dp'}, use_global_device_ids=true, to_apply=%region_26.27 | all-reduce | flops 512 | bytes 4096 | tf_op jit(solution)/shard_map/psum | solution.py:61
  1327.5 37.4 %reduce-scatter.27.cloned.1.call-done = bf16[32,256]{1,0:T(8,128)(2,1)} async-done(((bf16[512,256]{1,0:T(8,128)(2,1)}), bf16[32,256]{1,0:T(8,128)(2,1)}) %reduce-scatter.27.cloned.1.call-update) | async-done | bytes 16400 | tf_op jit(solution)/shard_map/reduce_scatter | solution.py:67
  1365.7 81.0 %reduce-scatter.29.cloned.1.call-done = bf16[32,1024]{1,0:T(8,128)(2,1)} async-done(((bf16[512,1024]{1,0:T(8,128)(2,1)}), bf16[32,1024]{1,0:T(8,128)(2,1)}) %reduce-scatter.29.cloned.1.call-update) | async-done | bytes 65552 | tf_op jit(solution)/shard_map/reduce_scatter | solution.py:64
  1449.0 47.0 %all-gather.14.cloned.1.call-done = bf16[512,1024]{1,0:T(8,128)(2,1)} async-done(((bf16[32,1024]{1,0:T(8,128)(2,1)}), bf16[512,1024]{1,0:T(8,128)(2,1)}) %all-gather.14.cloned.1.call-update) | async-done | bytes 1048592 | tf_op jit(solution)/shard_map/all_gather | solution.py:83
  1496.0 4.2 fusion.62
  1500.2 75.9 %all-reduce.14.cloned.1.call-done = bf16[512,1024]{1,0:T(8,128)(2,1)} async-done(((bf16[512,1024]{1,0:T(8,128)(2,1)}), bf16[512,1024]{1,0:T(8,128)(2,1)}) %all-reduce.14.cloned.1.call-update) | async-done | bytes 1048592 | tf_op jit(solution)/shard_map/psum | solution.py:87
  (142 shorter events, 85.3 us)
Async XLA Ops:
  6.5 91.2 %copy-start = (bf16[1,1024,1024]{2,1,0:T(8,128)(2,1)S(1)}, bf16[1,1024,1024]{2,1,0:T(8,128)(2,1)}, u32[]{:S(2)}) copy-start(bf16[1,1024,1024]{2,1,0:T(8,128)(2,1)} %param.11) | copy-start | bytes 6291460
  11.5 7.7 copy-start.9
  11.5 66.8 %all-to-all-start = ((bf16[128,16,1024]{2,0,1:T(8,128)(2,1)}), bf16[128,16,1024]{2,0,1:T(8,128)(2,1)}, u32[]{:S(2)}, u32[]{:S(2)}) async-start(bf16[128,16,1024]{2,0,1:T(8,128)(2,1)} %bitcast.266), calls=%async_computation | async-start | bytes 8388608 | tf_op jit(solution)/shard_map/all_to_all | solution.py:92
  19.1 161.1 %reduce-scatter.11.cloned.1.call-start = ((), (), s32[]{:S(2)}) async-start(), calls=%async_computation.11 | async-start | bytes 278528 | tf_op jit(solution)/shard_map/reduce_scatter | solution.py:67
  92.0 4.5 copy-start.10
  92.0 4.5 copy-start.15
  97.7 164.5 %reduce-scatter.13.cloned.1.call-start = ((), (), s32[]{:S(2)}) async-start(), calls=%async_computation.12 | async-start | bytes 1114112 | tf_op jit(solution)/shard_map/reduce_scatter | solution.py:64
  101.2 210.3 %all-gather.6.cloned.1.call-start = ((), (), s32[]{:S(2)}) async-start(), calls=%async_computation.13 | async-start | bytes 1114112 | tf_op jit(solution)/shard_map/all_gather | solution.py:83
  264.3 127.3 %all-reduce.6.cloned.1.call-start = ((), (), s32[]{:S(2)}) async-start(), calls=%async_computation.14 | async-start | bytes 2097152 | tf_op jit(solution)/shard_map/psum | solution.py:87
  315.7 160.1 %reduce-scatter.15.cloned.1.call-start = ((), (), s32[]{:S(2)}) async-start(), calls=%async_computation.15 | async-start | bytes 278528 | tf_op jit(solution)/shard_map/reduce_scatter | solution.py:67
  393.6 2.7 collective-permute-start
  399.2 158.4 %reduce-scatter.17.cloned.1.call-start = ((), (), s32[]{:S(2)}) async-start(), calls=%async_computation.16 | async-start | bytes 1114112 | tf_op jit(solution)/shard_map/reduce_scatter | solution.py:64
  401.5 205.4 %all-gather.8.cloned.1.call-start = ((), (), s32[]{:S(2)}) async-start(), calls=%async_computation.17 | async-start | bytes 1114112 | tf_op jit(solution)/shard_map/all_gather | solution.py:83
  559.6 127.3 %all-reduce.8.cloned.1.call-start = ((), (), s32[]{:S(2)}) async-start(), calls=%async_computation.18 | async-start | bytes 2097152 | tf_op jit(solution)/shard_map/psum | solution.py:87
  611.0 160.9 %reduce-scatter.19.cloned.1.call-start = ((), (), s32[]{:S(2)}) async-start(), calls=%async_computation.19 | async-start | bytes 278528 | tf_op jit(solution)/shard_map/reduce_scatter | solution.py:67
  688.5 5.6 copy-start.12
  688.6 2.9 collective-permute-start.1
  695.3 158.5 %reduce-scatter.21.cloned.1.call-start = ((), (), s32[]{:S(2)}) async-start(), calls=%async_computation.20 | async-start | bytes 1114112 | tf_op jit(solution)/shard_map/reduce_scatter | solution.py:64
  698.8 204.3 %all-gather.10.cloned.1.call-start = ((), (), s32[]{:S(2)}) async-start(), calls=%async_computation.21 | async-start | bytes 1114112 | tf_op jit(solution)/shard_map/all_gather | solution.py:83
  855.8 127.4 %all-reduce.10.cloned.1.call-start = ((), (), s32[]{:S(2)}) async-start(), calls=%async_computation.22 | async-start | bytes 2097152 | tf_op jit(solution)/shard_map/psum | solution.py:87
  907.3 162.1 %reduce-scatter.23.cloned.1.call-start = ((), (), s32[]{:S(2)}) async-start(), calls=%async_computation.23 | async-start | bytes 278528 | tf_op jit(solution)/shard_map/reduce_scatter | solution.py:67
  985.2 6.4 copy-start.13
  985.2 2.7 collective-permute-start.2
  992.8 158.4 %reduce-scatter.25.cloned.1.call-start = ((), (), s32[]{:S(2)}) async-start(), calls=%async_computation.24 | async-start | bytes 1114112 | tf_op jit(solution)/shard_map/reduce_scatter | solution.py:64
  996.3 204.0 %all-gather.12.cloned.1.call-start = ((), (), s32[]{:S(2)}) async-start(), calls=%async_computation.25 | async-start | bytes 1114112 | tf_op jit(solution)/shard_map/all_gather | solution.py:83
  1153.2 127.2 %all-reduce.12.cloned.1.call-start = ((), (), s32[]{:S(2)}) async-start(), calls=%async_computation.26 | async-start | bytes 2097152 | tf_op jit(solution)/shard_map/psum | solution.py:87
  1204.5 160.4 %reduce-scatter.27.cloned.1.call-start = ((), (), s32[]{:S(2)}) async-start(), calls=%async_computation.27 | async-start | bytes 278528 | tf_op jit(solution)/shard_map/reduce_scatter | solution.py:67
  1280.4 6.7 copy-start.14
  1283.4 2.7 collective-permute-start.3
  1288.2 158.4 %reduce-scatter.29.cloned.1.call-start = ((), (), s32[]{:S(2)}) async-start(), calls=%async_computation.28 | async-start | bytes 1114112 | tf_op jit(solution)/shard_map/reduce_scatter | solution.py:64
  1290.6 205.4 %all-gather.14.cloned.1.call-start = ((), (), s32[]{:S(2)}) async-start(), calls=%async_computation.29 | async-start | bytes 1114112 | tf_op jit(solution)/shard_map/all_gather | solution.py:83
  1448.7 127.4 %all-reduce.14.cloned.1.call-start = ((), (), s32[]{:S(2)}) async-start(), calls=%async_computation.30 | async-start | bytes 2097152 | tf_op jit(solution)/shard_map/psum | solution.py:87
  (9 other events, 14.9 us)
Sparse Core Ops, SparseCore 0:
  97.8 82.3 reduce-scatter.10
  183.7 78.5 reduce-scatter.12
  264.7 46.8 all-gather.5
  315.8 75.7 all-reduce.5
  399.3 76.4 reduce-scatter.14
  479.2 78.2 reduce-scatter.16
  560.0 46.8 all-gather.7
  611.1 75.7 all-reduce.7
  695.4 76.4 reduce-scatter.18
  775.3 78.4 reduce-scatter.20
  856.2 46.8 all-gather.9
  907.4 75.7 all-reduce.9
  992.9 76.4 reduce-scatter.22
  1072.7 78.3 reduce-scatter.24
  1153.4 46.8 all-gather.11
  1204.6 75.7 all-reduce.11
  1288.4 76.4 reduce-scatter.26
  1368.2 78.4 reduce-scatter.28
  1449.1 46.8 all-gather.13
  1500.3 75.7 all-reduce.13
where the time goes:
time: 1590 us
  waiting for transfers between devices  1270 us (80%)
  blocking collectives  185 us (12%)
  matrix products  48.2 us (3%)
  local copies, waits for them, and re-layouts  29.8 us (2%)
  other arithmetic  26 us (2%)
    reduce_scatter x5, waiting for transfers between devices, section_layer(): lax.psum_scatter(query_terms.astype(jnp.bfloat16), 'dp', scatter_dimensio...  405 us
    psum x5, waiting for transfers between devices, section_layer(): lax.psum(head_terms.astype(jnp.bfloat16), 'tensor').astype(jnp.float32)  379 us
    all_gather x5, waiting for transfers between devices, section_layer(): lax.all_gather(attended_rows, 'dp', axis=0, tiled=True)  236 us
    psum x5, blocking collectives, section_layer(): all_squares = lax.psum(square_terms, 'dp')  185 us
    reduce_scatter x5, waiting for transfers between devices, section_layer(): lax.psum_scatter(keyval_terms.astype(jnp.bfloat16), 'dp', scatter_dimensi...  185 us
    all_to_all x1, waiting for transfers between devices, on_device(): lax.all_to_all(tokens, 'dp', split_axis=1, concat_axis=0, tiled=True)  59.1 us
  transfers between devices with their start and end apart: 25, of which 25 were waited for; matrix products, arithmetic and copies ran while one was open for 1% of the time, Pallas kernels for 0%

commit v1 on v0

v1 whole, which is shorter than its diff:
```python
import math

import jax
import jax.numpy as jnp
from jax import lax
from jax.sharding import PartitionSpec as P

MODEL_WIDTH = 16384
KEYVALUE_HEADS = 8
QUERY_HEADS = 64
MICRO_TOKENS = 32
M = 4


norm_epsilon = 1e-05


def causal_block_attend(query_rows, key_value_rows, sentence_segment_rows, query_group_width):
    block_count, row_count = sentence_segment_rows.shape
    kv_heads = key_value_rows.shape[1]
    head_size = key_value_rows.shape[2] // 2
    query_head_rows = query_rows.reshape(
        block_count, row_count, kv_heads, query_group_width, head_size
    )
    key_value_blocks = key_value_rows.reshape(block_count, row_count, kv_heads, 2 * head_size)
    key_heads = key_value_blocks[..., :head_size]
    value_heads = key_value_blocks[..., head_size:]
    scores = jnp.einsum(
        "bqkgd,bskd->bkgqs", query_head_rows, key_heads, preferred_element_type=jnp.float32
    ) / math.sqrt(head_size)
    position = jnp.arange(row_count)
    allowed = (sentence_segment_rows[:, :, None] == sentence_segment_rows[:, None, :]) & (
        position[None, :] <= position[:, None]
    )[None]
    raw_weights = jnp.where(allowed[:, None, None], jnp.exp(scores), 0.0)
    totals = jnp.sum(raw_weights, axis=-1, keepdims=True)
    probs = (raw_weights / totals).astype(jnp.bfloat16)
    attended_rows = jnp.einsum(
        "bkgqs,bskd->bqkgd", probs, value_heads, preferred_element_type=jnp.float32
    )
    return attended_rows.astype(jnp.bfloat16).reshape(
        block_count * row_count, kv_heads * query_group_width * head_size
    )


def section_layer(
    hidden, sentence_segment_rows, gain_row, query_weight, key_value_matrix, out_weight
):
    slice_width = hidden.shape[1]
    row_count = hidden.shape[0]
    widened = hidden.astype(jnp.float32)
    normed_rows = (widened * gain_row[None, :]).astype(jnp.bfloat16)
    query_terms = jnp.dot(normed_rows, query_weight, preferred_element_type=jnp.float32)
    keyval_terms = jnp.dot(
        normed_rows, key_value_matrix.reshape(slice_width, -1), preferred_element_type=jnp.float32
    )
    query_width = query_terms.shape[1]
    square_terms = jnp.sum(widened * widened, axis=1)
    all_squares = lax.psum(square_terms, "dp")
    joined_sums = lax.psum(
        jnp.concatenate([query_terms, keyval_terms], axis=1).astype(jnp.bfloat16), "dp"
    ).astype(jnp.float32)
    root_mean_square = jnp.sqrt(all_squares / MODEL_WIDTH + norm_epsilon)
    scaled_sums = joined_sums / root_mean_square[:, None]
    query_rows = scaled_sums[:, :query_width].astype(jnp.bfloat16)
    kv_heads = key_value_matrix.shape[1]
    key_value_rows = (
        scaled_sums[:, query_width:]
        .astype(jnp.bfloat16)
        .reshape(row_count, kv_heads, key_value_matrix.shape[2])
    )
    attended_rows = causal_block_attend(
        query_rows, key_value_rows, sentence_segment_rows, QUERY_HEADS // KEYVALUE_HEADS
    )
    head_terms = jnp.dot(attended_rows, out_weight, preferred_element_type=jnp.float32)
    head_total = lax.psum(head_terms.astype(jnp.bfloat16), "tensor").astype(jnp.float32)
    return (widened + head_total).astype(jnp.bfloat16)


def on_device(tokens, order, segments, gain, w_query, key_value_weight, w_out):
    section_count = lax.axis_size("section")
    section_index = lax.axis_index("section")
    own = (gain[0], w_query[0], key_value_weight[0], w_out[0])
    other = lax.ppermute(own, "section", [(i, (i + 1) % section_count) for i in range(section_count)])
    spread = lax.all_to_all(tokens, "dp", split_axis=1, concat_axis=0, tiled=True)
    rows_here = spread.shape[0] // section_count
    my_order = lax.dynamic_slice_in_dim(order, section_index * rows_here, rows_here)
    hidden = jnp.take(spread, my_order, axis=0)
    my_segments = lax.dynamic_slice_in_dim(
        segments, section_index * rows_here, rows_here
    ).reshape(-1, MICRO_TOKENS)
    for layer_index in range(section_count):
        params = jax.tree.map(
            lambda mine, theirs: jnp.where(section_index == layer_index, mine, theirs), own, other
        )
        hidden = section_layer(hidden, my_segments, *params)
    return hidden


def solution(mesh):
    placed = (
        P("dp", None),
        P(),
        P(),
        P("section", "dp"),
        P("section", "dp", "tensor"),
        P("section", "dp", "tensor", None),
        P("section", "tensor", "dp"),
    )
    return jax.shard_map(
        on_device, mesh=mesh, in_specs=placed, out_specs=P("section", "dp"), check_vma=False
    )
```

time: 1590 us -> 535 us (0.34)
  waiting for transfers between devices: 1270 us -> 353 us
  blocking collectives: 185 us -> 77.1 us
    reduce_scatter x10 -> x0, waiting for transfers between devices: 590 us -> none  [the longest x5 405 us: section_layer(): lax.psum_scatter(query_terms.astype(jnp.bfloat16), 'dp', scatter_dimensio...]
    all_gather x5 -> x0, waiting for transfers between devices: 236 us -> none  [section_layer(): lax.all_gather(attended_rows, 'dp', axis=0, tiled=True)]
    psum x5 -> x2, waiting for transfers between devices: 379 us -> 165 us  [section_layer(): lax.psum(head_terms.astype(jnp.bfloat16), 'tensor').astype(jnp.float32)]
    psum x0 -> x2, waiting for transfers between devices: none -> 130 us  [section_layer(): lax.psum(jnp.concatenate([query_terms, keyval_terms], axis=1).astype(jnp....]
    psum x5 -> x2, blocking collectives: 185 us -> 77.1 us  [section_layer(): all_squares = lax.psum(square_terms, 'dp')]
  transfers between devices with their start and end apart: 25 -> 9, of which waited for: 25 -> 6; matrix products, arithmetic and copies ran while one was open for 1% -> 6% of each run, Pallas kernels for 0% -> 0%
where the time goes in v1:
time: 535 us; the launch traced here: 534 us
  waiting for transfers between devices  353 us (66%)
  blocking collectives  77.1 us (14%)
  local copies, waits for them, and re-layouts  33.4 us (6%)
  matrix products  32.8 us (6%)
  other arithmetic  16.1 us (3%)
  between operations  13.5 us (3%)
  starting transfers between devices  8.56 us (2%)
    psum x2, waiting for transfers between devices, section_layer(): lax.psum(head_terms.astype(jnp.bfloat16), 'tensor').astype(jnp.float32)  165 us
    psum x2, waiting for transfers between devices, section_layer(): lax.psum(jnp.concatenate([query_terms, keyval_terms], axis=1).astype(jnp....  130 us
    psum x2, blocking collectives, section_layer(): all_squares = lax.psum(square_terms, 'dp')  77.1 us
    all_to_all x1, waiting for transfers between devices, on_device(): lax.all_to_all(tokens, 'dp', split_axis=1, concat_axis=0, tiled=True)  54.6 us
  transfers between devices with their start and end apart: 9, of which 6 were waited for; matrix products, arithmetic and copies ran while one was open for 6% of the time, Pallas kernels for 0%

profile of v1, /device:TPU:2, one launch (start us, length us, event | category | flops | bytes accessed | tf_op | source)
XLA Modules:
  0.0 534.3 jit_solution(11576190769520700399)
XLA Ops:
  6.5 4.8 copy.60
  11.3 7.6 %all-to-all-start = ((bf16[128,16,1024]{2,0,1:T(8,128)(2,1)}), bf16[128,16,1024]{2,0,1:T(8,128)(2,1)}, u32[]{:S(2)}, u32[]{:S(2)}) async-start(bf16[128,16,1024]{2,0,1:T(8,128)(2,1)} %bitcast.137), calls=%async_computation | async-start | bytes 8388608 | tf_op jit(solution)/shard_map/all_to_all | solution.py:85
  19.7 3.8 collective-permute-done
  23.6 54.6 %all-to-all-done = bf16[128,16,1024]{2,0,1:T(8,128)(2,1)} async-done(((bf16[128,16,1024]{2,0,1:T(8,128)(2,1)}), bf16[128,16,1024]{2,0,1:T(8,128)(2,1)}, u32[]{:S(2)}, u32[]{:S(2)}) %all-to-all-start) | async-done | bytes 4194336 | tf_op jit(solution)/shard_map/all_to_all | solution.py:85
  78.1 7.7 %gather_fusion = bf16[1024,1024]{1,0:T(8,128)(2,1)S(1)} fusion(bf16[2048,1024]{1,0:T(8,128)(2,1)} %bitcast.1, s32[1024]{0:T(1024)S(1)} %fusion.76), kind=kCustom, calls=%fused_computation | custom fusion | bytes 4198400 | tf_op jit(solution)/shard_map/jit(_take)/gather | solution.py:88
  85.9 4.2 fusion.42
  91.1 1.8 pad_maximum_fusion
  94.6 40.1 %psum.43 = f32[1024]{0:T(1024)S(1)} all-reduce(f32[1024]{0:T(1024)S(1)} %fusion.1), channel_id=1, replica_groups=mesh['dp'=16,'section'=2,'tensor'=8] {'dp'}, use_global_device_ids=true, to_apply=%region_2.3 | all-reduce | flops 1024 | bytes 8192 | tf_op jit(solution)/shard_map/psum | solution.py:59
  134.7 65.2 %all-reduce.5.cloned.1.call-done = bf16[1024,1280]{0,1:T(8,128)(2,1)} async-done(((bf16[1024,1280]{0,1:T(8,128)(2,1)}), bf16[1024,1280]{0,1:T(8,128)(2,1)}) %all-reduce.5.cloned.1.call-update) | async-done | bytes 2621456 | tf_op jit(solution)/shard_map/psum | solution.py:60
  200.0 2.5 divide_convert_fusion.1
  202.4 1.6 slice.41
  204.6 3.9 copy.19
  208.6 3.6 copy.35
  212.4 5.0 fusion.6
  217.3 1.2 convert_bitcast_fusion.1
  218.6 1.0 copy.22
  220.2 3.7 fusion.48
  223.9 82.3 %all-reduce.7.cloned.1.call-done = bf16[1024,1024]{1,0:T(8,128)(2,1)} async-done(((bf16[1024,1024]{1,0:T(8,128)(2,1)}), bf16[1024,1024]{1,0:T(8,128)(2,1)}) %all-reduce.7.cloned.1.call-update) | async-done | bytes 2097168 | tf_op jit(solution)/shard_map/psum | solution.py:76
  306.2 2.8 fusion.4
  309.0 5.5 %fusion.45 = bf16[1024,1024]{0,1:T(8,128)(2,1)S(1)} fusion(bf16[1024,1024]{1,0:T(8,128)(2,1)} %collective-permute-done.1, pred[]{:T(512)S(6)} %eq.21, bf16[1024,1024]{1,0:T(8,128)(2,1)S(1)} %get-tuple-element.6, f32[1024]{0:T(1024)S(1)} %get-tuple-element.7, bf16[1,1024,1024]{2,1,0:T(8,128)(2,1)} %param.11), kind=kOutput, calls=%fused_computation.58 | convolution fusion | flops 2152726528 | bytes 8392705 | tf_op jit(solution)/shard_map/dot_general | solution.py:53
  315.3 1.8 pad_maximum_fusion.1
  317.1 37.0 %psum.46 = f32[1024]{0:T(1024)S(1)} all-reduce(f32[1024]{0:T(1024)S(1)} %get-tuple-element.5), channel_id=1, replica_groups=mesh['dp'=16,'section'=2,'tensor'=8] {'dp'}, use_global_device_ids=true, to_apply=%region_7.8 | all-reduce | flops 1024 | bytes 8192 | tf_op jit(solution)/shard_map/psum | solution.py:59
  354.2 64.6 %all-reduce.9.cloned.1.call-done = bf16[1024,1280]{0,1:T(8,128)(2,1)} async-done(((bf16[1024,1280]{0,1:T(8,128)(2,1)}), bf16[1024,1280]{0,1:T(8,128)(2,1)}) %all-reduce.9.cloned.1.call-update) | async-done | bytes 2621456 | tf_op jit(solution)/shard_map/psum | solution.py:60
  418.8 2.5 divide_convert_fusion
  421.3 1.6 slice.45
  423.5 2.9 copy.24
  426.4 2.0 copy.37
  428.5 5.0 fusion.7
  433.5 1.2 convert_bitcast_fusion
  436.3 5.3 fusion.53
  441.6 82.3 %all-reduce.11.cloned.1.call-done = bf16[1024,1024]{1,0:T(8,128)(2,1)} async-done(((bf16[1024,1024]{1,0:T(8,128)(2,1)}), bf16[1024,1024]{1,0:T(8,128)(2,1)}) %all-reduce.11.cloned.1.call-update) | async-done | bytes 2097168 | tf_op jit(solution)/shard_map/psum | solution.py:76
  523.9 3.9 fusion.5
  (59 shorter events, 8.1 us)
Async XLA Ops:
  11.3 7.8 %copy-start.5 = (f32[1,1024]{1,0:T(1,128)S(1)}, f32[1,1024]{1,0:T(1,128)}, u32[]{:S(2)}) copy-start(f32[1,1024]{1,0:T(1,128)} %param.10) | copy-start | bytes 12292
  11.3 8.3 %copy-start.8 = (bf16[1,1024,1,256]{3,1,2,0:T(8,128)(2,1)S(1)}, bf16[1,1024,1,256]{3,1,2,0:T(8,128)(2,1)}, u32[]{:S(2)}) copy-start(bf16[1,1024,1,256]{3,1,2,0:T(8,128)(2,1)} %param.12) | copy-start | bytes 1572868
  11.3 8.4 %copy-start.4 = (s32[2048]{0:T(1024)S(1)}, s32[2048]{0:T(1024)}, u32[]{:S(2)}) copy-start(s32[2048]{0:T(1024)} %param.8) | copy-start | bytes 24580
  11.3 66.8 %all-to-all-start = ((bf16[128,16,1024]{2,0,1:T(8,128)(2,1)}), bf16[128,16,1024]{2,0,1:T(8,128)(2,1)}, u32[]{:S(2)}, u32[]{:S(2)}) async-start(bf16[128,16,1024]{2,0,1:T(8,128)(2,1)} %bitcast.137), calls=%async_computation | async-start | bytes 8388608 | tf_op jit(solution)/shard_map/all_to_all | solution.py:85
  18.9 181.0 %all-reduce.5.cloned.1.call-start = ((), (), s32[]{:S(2)}) async-start(), calls=%async_computation.1 | async-start | bytes 5242880 | tf_op jit(solution)/shard_map/psum | solution.py:60
  19.0 66.9 %collective-permute-start.1 = (bf16[1024,1024]{1,0:T(8,128)(2,1)}, bf16[1024,1024]{1,0:T(8,128)(2,1)}, u32[]{:S(2)}, u32[]{:S(2)}) collective-permute-start(bf16[1024,1024]{1,0:T(8,128)(2,1)} %bitcast.3), channel_id=1, source_target_pairs={{0,8},{8,0},{1,9},{9,1},{2,10},{10,2},{3,11},{11,3},{4,12},{12,4},... | collective-permute-start | bytes 6291464 | tf_op jit(solution)/shard_map/ppermute | solution.py:84
  19.1 4.5 collective-permute-start
  19.6 70.5 %collective-permute-start.2 = (bf16[1024,1,256]{2,0,1:T(8,128)(2,1)S(1)}, bf16[1024,1,256]{2,0,1:T(8,128)(2,1)S(1)}, u32[]{:S(2)}, u32[]{:S(2)}) collective-permute-start(bf16[1024,1,256]{2,0,1:T(8,128)(2,1)S(1)} %bitcast.152), channel_id=1, source_target_pairs={{0,8},{8,0},{1,9},{9,1},{2,10},{10,2},{3,11},{11,3},{4,12},{12,4},... | collective-permute-start | bytes 1572872 | tf_op jit(solution)/shard_map/ppermute | solution.py:84
  90.1 1.0 copy-start.10
  92.9 0.7 dynamic-slice-start
  92.9 213.3 %all-reduce.7.cloned.1.call-start = ((), (), s32[]{:S(2)}) async-start(), calls=%async_computation.2 | async-start | bytes 4194304 | tf_op jit(solution)/shard_map/psum | solution.py:76
  92.9 126.7 %collective-permute-start.3 = (bf16[1024,1024]{1,0:T(8,128)(2,1)}, bf16[1024,1024]{1,0:T(8,128)(2,1)}, u32[]{:S(2)}, u32[]{:S(2)}) collective-permute-start(bf16[1024,1024]{1,0:T(8,128)(2,1)} %bitcast.151), channel_id=1, source_target_pairs={{0,8},{8,0},{1,9},{9,1},{2,10},{10,2},{3,11},{11,3},{4,12},{12,4},... | collective-permute-start | bytes 6291464 | tf_op jit(solution)/shard_map/ppermute | solution.py:84
  202.4 2.2 copy-start
  208.6 3.6 slice-start
  218.6 1.6 copy-start.6
  223.8 194.9 %all-reduce.9.cloned.1.call-start = ((), (), s32[]{:S(2)}) async-start(), calls=%async_computation.3 | async-start | bytes 5242880 | tf_op jit(solution)/shard_map/psum | solution.py:60
  309.0 5.5 %copy-start.2 = (bf16[1024,1024]{1,0:T(8,128)(2,1)}, bf16[1024,1024]{1,0:T(8,128)(2,1)S(1)}, u32[]{:S(2)}) copy-start(bf16[1024,1024]{1,0:T(8,128)(2,1)S(1)} %get-tuple-element.6) | copy-start | bytes 6291460
  309.0 5.5 %copy-start.9 = (bf16[1,1024,1,256]{3,1,2,0:T(8,128)(2,1)S(1)}, bf16[1,1024,1,256]{3,1,2,0:T(8,128)(2,1)}, u32[]{:S(2)}) copy-start(bf16[1,1024,1,256]{3,1,2,0:T(8,128)(2,1)} %param.12) | copy-start | bytes 1572868
  309.0 5.5 %copy-start.11 = (bf16[1024,1,256]{2,0,1:T(8,128)(2,1)S(1)}, bf16[1024,1,256]{2,0,1:T(8,128)(2,1)}, u32[]{:S(2)}) copy-start(bf16[1024,1,256]{2,0,1:T(8,128)(2,1)} %copy-done.10) | copy-start | bytes 1572868
  317.1 206.9 %all-reduce.11.cloned.1.call-start = ((), (), s32[]{:S(2)}) async-start(), calls=%async_computation.4 | async-start | bytes 4194304 | tf_op jit(solution)/shard_map/psum | solution.py:76
  421.3 2.2 copy-start.1
  426.4 2.0 slice-start.1
  434.7 1.6 copy-start.7
  441.6 82.3 %copy-start.3 = (bf16[1024,1024]{1,0:T(8,128)(2,1)S(1)}, bf16[1024,1024]{1,0:T(8,128)(2,1)}, u32[]{:S(2)}) copy-start(bf16[1024,1024]{1,0:T(8,128)(2,1)} %copy-done.2) | copy-start | bytes 6291460
Sparse Core Ops, SparseCore 0:
  93.0 106.9 all-reduce.4
  224.0 82.2 all-reduce.6
  317.2 101.5 all-reduce.8
  441.8 82.1 all-reduce.10

commit v2 on v1

--- a/solution.py
+++ b/solution.py
@@ -43,11 +43,25 @@
     )
 
 
+def gathered_over(block, axis):
+    count = lax.axis_size(axis)
+    spread = jnp.broadcast_to(block[None], (count,) + block.shape)
+    return lax.all_to_all(spread, axis, 0, 0, tiled=False).reshape(
+        (count * block.shape[0],) + block.shape[1:]
+    )
+
+
 def section_layer(
     hidden, sentence_segment_rows, gain_row, query_weight, key_value_matrix, out_weight
 ):
     slice_width = hidden.shape[1]
     row_count = hidden.shape[0]
+    group_count = lax.axis_size("dp")
+    own_rows = row_count // group_count
+    own_blocks = own_rows // MICRO_TOKENS
+    own_segments = lax.dynamic_slice_in_dim(
+        sentence_segment_rows, lax.axis_index("dp") * own_blocks, own_blocks
+    )
     widened = hidden.astype(jnp.float32)
     normed_rows = (widened * gain_row[None, :]).astype(jnp.bfloat16)
     query_terms = jnp.dot(normed_rows, query_weight, preferred_element_type=jnp.float32)
@@ -55,24 +69,40 @@
         normed_rows, key_value_matrix.reshape(slice_width, -1), preferred_element_type=jnp.float32
     )
     query_width = query_terms.shape[1]
-    square_terms = jnp.sum(widened * widened, axis=1)
-    all_squares = lax.psum(square_terms, "dp")
-    joined_sums = lax.psum(
-        jnp.concatenate([query_terms, keyval_terms], axis=1).astype(jnp.bfloat16), "dp"
-    ).astype(jnp.float32)
-    root_mean_square = jnp.sqrt(all_squares / MODEL_WIDTH + norm_epsilon)
-    scaled_sums = joined_sums / root_mean_square[:, None]
+    keyval_width = keyval_terms.shape[1]
+    square_terms = jnp.sum(widened * widened, axis=1, keepdims=True)
+    square_high = lax.reduce_precision(square_terms, exponent_bits=8, mantissa_bits=7)
+    square_low = square_terms - square_high
+    payload = jnp.concatenate(
+        [
+            query_terms.astype(jnp.bfloat16),
+            keyval_terms.astype(jnp.bfloat16),
+            square_high.astype(jnp.bfloat16),
+            square_low.astype(jnp.bfloat16),
+            jnp.zeros((row_count, 126), jnp.bfloat16),
+        ],
+        axis=1,
+    )
+    arrived = lax.all_to_all(
+        payload.reshape(group_count, own_rows, payload.shape[1]), "dp", 0, 0, tiled=False
+    )
+    summed = jnp.sum(arrived.astype(jnp.float32), axis=0)
+    own_squares = summed[:, query_width + keyval_width] + summed[:, query_width + keyval_width + 1]
+    root_mean_square = jnp.sqrt(own_squares / MODEL_WIDTH + norm_epsilon)
+    scaled_sums = summed[:, : query_width + keyval_width] / root_mean_square[:, None]
     query_rows = scaled_sums[:, :query_width].astype(jnp.bfloat16)
     kv_heads = key_value_matrix.shape[1]
     key_value_rows = (
         scaled_sums[:, query_width:]
         .astype(jnp.bfloat16)
-        .reshape(row_count, kv_heads, key_value_matrix.shape[2])
+        .reshape(own_rows, kv_heads, key_value_matrix.shape[2])
     )
     attended_rows = causal_block_attend(
-        query_rows, key_value_rows, sentence_segment_rows, QUERY_HEADS // KEYVALUE_HEADS
+        query_rows, key_value_rows, own_segments, QUERY_HEADS // KEYVALUE_HEADS
     )
-    head_terms = jnp.dot(attended_rows, out_weight, preferred_element_type=jnp.float32)
+    head_terms = jnp.dot(
+        gathered_over(attended_rows, "dp"), out_weight, preferred_element_type=jnp.float32
+    )
     head_total = lax.psum(head_terms.astype(jnp.bfloat16), "tensor").astype(jnp.float32)
     return (widened + head_total).astype(jnp.bfloat16)
 
@@ -80,12 +110,31 @@
 def on_device(tokens, order, segments, gain, w_query, key_value_weight, w_out):
     section_count = lax.axis_size("section")
     section_index = lax.axis_index("section")
+    group_count = lax.axis_size("dp")
     own = (gain[0], w_query[0], key_value_weight[0], w_out[0])
-    other = lax.ppermute(own, "section", [(i, (i + 1) % section_count) for i in range(section_count)])
-    spread = lax.all_to_all(tokens, "dp", split_axis=1, concat_axis=0, tiled=True)
-    rows_here = spread.shape[0] // section_count
-    my_order = lax.dynamic_slice_in_dim(order, section_index * rows_here, rows_here)
-    hidden = jnp.take(spread, my_order, axis=0)
+    swap = [(i, (i + 1) % section_count) for i in range(section_count)]
+    other = lax.ppermute(own, "section", swap)
+    entry_rows, model_width = tokens.shape
+    slice_width = model_width // group_count
+    half_width = slice_width // section_count
+    my_columns = lax.dynamic_slice_in_dim(
+        tokens.reshape(entry_rows, group_count, section_count, half_width),
+        section_index,
+        1,
+        axis=2,
+    ).reshape(entry_rows, group_count, half_width)
+    spread = lax.all_to_all(my_columns, "dp", 1, 0, tiled=True).reshape(-1, half_width)
+    arranged = jnp.take(spread, order, axis=0)
+    rows_here = arranged.shape[0] // section_count
+    both = arranged.reshape(section_count, rows_here, half_width)
+    mine = lax.dynamic_index_in_dim(both, section_index, 0, keepdims=False)
+    theirs = lax.dynamic_index_in_dim(both, 1 - section_index, 0, keepdims=False)
+    received = lax.ppermute(theirs, "section", swap)
+    hidden = jnp.where(
+        section_index == 0,
+        jnp.concatenate([mine, received], axis=1),
+        jnp.concatenate([received, mine], axis=1),
+    )
     my_segments = lax.dynamic_slice_in_dim(
         segments, section_index * rows_here, rows_here
     ).reshape(-1, MICRO_TOKENS)

time: 535 us -> 448 us (0.84)
  waiting for transfers between devices: 353 us -> 262 us
  starting transfers between devices: 8.56 us -> 26.8 us
  blocking collectives: 77.1 us -> 64 us
  local copies, waits for them, and re-layouts: 33.4 us -> 43.3 us
  matrix products: 32.8 us -> 25.9 us
    psum x2 -> x0, waiting for transfers between devices: 130 us -> none  [section_layer(): lax.psum(jnp.concatenate([query_terms, keyval_terms], axis=1).astype(jnp....]
    psum x2 -> x0, blocking collectives: 77.1 us -> none  [section_layer(): all_squares = lax.psum(square_terms, 'dp')]
    all_to_all x0 -> x2, blocking collectives: none -> 64 us  [the longest x1 38 us: section_layer(): lax.all_to_all(payload.reshape(group_count, own_rows, payload.shape[1]),...]
    all_to_all x1 -> x3, waiting for transfers between devices: 54.6 us -> 95.9 us  [the longest x1 39.1 us: section_layer(): lax.all_to_all(payload.reshape(group_count, own_rows, payload.shape[1]),...]
    all_to_all x1 -> x3, starting transfers between devices: 7.61 us -> 24.5 us  [the longest x1 8.51 us: gathered_over(): lax.all_to_all(spread, axis, 0, 0, tiled=False)]
    dynamic_slice x0 -> x3, local copies, waits for them, and re-layouts: none -> 10.6 us  [the longest x2 10.6 us: on_device(): lax.dynamic_slice_in_dim(tokens.reshape(entry_rows, group_count, section_...]
    concatenate x0 -> x3, local copies, waits for them, and re-layouts: none -> 10.4 us  [section_layer(): jnp.concatenate([query_terms.astype(jnp.bfloat16), keyval_terms.astype(jn...]
    slice x4 -> x0, local copies, waits for them, and re-layouts: 10 us -> none  [section_layer(): query_rows = scaled_sums[:, :query_width].astype(jnp.bfloat16)]
  transfers between devices with their start and end apart: 9 -> 10, of which waited for: 6 -> 6; matrix products, arithmetic and copies ran while one was open for 6% -> 4% of each run, Pallas kernels for 0% -> 0%
where the time goes in v2:
time: 448 us; the launch traced here: 447 us
  waiting for transfers between devices  262 us (58%)
  blocking collectives  64 us (14%)
  local copies, waits for them, and re-layouts  43.3 us (10%)
  starting transfers between devices  26.8 us (6%)
  matrix products  25.9 us (6%)
  between operations  13.8 us (3%)
  other arithmetic  11 us (2%)
    psum x2, waiting for transfers between devices, section_layer(): lax.psum(head_terms.astype(jnp.bfloat16), 'tensor').astype(jnp.float32)  165 us
    all_to_all x1, waiting for transfers between devices, section_layer(): lax.all_to_all(payload.reshape(group_count, own_rows, payload.shape[1]),...  39.1 us
    all_to_all x1, blocking collectives, section_layer(): lax.all_to_all(payload.reshape(group_count, own_rows, payload.shape[1]),...  38 us
    all_to_all x1, waiting for transfers between devices, gathered_over(): lax.all_to_all(spread, axis, 0, 0, tiled=False)  29.7 us
    all_to_all x1, waiting for transfers between devices, on_device(): lax.all_to_all(my_columns, 'dp', 1, 0, tiled=True).reshape(-1, half_width)  27.1 us
    all_to_all x1, blocking collectives, gathered_over(): lax.all_to_all(spread, axis, 0, 0, tiled=False)  25.9 us
    dynamic_slice x2, local copies, waits for them, and re-layouts, on_device(): lax.dynamic_slice_in_dim(tokens.reshape(entry_rows, group_count, section_...  10.6 us
    dot_general x2, matrix products, section_layer(): jnp.dot(gathered_over(attended_rows, 'dp'), out_weight, preferred_element...  10.5 us
  transfers between devices with their start and end apart: 10, of which 6 were waited for; matrix products, arithmetic and copies ran while one was open for 4% of the time, Pallas kernels for 0%

profile of v2, /device:TPU:2, one launch (start us, length us, event | category | flops | bytes accessed | tf_op | source)
XLA Modules:
  0.0 447.0 jit_solution(3880165584155092383)
XLA Ops:
  6.5 7.8 %reshape.191 = bf16[128,16,2,512]{3,2,1,0:T(2,128)(2,1)} reshape(bf16[128,16384]{1,0:T(8,128)(2,1)} %param.7) | data formatting | bytes 8388608 | tf_op jit(solution)/shard_map/reshape | solution.py:121
  14.3 7.0 %constant_dynamic-slice_fusion.1 = bf16[128,16,1,512]{3,2,1,0:T(2,128)(2,1)S(1)} fusion(bf16[128,16,2,512]{3,2,1,0:T(2,128)(2,1)} %reshape.191, s32[]{:T(128)S(6)} %select_n.88), kind=kLoop, calls=%fused_computation.100 | loop fusion | bytes 4194308 | tf_op jit(solution)/shard_map/dynamic_slice | solution.py:120
  21.4 3.5 copy.56
  24.9 7.6 %all-to-all-start = ((bf16[128,16,512]{2,0,1:T(8,128)(2,1)}), bf16[128,16,512]{2,0,1:T(8,128)(2,1)S(1)}, u32[]{:S(2)}, u32[]{:S(2)}) async-start(bf16[128,16,512]{2,0,1:T(8,128)(2,1)} %bitcast.133), calls=%async_computation | async-start | bytes 4194304 | tf_op jit(solution)/shard_map/all_to_all | solution.py:126
  32.6 27.1 %all-to-all-done = bf16[128,16,512]{2,0,1:T(8,128)(2,1)S(1)} async-done(((bf16[128,16,512]{2,0,1:T(8,128)(2,1)}), bf16[128,16,512]{2,0,1:T(8,128)(2,1)S(1)}, u32[]{:S(2)}, u32[]{:S(2)}) %all-to-all-start) | async-done | bytes 2097184 | tf_op jit(solution)/shard_map/all_to_all | solution.py:126
  59.7 9.2 %gather_fusion = bf16[2048,512]{1,0:T(8,128)(2,1)} fusion(bf16[2048,512]{1,0:T(8,128)(2,1)S(1)} %bitcast.131, s32[2048]{0:T(1024)S(1)} %fusion.72), kind=kCustom, calls=%fused_computation | custom fusion | bytes 4202496 | tf_op jit(solution)/shard_map/jit(_take)/gather | solution.py:127
  68.9 1.8 broadcast_select_fusion
  71.4 0.4 collective-permute-start.3
  71.8 1.7 collective-permute-done.1
  73.6 0.6 fusion.1
  74.8 1.9 fusion.36
  76.7 3.7 fusion.18
  80.5 5.6 %concatenate.29 = bf16[16,64,1408]{2,1,0:T(8,128)(2,1)} concatenate(bf16[16,64,1024]{2,1,0:T(8,128)(2,1)} %bitcast.135, bf16[16,64,256]{2,1,0:T(8,128)(2,1)S(1)} %bitcast.138, bf16[16,64,1]{2,1,0:T(8,128)(2,1)S(1)} %copy.25, bf16[16,64,1]{2,1,0:T(8,128)(2,1)S(1)} %copy.26, bf16[16,64,126]{2,1,0:T(8,128)(2,1)S(1)} %concatenate.28), dimensions={2} | concatenate | bytes 5767168 | tf_op jit(solution)/shard_map/concatenate | solution.py:76
  86.0 8.4 %all-to-all-start.1 = ((bf16[16,64,1408]{2,1,0:T(8,128)(2,1)}), bf16[16,64,1408]{2,1,0:T(8,128)(2,1)S(1)}, u32[]{:S(2)}, u32[]{:S(2)}) async-start(bf16[16,64,1408]{2,1,0:T(8,128)(2,1)} %concatenate.29), calls=%async_computation.1 | async-start | bytes 5767168 | tf_op jit(solution)/shard_map/all_to_all | solution.py:86
  94.4 1.6 collective-permute-start.4
  96.2 39.1 %all-to-all-done.1 = bf16[16,64,1408]{2,1,0:T(8,128)(2,1)S(1)} async-done(((bf16[16,64,1408]{2,1,0:T(8,128)(2,1)}), bf16[16,64,1408]{2,1,0:T(8,128)(2,1)S(1)}, u32[]{:S(2)}, u32[]{:S(2)}) %all-to-all-start.1) | async-done | bytes 2883616 | tf_op jit(solution)/shard_map/all_to_all | solution.py:86
  136.7 1.6 broadcast_in_dim.71
  138.3 8.5 %all-to-all-start.2 = ((bf16[16,64,1024]{2,1,0:T(8,128)(2,1)}), bf16[16,64,1024]{2,1,0:T(8,128)(2,1)S(1)}, u32[]{:S(2)}, u32[]{:S(2)}) async-start(bf16[16,64,1024]{2,1,0:T(8,128)(2,1)} %broadcast_in_dim.71), calls=%async_computation.2 | async-start | bytes 4194304 | tf_op jit(solution)/shard_map/all_to_all | solution.py:49
  146.9 29.7 %all-to-all-done.2 = bf16[16,64,1024]{2,1,0:T(8,128)(2,1)S(1)} async-done(((bf16[16,64,1024]{2,1,0:T(8,128)(2,1)}), bf16[16,64,1024]{2,1,0:T(8,128)(2,1)S(1)}, u32[]{:S(2)}, u32[]{:S(2)}) %all-to-all-start.2) | async-done | bytes 2097184 | tf_op jit(solution)/shard_map/all_to_all | solution.py:49
  176.6 5.2 %fusion.21 = bf16[1024,1024]{1,0:T(8,128)(2,1)} fusion(bf16[1024,1024]{1,0:T(8,128)(2,1)S(1)} %bitcast.136, bf16[1024,1024]{1,0:T(8,128)(2,1)} %collective-permute-done.4, pred[]{:T(512)S(6)} %eq.14, bf16[1,1024,1024]{2,1,0:T(8,128)(2,1)} %param.13), kind=kOutput, calls=%fused_computation.31 | convolution fusion | flops 2149580800 | bytes 8388609 | tf_op jit(solution)/shard_map/dot_general | solution.py:103
  181.9 86.2 %all-reduce.3.cloned.1.call-done = bf16[1024,1024]{1,0:T(8,128)(2,1)} async-done(((bf16[1024,1024]{1,0:T(8,128)(2,1)}), bf16[1024,1024]{1,0:T(8,128)(2,1)}) %all-reduce.3.cloned.1.call-update) | async-done | bytes 2097168 | tf_op jit(solution)/shard_map/psum | solution.py:106
  268.1 3.3 fusion.4
  271.5 1.1 copy.30
  272.7 0.9 copy.31
  273.6 5.9 %fusion.24 = bf16[1024,1024]{1,0:T(8,128)(2,1)} fusion(bf16[1024,1024]{1,0:T(8,128)(2,1)} %collective-permute-done.2, pred[]{:T(512)S(6)} %eq.18, bf16[1024,1024]{1,0:T(8,128)(2,1)S(1)} %get-tuple-element.6, f32[1024]{0:T(1024)S(1)} %get-tuple-element.11, bf16[1,1024,1024]{2,1,0:T(8,128)(2,1)} %param.11), kind=kOutput, calls=%fused_computation.32 | convolution fusion | flops 2152726528 | bytes 8392705 | tf_op jit(solution)/shard_map/dot_general | solution.py:67
  279.5 2.7 fusion.39
  282.2 4.8 %concatenate.32 = bf16[16,64,1408]{2,1,0:T(8,128)(2,1)S(1)} concatenate(bf16[16,64,1024]{2,1,0:T(8,128)(2,1)} %bitcast.134, bf16[16,64,256]{2,1,0:T(8,128)(2,1)} %bitcast.139, bf16[16,64,1]{2,1,0:T(8,128)(2,1)} %copy.30, bf16[16,64,1]{2,1,0:T(8,128)(2,1)} %copy.31, bf16[16,64,126]{2,1,0:T(8,128)(2,1)S(1)} %concatenate.28), dimensions={2} | concatenate | bytes 5767168 | tf_op jit(solution)/shard_map/concatenate | solution.py:76
  287.0 38.0 %all_to_all.35 = bf16[16,64,1408]{2,1,0:T(8,128)(2,1)S(1)} all-to-all(bf16[16,64,1408]{2,1,0:T(8,128)(2,1)S(1)} %concatenate.32), channel_id=1, replica_groups=mesh['dp'=16,'section'=2,'tensor'=8] {'dp'}, dimensions={0} | all-to-all | bytes 5767168 | tf_op jit(solution)/shard_map/all_to_all | solution.py:86
  326.7 25.9 %all_to_all.36 = bf16[16,64,1024]{2,1,0:T(8,128)(2,1)S(1)} all-to-all(bf16[16,64,1024]{2,1,0:T(8,128)(2,1)S(1)} %broadcast_in_dim.73), channel_id=1, replica_groups=mesh['dp'=16,'section'=2,'tensor'=8] {'dp'}, dimensions={0} | all-to-all | bytes 4194304 | tf_op jit(solution)/shard_map/all_to_all | solution.py:49
  352.6 5.3 %fusion.27 = bf16[1024,1024]{1,0:T(8,128)(2,1)} fusion(bf16[1024,1024]{1,0:T(8,128)(2,1)S(1)} %bitcast.137, bf16[1024,1024]{1,0:T(8,128)(2,1)} %collective-permute-done.4, pred[]{:T(512)S(6)} %eq.18, bf16[1,1024,1024]{2,1,0:T(8,128)(2,1)S(1)} %copy-done.9), kind=kOutput, calls=%fused_computation.33 | convolution fusion | flops 2149580800 | bytes 8388609 | tf_op jit(solution)/shard_map/dot_general | solution.py:103
  357.9 78.4 %all-reduce.5.cloned.1.call-done = bf16[1024,1024]{1,0:T(8,128)(2,1)} async-done(((bf16[1024,1024]{1,0:T(8,128)(2,1)}), bf16[1024,1024]{1,0:T(8,128)(2,1)}) %all-reduce.5.cloned.1.call-update) | async-done | bytes 2097168 | tf_op jit(solution)/shard_map/psum | solution.py:106
  436.3 3.9 fusion.5
  (69 shorter events, 4.7 us)
Async XLA Ops:
  24.9 7.6 %copy-start.5 = (s32[2048]{0:T(1024)S(1)}, s32[2048]{0:T(1024)}, u32[]{:S(2)}) copy-start(s32[2048]{0:T(1024)} %param.8) | copy-start | bytes 24580
  24.9 34.7 %all-to-all-start = ((bf16[128,16,512]{2,0,1:T(8,128)(2,1)}), bf16[128,16,512]{2,0,1:T(8,128)(2,1)S(1)}, u32[]{:S(2)}, u32[]{:S(2)}) async-start(bf16[128,16,512]{2,0,1:T(8,128)(2,1)} %bitcast.133), calls=%async_computation | async-start | bytes 4194304 | tf_op jit(solution)/shard_map/all_to_all | solution.py:126
  32.5 44.2 %collective-permute-start.2 = (bf16[1024,1024]{1,0:T(8,128)(2,1)}, bf16[1024,1024]{1,0:T(8,128)(2,1)}, u32[]{:S(2)}, u32[]{:S(2)}) collective-permute-start(bf16[1024,1024]{1,0:T(8,128)(2,1)} %bitcast.152), channel_id=1, source_target_pairs={{0,8},{8,0},{1,9},{9,1},{2,10},{10,2},{3,11},{11,3},{4,12},{12,4},... | collective-permute-start | bytes 6291464 | tf_op jit(solution)/shard_map/ppermute | solution.py:116
  70.6 0.7 copy-start.6
  70.8 5.9 %copy-start = (bf16[1024,512]{1,0:T(8,128)(2,1)}, bf16[1024,512]{1,0:T(8,128)(2,1)S(1)}, u32[]{:S(2)}) copy-start(bf16[1024,512]{1,0:T(8,128)(2,1)S(1)} %get-tuple-element.7) | copy-start | bytes 3145732
  70.8 2.8 collective-permute-start
  71.3 2.2 collective-permute-start.1
  71.4 3.3 collective-permute-start.3
  73.6 3.1 copy-start.4
  74.7 2.0 copy-start.8
  86.0 10.0 %copy-start.7 = (s32[2048]{0:T(1024)S(1)}, s32[2048]{0:T(1024)}, u32[]{:S(2)}) copy-start(s32[2048]{0:T(1024)} %param.9) | copy-start | bytes 24580
  86.0 49.3 %all-to-all-start.1 = ((bf16[16,64,1408]{2,1,0:T(8,128)(2,1)}), bf16[16,64,1408]{2,1,0:T(8,128)(2,1)S(1)}, u32[]{:S(2)}, u32[]{:S(2)}) async-start(bf16[16,64,1408]{2,1,0:T(8,128)(2,1)} %concatenate.29), calls=%async_computation.1 | async-start | bytes 5767168 | tf_op jit(solution)/shard_map/all_to_all | solution.py:86
  94.4 52.4 %collective-permute-start.4 = (bf16[1024,1024]{1,0:T(8,128)(2,1)}, bf16[1024,1024]{1,0:T(8,128)(2,1)}, u32[]{:S(2)}, u32[]{:S(2)}) collective-permute-start(bf16[1024,1024]{1,0:T(8,128)(2,1)} %bitcast.153), channel_id=1, source_target_pairs={{0,8},{8,0},{1,9},{9,1},{2,10},{10,2},{3,11},{11,3},{4,12},{12,4},... | collective-permute-start | bytes 6291464 | tf_op jit(solution)/shard_map/ppermute | solution.py:116
  138.3 38.3 %all-to-all-start.2 = ((bf16[16,64,1024]{2,1,0:T(8,128)(2,1)}), bf16[16,64,1024]{2,1,0:T(8,128)(2,1)S(1)}, u32[]{:S(2)}, u32[]{:S(2)}) async-start(bf16[16,64,1024]{2,1,0:T(8,128)(2,1)} %broadcast_in_dim.71), calls=%async_computation.2 | async-start | bytes 4194304 | tf_op jit(solution)/shard_map/all_to_all | solution.py:49
  146.8 121.3 %all-reduce.3.cloned.1.call-start = ((), (), s32[]{:S(2)}) async-start(), calls=%async_computation.5 | async-start | bytes 4194304 | tf_op jit(solution)/shard_map/psum | solution.py:106
  181.9 86.3 %copy-start.1 = (bf16[1024,512]{1,0:T(8,128)(2,1)S(1)}, bf16[1024,512]{1,0:T(8,128)(2,1)}, u32[]{:S(2)}) copy-start(bf16[1024,512]{1,0:T(8,128)(2,1)} %copy-done) | copy-start | bytes 3145732
  181.9 254.4 %all-reduce.5.cloned.1.call-start = ((), (), s32[]{:S(2)}) async-start(), calls=%async_computation.6 | async-start | bytes 4194304 | tf_op jit(solution)/shard_map/psum | solution.py:106
  271.4 8.0 %copy-start.2 = (bf16[1024,1024]{1,0:T(8,128)(2,1)}, bf16[1024,1024]{1,0:T(8,128)(2,1)S(1)}, u32[]{:S(2)}) copy-start(bf16[1024,1024]{1,0:T(8,128)(2,1)S(1)} %get-tuple-element.6) | copy-start | bytes 6291460
  326.7 26.0 %copy-start.9 = (bf16[1,1024,1024]{2,1,0:T(8,128)(2,1)S(1)}, bf16[1,1024,1024]{2,1,0:T(8,128)(2,1)}, u32[]{:S(2)}) copy-start(bf16[1,1024,1024]{2,1,0:T(8,128)(2,1)} %param.13) | copy-start | bytes 6291460
  357.9 78.4 %copy-start.3 = (bf16[1024,1024]{1,0:T(8,128)(2,1)S(1)}, bf16[1024,1024]{1,0:T(8,128)(2,1)}, u32[]{:S(2)}) copy-start(bf16[1024,1024]{1,0:T(8,128)(2,1)} %copy-done.2) | copy-start | bytes 6291460
Sparse Core Ops, SparseCore 0:
  182.0 86.0 all-reduce.2
  358.1 78.1 all-reduce.4

commit v3 on v2

--- a/solution.py
+++ b/solution.py
@@ -9,6 +9,7 @@
 KEYVALUE_HEADS = 8
 QUERY_HEADS = 64
 MICRO_TOKENS = 32
+HEAD_WIDTH = 128
 M = 4
 
 
@@ -51,9 +52,7 @@
     )
 
 
-def section_layer(
-    hidden, sentence_segment_rows, gain_row, query_weight, key_value_matrix, out_weight
-):
+def section_layer(hidden, sentence_segment_rows, gain_row, joined_weight, out_weight):
     slice_width = hidden.shape[1]
     row_count = hidden.shape[0]
     group_count = lax.axis_size("dp")
@@ -64,19 +63,15 @@
     )
     widened = hidden.astype(jnp.float32)
     normed_rows = (widened * gain_row[None, :]).astype(jnp.bfloat16)
-    query_terms = jnp.dot(normed_rows, query_weight, preferred_element_type=jnp.float32)
-    keyval_terms = jnp.dot(
-        normed_rows, key_value_matrix.reshape(slice_width, -1), preferred_element_type=jnp.float32
-    )
-    query_width = query_terms.shape[1]
-    keyval_width = keyval_terms.shape[1]
+    joined_terms = jnp.dot(normed_rows, joined_weight, preferred_element_type=jnp.float32)
+    query_width = out_weight.shape[0]
+    keyval_width = joined_terms.shape[1] - query_width
     square_terms = jnp.sum(widened * widened, axis=1, keepdims=True)
     square_high = lax.reduce_precision(square_terms, exponent_bits=8, mantissa_bits=7)
     square_low = square_terms - square_high
     payload = jnp.concatenate(
         [
-            query_terms.astype(jnp.bfloat16),
-            keyval_terms.astype(jnp.bfloat16),
+            joined_terms.astype(jnp.bfloat16),
             square_high.astype(jnp.bfloat16),
             square_low.astype(jnp.bfloat16),
             jnp.zeros((row_count, 126), jnp.bfloat16),
@@ -91,11 +86,10 @@
     root_mean_square = jnp.sqrt(own_squares / MODEL_WIDTH + norm_epsilon)
     scaled_sums = summed[:, : query_width + keyval_width] / root_mean_square[:, None]
     query_rows = scaled_sums[:, :query_width].astype(jnp.bfloat16)
-    kv_heads = key_value_matrix.shape[1]
     key_value_rows = (
         scaled_sums[:, query_width:]
         .astype(jnp.bfloat16)
-        .reshape(own_rows, kv_heads, key_value_matrix.shape[2])
+        .reshape(own_rows, -1, 2 * HEAD_WIDTH)
     )
     attended_rows = causal_block_attend(
         query_rows, key_value_rows, own_segments, QUERY_HEADS // KEYVALUE_HEADS
@@ -111,30 +105,32 @@
     section_count = lax.axis_size("section")
     section_index = lax.axis_index("section")
     group_count = lax.axis_size("dp")
-    own = (gain[0], w_query[0], key_value_weight[0], w_out[0])
+    slice_width = w_query.shape[1]
+    joined = jnp.concatenate(
+        [w_query[0], key_value_weight[0].reshape(slice_width, -1)], axis=1
+    )
+    own = (gain[0], joined, w_out[0])
     swap = [(i, (i + 1) % section_count) for i in range(section_count)]
     other = lax.ppermute(own, "section", swap)
     entry_rows, model_width = tokens.shape
-    slice_width = model_width // group_count
-    half_width = slice_width // section_count
-    my_columns = lax.dynamic_slice_in_dim(
-        tokens.reshape(entry_rows, group_count, section_count, half_width),
-        section_index,
-        1,
-        axis=2,
-    ).reshape(entry_rows, group_count, half_width)
-    spread = lax.all_to_all(my_columns, "dp", 1, 0, tiled=True).reshape(-1, half_width)
-    arranged = jnp.take(spread, order, axis=0)
-    rows_here = arranged.shape[0] // section_count
-    both = arranged.reshape(section_count, rows_here, half_width)
-    mine = lax.dynamic_index_in_dim(both, section_index, 0, keepdims=False)
-    theirs = lax.dynamic_index_in_dim(both, 1 - section_index, 0, keepdims=False)
-    received = lax.ppermute(theirs, "section", swap)
-    hidden = jnp.where(
-        section_index == 0,
-        jnp.concatenate([mine, received], axis=1),
-        jnp.concatenate([received, mine], axis=1),
+    part_rows = entry_rows // section_count
+    my_rows = lax.dynamic_slice_in_dim(tokens, section_index * part_rows, part_rows)
+    got = lax.all_to_all(
+        my_rows.reshape(part_rows, group_count, model_width // group_count), "dp", 1, 0, tiled=True
+    ).reshape(group_count * part_rows, -1)
+    received = lax.ppermute(got, "section", swap)
+    pool = jnp.concatenate([got, received], axis=0)
+    rows_here = group_count * entry_rows // section_count
+    my_order = lax.dynamic_slice_in_dim(order, section_index * rows_here, rows_here)
+    source_group = my_order // entry_rows
+    within = my_order % entry_rows
+    from_other = (within // part_rows) != section_index
+    pool_index = (
+        jnp.where(from_other, group_count * part_rows, 0)
+        + source_group * part_rows
+        + within % part_rows
     )
+    hidden = jnp.take(pool, pool_index, axis=0)
     my_segments = lax.dynamic_slice_in_dim(
         segments, section_index * rows_here, rows_here
     ).reshape(-1, MICRO_TOKENS)

time: 448 us -> 437 us (0.975)
  blocking collectives: 64 us -> 98.4 us
  waiting for transfers between devices: 262 us -> 240 us
  local copies, waits for them, and re-layouts: 43.3 us -> 24.2 us
  starting transfers between devices: 26.8 us -> 16.4 us
  other arithmetic: 11 us -> 17.8 us
    all_to_all x0 -> x1, blocking collectives: none -> 34.4 us  [on_device(): lax.all_to_all(my_rows.reshape(part_rows, group_count, model_width // gro...]
    all_to_all x1 -> x0, waiting for transfers between devices: 27.1 us -> none  [on_device(): lax.all_to_all(my_columns, 'dp', 1, 0, tiled=True).reshape(-1, half_width)]
    dynamic_slice x2 -> x1, local copies, waits for them, and re-layouts: 10.6 us -> 1.73 us  [on_device(): lax.dynamic_slice_in_dim(tokens, section_index * part_rows, part_rows)]
    all_to_all x1 -> x0, starting transfers between devices: 7.61 us -> none  [on_device(): lax.all_to_all(my_columns, 'dp', 1, 0, tiled=True).reshape(-1, half_width)]
    reshape x1, local copies, waits for them, and re-layouts: 7.79 us -> 0.23 us  [on_device(): my_rows.reshape(part_rows, group_count, model_width // group_count)]
    concatenate x0 -> x2, other arithmetic: none -> 5.86 us  [the longest x1 4.13 us: on_device(): pool = jnp.concatenate([got, received], axis=0)]
    dot_general x4 -> x2, matrix products: 14.2 us -> 13.6 us  [section_layer(): jnp.dot(normed_rows, joined_weight, preferred_element_type=jnp.float32)]
  transfers between devices with their start and end apart: 10 -> 8, of which waited for: 6 -> 5; matrix products, arithmetic and copies ran while one was open for 4% -> 5% of each run, Pallas kernels for 0% -> 0%
where the time goes in v3:
time: 437 us; the launch traced here: 436 us
  waiting for transfers between devices  240 us (55%)
  blocking collectives  98.4 us (23%)
  matrix products  25.9 us (6%)
  local copies, waits for them, and re-layouts  24.2 us (6%)
  other arithmetic  17.8 us (4%)
  starting transfers between devices  16.4 us (4%)
  between operations  13.7 us (3%)
    psum x2, waiting for transfers between devices, section_layer(): lax.psum(head_terms.astype(jnp.bfloat16), 'tensor').astype(jnp.float32)  164 us
    all_to_all x1, waiting for transfers between devices, section_layer(): lax.all_to_all(payload.reshape(group_count, own_rows, payload.shape[1]),...  41.8 us
    all_to_all x1, blocking collectives, section_layer(): lax.all_to_all(payload.reshape(group_count, own_rows, payload.shape[1]),...  38 us
    all_to_all x1, blocking collectives, on_device(): lax.all_to_all(my_rows.reshape(part_rows, group_count, model_width // gro...  34.4 us
    all_to_all x1, waiting for transfers between devices, gathered_over(): lax.all_to_all(spread, axis, 0, 0, tiled=False)  27.5 us
    all_to_all x1, blocking collectives, gathered_over(): lax.all_to_all(spread, axis, 0, 0, tiled=False)  26 us
    dot_general x2, matrix products, section_layer(): jnp.dot(normed_rows, joined_weight, preferred_element_type=jnp.float32)  13.6 us
    dot_general x2, matrix products, section_layer(): jnp.dot(gathered_over(attended_rows, 'dp'), out_weight, preferred_element...  11.2 us
  transfers between devices with their start and end apart: 8, of which 5 were waited for; matrix products, arithmetic and copies ran while one was open for 5% of the time, Pallas kernels for 0%

profile of v3, /device:TPU:2, one launch (start us, length us, event | category | flops | bytes accessed | tf_op | source)
XLA Modules:
  0.0 436.0 jit_solution(9176898702532112345)
XLA Ops:
  6.5 1.7 constant_dynamic-slice_fusion.1
  8.5 34.4 %all_to_all.35 = bf16[64,16,1024]{2,0,1:T(8,128)(2,1)S(1)} all-to-all(bf16[64,16,1024]{2,0,1:T(8,128)(2,1)S(1)} %bitcast.104), channel_id=1, replica_groups=mesh['dp'=16,'section'=2,'tensor'=8] {'dp'}, dimensions={1} | all-to-all | bytes 4194304 | tf_op jit(solution)/shard_map/all_to_all | solution.py:118
  43.0 1.7 pad_maximum_fusion.1
  44.7 0.5 collective-permute-start.2
  45.3 5.7 %collective-permute-done.1 = f32[1024]{0:T(1024)S(1)} collective-permute-done((f32[1024]{0:T(1024)S(1)}, f32[1024]{0:T(1024)S(1)}, u32[]{:S(2)}, u32[]{:S(2)}) %collective-permute-start.1) | collective-permute-done | bytes 4128 | tf_op jit(solution)/shard_map/ppermute | solution.py:114
  51.0 4.1 pad_maximum_fusion
  55.1 7.7 %gather_fusion = bf16[1024,1024]{1,0:T(8,128)(2,1)S(1)} fusion(bf16[2048,1024]{1,0:T(8,128)(2,1)} %pad_maximum_fusion, s32[1024]{0:T(1024)S(1)} %broadcast_clamp_fusion), kind=kCustom, calls=%fused_computation | custom fusion | bytes 4198400 | tf_op jit(solution)/shard_map/jit(_take)/gather | solution.py:133
  62.9 0.7 fusion.1
  64.2 6.2 %convolution_convert_fusion.1 = bf16[1024,1280]{1,0:T(8,128)(2,1)} fusion(bf16[1024,1280]{1,0:T(8,128)(2,1)} %collective-permute-done.2, pred[]{:T(512)S(6)} %eq.17, f32[1024]{0:T(1024)S(1)} %get-tuple-element.12, bf16[1024,1024]{1,0:T(8,128)(2,1)S(1)} %gather_fusion, pred[1024]{0:T(1024)(128)(4,1)S(1)} %get-tuple-element.7, ...), kind=kOutput, calls=%fused_computation.17 | convolution fusion | flops 2696413184 | bytes 9966593 | tf_op jit(solution)/shard_map/dot_general | solution.py:66
  70.4 5.8 %concatenate.24 = bf16[16,64,1408]{2,1,0:T(8,128)(2,1)} concatenate(bf16[16,64,1280]{2,1,0:T(8,128)(2,1)} %bitcast.107, bf16[16,64,1]{2,1,0:T(8,128)(2,1)S(1)} %copy.35, bf16[16,64,1]{2,1,0:T(8,128)(2,1)S(1)} %copy.36, bf16[16,64,126]{2,1,0:T(8,128)(2,1)S(1)} %concatenate.23), dimensions={2} | concatenate | bytes 5767168 | tf_op jit(solution)/shard_map/concatenate | solution.py:72
  76.2 5.8 %all-to-all-start.1 = ((bf16[16,64,1408]{2,1,0:T(8,128)(2,1)}), bf16[16,64,1408]{2,1,0:T(8,128)(2,1)}, u32[]{:S(2)}, u32[]{:S(2)}) async-start(bf16[16,64,1408]{2,1,0:T(8,128)(2,1)} %concatenate.24), calls=%async_computation.1 | async-start | bytes 5767168 | tf_op jit(solution)/shard_map/all_to_all | solution.py:81
  82.0 0.6 collective-permute-start.3
  82.8 41.8 %all-to-all-done.1 = bf16[16,64,1408]{2,1,0:T(8,128)(2,1)} async-done(((bf16[16,64,1408]{2,1,0:T(8,128)(2,1)}), bf16[16,64,1408]{2,1,0:T(8,128)(2,1)}, u32[]{:S(2)}, u32[]{:S(2)}) %all-to-all-start.1) | async-done | bytes 2883616 | tf_op jit(solution)/shard_map/all_to_all | solution.py:81
  124.5 2.2 convert_reduce_fusion.1
  127.1 0.3 fusion.61
  127.8 1.6 broadcast_in_dim.75
  129.4 9.2 %all-to-all-start.2 = ((bf16[16,64,1024]{2,1,0:T(8,128)(2,1)}), bf16[16,64,1024]{2,1,0:T(8,128)(2,1)}, u32[]{:S(2)}, u32[]{:S(2)}) async-start(bf16[16,64,1024]{2,1,0:T(8,128)(2,1)} %broadcast_in_dim.75), calls=%async_computation.2 | async-start | bytes 4194304 | tf_op jit(solution)/shard_map/all_to_all | solution.py:50
  138.8 27.5 %all-to-all-done.2 = bf16[16,64,1024]{2,1,0:T(8,128)(2,1)} async-done(((bf16[16,64,1024]{2,1,0:T(8,128)(2,1)}), bf16[16,64,1024]{2,1,0:T(8,128)(2,1)}, u32[]{:S(2)}, u32[]{:S(2)}) %all-to-all-start.2) | async-done | bytes 2097184 | tf_op jit(solution)/shard_map/all_to_all | solution.py:50
  166.3 5.9 %fusion.20 = bf16[1024,1024]{1,0:T(8,128)(2,1)} fusion(bf16[1024,1024]{1,0:T(8,128)(2,1)} %bitcast.21, bf16[1024,1024]{1,0:T(8,128)(2,1)} %collective-permute-done.3, pred[]{:T(512)S(6)} %eq.17, bf16[1,1024,1024]{2,1,0:T(8,128)(2,1)} %param.13), kind=kOutput, calls=%fused_computation.33 | convolution fusion | flops 2149580800 | bytes 8388609 | tf_op jit(solution)/shard_map/dot_general | solution.py:97
  172.3 86.3 %all-reduce.3.cloned.1.call-done = bf16[1024,1024]{1,0:T(8,128)(2,1)} async-done(((bf16[1024,1024]{1,0:T(8,128)(2,1)}), bf16[1024,1024]{1,0:T(8,128)(2,1)}) %all-reduce.3.cloned.1.call-update) | async-done | bytes 2097168 | tf_op jit(solution)/shard_map/psum | solution.py:100
  258.6 4.0 fusion.4
  262.9 0.9 copy.41
  263.8 7.5 %convolution_convert_fusion = bf16[1024,1280]{1,0:T(8,128)(2,1)} fusion(bf16[1024,1280]{1,0:T(8,128)(2,1)} %collective-permute-done.2, pred[]{:T(512)S(6)} %eq.21, bf16[1024,1024]{1,0:T(8,128)(2,1)} %get-tuple-element.6, f32[1024]{0:T(1024)S(1)} %get-tuple-element.11, bf16[1024,256]{1,0:T(8,128)(2,1)S(1)} %bitcast.115, bf16[1024,1024]{1,0:T(8,128)(2,1)} %bitcast.110), kind=kOutput, calls=%fused_computation.16 | convolution fusion | flops 2695364608 | bytes 9965569 | tf_op jit(solution)/shard_map/dot_general | solution.py:66
  271.3 4.8 %concatenate.26 = bf16[16,64,1408]{2,1,0:T(8,128)(2,1)S(1)} concatenate(bf16[16,64,1280]{2,1,0:T(8,128)(2,1)} %bitcast.108, bf16[16,64,1]{2,1,0:T(8,128)(2,1)S(1)} %copy.40, bf16[16,64,1]{2,1,0:T(8,128)(2,1)} %copy.41, bf16[16,64,126]{2,1,0:T(8,128)(2,1)S(1)} %concatenate.23), dimensions={2} | concatenate | bytes 5767168 | tf_op jit(solution)/shard_map/concatenate | solution.py:72
  276.1 38.0 %all_to_all.36 = bf16[16,64,1408]{2,1,0:T(8,128)(2,1)S(1)} all-to-all(bf16[16,64,1408]{2,1,0:T(8,128)(2,1)S(1)} %concatenate.26), channel_id=1, replica_groups=mesh['dp'=16,'section'=2,'tensor'=8] {'dp'}, dimensions={0} | all-to-all | bytes 5767168 | tf_op jit(solution)/shard_map/all_to_all | solution.py:81
  314.1 0.4 convert_reduce_fusion
  314.9 0.3 fusion.62
  315.6 0.3 broadcast_in_dim.77
  315.8 26.0 %all_to_all.37 = bf16[16,64,1024]{2,1,0:T(8,128)(2,1)S(1)} all-to-all(bf16[16,64,1024]{2,1,0:T(8,128)(2,1)S(1)} %broadcast_in_dim.77), channel_id=1, replica_groups=mesh['dp'=16,'section'=2,'tensor'=8] {'dp'}, dimensions={0} | all-to-all | bytes 4194304 | tf_op jit(solution)/shard_map/all_to_all | solution.py:50
  341.8 5.3 %fusion.23 = bf16[1024,1024]{1,0:T(8,128)(2,1)} fusion(bf16[1024,1024]{1,0:T(8,128)(2,1)S(1)} %bitcast.112, bf16[1024,1024]{1,0:T(8,128)(2,1)} %collective-permute-done.3, pred[]{:T(512)S(6)} %eq.21, bf16[1,1024,1024]{2,1,0:T(8,128)(2,1)S(1)} %copy-done.6), kind=kOutput, calls=%fused_computation.34 | convolution fusion | flops 2149580800 | bytes 8388609 | tf_op jit(solution)/shard_map/dot_general | solution.py:97
  347.2 78.2 %all-reduce.5.cloned.1.call-done = bf16[1024,1024]{1,0:T(8,128)(2,1)} async-done(((bf16[1024,1024]{1,0:T(8,128)(2,1)}), bf16[1024,1024]{1,0:T(8,128)(2,1)}) %all-reduce.5.cloned.1.call-update) | async-done | bytes 2097168 | tf_op jit(solution)/shard_map/psum | solution.py:100
  425.3 3.9 fusion.5
  (57 shorter events, 3.0 us)
Async XLA Ops:
  8.5 34.5 %copy-start.1 = (bf16[1,1024,1024]{2,1,0:T(8,128)(2,1)S(1)}, bf16[1,1024,1024]{2,1,0:T(8,128)(2,1)}, u32[]{:S(2)}) copy-start(bf16[1,1024,1024]{2,1,0:T(8,128)(2,1)} %param.11) | copy-start | bytes 6291460
  8.5 34.4 %copy-start.2 = (bf16[1,1024,1,256]{3,1,2,0:T(8,128)(2,1)S(1)}, bf16[1,1024,1,256]{3,1,2,0:T(8,128)(2,1)}, u32[]{:S(2)}) copy-start(bf16[1,1024,1,256]{3,1,2,0:T(8,128)(2,1)} %param.12) | copy-start | bytes 1572868
  43.0 8.0 %collective-permute-start = (bf16[1024,1024]{1,0:T(8,128)(2,1)S(1)}, bf16[1024,1024]{1,0:T(8,128)(2,1)}, u32[]{:S(2)}, u32[]{:S(2)}) collective-permute-start(bf16[1024,1024]{1,0:T(8,128)(2,1)S(1)} %bitcast.105), channel_id=1, source_target_pairs={{0,8},{8,0},{1,9},{9,1},{2,10},{10,2},{3,11},{11,3},{4,12},{12,4},... | collective-permute-start | bytes 6291464 | tf_op jit(solution)/shard_map/ppermute | solution.py:121
  43.0 2.2 copy-start.4
  43.0 2.3 copy-start.5
  44.7 19.4 %collective-permute-start.2 = (bf16[1024,1280]{1,0:T(8,128)(2,1)}, bf16[1024,1280]{1,0:T(8,128)(2,1)}, u32[]{:S(2)}, u32[]{:S(2)}) collective-permute-start(bf16[1024,1280]{1,0:T(8,128)(2,1)} %pad_maximum_fusion.1), channel_id=1, source_target_pairs={{0,8},{8,0},{1,9},{9,1},{2,10},{10,2},{3,11},{11,3},{4,12},{12,4},... | collective-permute-start | bytes 7864328 | tf_op jit(solution)/shard_map/ppermute | solution.py:114
  45.2 5.8 %collective-permute-start.1 = (f32[1024]{0:T(1024)S(1)}, f32[1024]{0:T(1024)S(1)}, u32[]{:S(2)}, u32[]{:S(2)}) collective-permute-start(f32[1024]{0:T(1024)S(1)} %bitcast.126), channel_id=1, source_target_pairs={{0,8},{8,0},{1,9},{9,1},{2,10},{10,2},{3,11},{11,3},{4,12},{12,4},... | collective-permute-start | bytes 12296 | tf_op jit(solution)/shard_map/ppermute | solution.py:114
  76.2 6.4 %dynamic-slice-start = ((s32[2048]{0:T(1024)}, s32[]{:T(128)}), s32[1024]{0:T(1024)S(1)}, s32[]{:S(2)}) async-start(s32[2048]{0:T(1024)} %param.9, s32[]{:T(128)} %select_n.91), calls=%async_computation.7 | async-start | bytes 8704 | tf_op jit(solution)/shard_map/dynamic_slice | solution.py:134
  76.2 48.4 %all-to-all-start.1 = ((bf16[16,64,1408]{2,1,0:T(8,128)(2,1)}), bf16[16,64,1408]{2,1,0:T(8,128)(2,1)}, u32[]{:S(2)}, u32[]{:S(2)}) async-start(bf16[16,64,1408]{2,1,0:T(8,128)(2,1)} %concatenate.24), calls=%async_computation.1 | async-start | bytes 5767168 | tf_op jit(solution)/shard_map/all_to_all | solution.py:81
  82.0 56.8 %collective-permute-start.3 = (bf16[1024,1024]{1,0:T(8,128)(2,1)}, bf16[1024,1024]{1,0:T(8,128)(2,1)}, u32[]{:S(2)}, u32[]{:S(2)}) collective-permute-start(bf16[1024,1024]{1,0:T(8,128)(2,1)} %bitcast.128), channel_id=1, source_target_pairs={{0,8},{8,0},{1,9},{9,1},{2,10},{10,2},{3,11},{11,3},{4,12},{12,4},... | collective-permute-start | bytes 6291464 | tf_op jit(solution)/shard_map/ppermute | solution.py:114
  129.4 36.9 %all-to-all-start.2 = ((bf16[16,64,1024]{2,1,0:T(8,128)(2,1)}), bf16[16,64,1024]{2,1,0:T(8,128)(2,1)}, u32[]{:S(2)}, u32[]{:S(2)}) async-start(bf16[16,64,1024]{2,1,0:T(8,128)(2,1)} %broadcast_in_dim.75), calls=%async_computation.2 | async-start | bytes 4194304 | tf_op jit(solution)/shard_map/all_to_all | solution.py:50
  138.6 120.0 %all-reduce.3.cloned.1.call-start = ((), (), s32[]{:S(2)}) async-start(), calls=%async_computation.5 | async-start | bytes 4194304 | tf_op jit(solution)/shard_map/psum | solution.py:100
  172.2 91.6 %copy-start.3 = (bf16[1,1024,1,256]{3,1,2,0:T(8,128)(2,1)S(1)}, bf16[1,1024,1,256]{3,1,2,0:T(8,128)(2,1)}, u32[]{:S(2)}) copy-start(bf16[1,1024,1,256]{3,1,2,0:T(8,128)(2,1)} %param.12) | copy-start | bytes 1572868
  172.2 253.1 %all-reduce.5.cloned.1.call-start = ((), (), s32[]{:S(2)}) async-start(), calls=%async_computation.6 | async-start | bytes 4194304 | tf_op jit(solution)/shard_map/psum | solution.py:100
  315.8 26.0 %copy-start.6 = (bf16[1,1024,1024]{2,1,0:T(8,128)(2,1)S(1)}, bf16[1,1024,1024]{2,1,0:T(8,128)(2,1)}, u32[]{:S(2)}) copy-start(bf16[1,1024,1024]{2,1,0:T(8,128)(2,1)} %param.13) | copy-start | bytes 6291460
  347.1 78.2 %copy-start = (bf16[1024,1024]{1,0:T(8,128)(2,1)S(1)}, bf16[1024,1024]{1,0:T(8,128)(2,1)}, u32[]{:S(2)}) copy-start(bf16[1024,1024]{1,0:T(8,128)(2,1)} %get-tuple-element.6) | copy-start | bytes 6291460
Sparse Core Ops, SparseCore 0:
  172.3 86.2 all-reduce.2
  347.3 78.0 all-reduce.4

commit v4 on v3

--- a/solution.py
+++ b/solution.py
@@ -10,6 +10,7 @@
 QUERY_HEADS = 64
 MICRO_TOKENS = 32
 HEAD_WIDTH = 128
+SPARE_COLUMNS = 128
 M = 4
 
 
@@ -65,19 +66,17 @@
     normed_rows = (widened * gain_row[None, :]).astype(jnp.bfloat16)
     joined_terms = jnp.dot(normed_rows, joined_weight, preferred_element_type=jnp.float32)
     query_width = out_weight.shape[0]
-    keyval_width = joined_terms.shape[1] - query_width
+    keyval_width = joined_terms.shape[1] - query_width - SPARE_COLUMNS
     square_terms = jnp.sum(widened * widened, axis=1, keepdims=True)
     square_high = lax.reduce_precision(square_terms, exponent_bits=8, mantissa_bits=7)
     square_low = square_terms - square_high
-    payload = jnp.concatenate(
-        [
-            joined_terms.astype(jnp.bfloat16),
-            square_high.astype(jnp.bfloat16),
-            square_low.astype(jnp.bfloat16),
-            jnp.zeros((row_count, 126), jnp.bfloat16),
-        ],
-        axis=1,
-    )
+    column = lax.broadcasted_iota(jnp.int32, joined_terms.shape, 1)
+    square_column = query_width + keyval_width
+    payload = jnp.where(
+        column == square_column,
+        square_high,
+        jnp.where(column == square_column + 1, square_low, joined_terms),
+    ).astype(jnp.bfloat16)
     arrived = lax.all_to_all(
         payload.reshape(group_count, own_rows, payload.shape[1]), "dp", 0, 0, tiled=False
     )
@@ -107,7 +106,12 @@
     group_count = lax.axis_size("dp")
     slice_width = w_query.shape[1]
     joined = jnp.concatenate(
-        [w_query[0], key_value_weight[0].reshape(slice_width, -1)], axis=1
+        [
+            w_query[0],
+            key_value_weight[0].reshape(slice_width, -1),
+            jnp.zeros((slice_width, SPARE_COLUMNS), w_query.dtype),
+        ],
+        axis=1,
     )
     own = (gain[0], joined, w_out[0])
     swap = [(i, (i + 1) % section_count) for i in range(section_count)]

time: 437 us -> 426 us (0.975)
  blocking collectives: 98.4 us -> 60.4 us
  waiting for transfers between devices: 240 us -> 266 us
  local copies, waits for them, and re-layouts: 24.2 us -> 13.1 us
  starting transfers between devices: 16.4 us -> 27.4 us
    all_to_all x1 -> x0, blocking collectives: 34.4 us -> none  [on_device(): lax.all_to_all(my_rows.reshape(part_rows, group_count, model_width // gro...]
    all_to_all x0 -> x1, waiting for transfers between devices: none -> 27.1 us  [on_device(): lax.all_to_all(my_rows.reshape(part_rows, group_count, model_width // gro...]
    concatenate x3 -> x1, local copies, waits for them, and re-layouts: 10.7 us -> 0.01 us  [on_device(): jnp.concatenate([w_query[0], key_value_weight[0].reshape(slice_width, -1)...]
    all_to_all x0 -> x1, starting transfers between devices: none -> 7.61 us  [on_device(): lax.all_to_all(my_rows.reshape(part_rows, group_count, model_width // gro...]
  transfers between devices with their start and end apart: 8 -> 9, of which waited for: 5 -> 6; matrix products, arithmetic and copies ran while one was open for 5% -> 5% of each run, Pallas kernels for 0% -> 0%
where the time goes in v4:
time: 426 us; the launch traced here: 425 us
  waiting for transfers between devices  266 us (62%)
  blocking collectives  60.4 us (14%)
  starting transfers between devices  27.4 us (6%)
  matrix products  25.4 us (6%)
  other arithmetic  18.7 us (4%)
  between operations  13.7 us (3%)
  local copies, waits for them, and re-layouts  13.1 us (3%)
    psum x2, waiting for transfers between devices, section_layer(): lax.psum(head_terms.astype(jnp.bfloat16), 'tensor').astype(jnp.float32)  165 us
    all_to_all x1, waiting for transfers between devices, section_layer(): lax.all_to_all(payload.reshape(group_count, own_rows, payload.shape[1]),...  41 us
    all_to_all x1, blocking collectives, section_layer(): lax.all_to_all(payload.reshape(group_count, own_rows, payload.shape[1]),...  36.4 us
    all_to_all x1, waiting for transfers between devices, gathered_over(): lax.all_to_all(spread, axis, 0, 0, tiled=False)  28.4 us
    all_to_all x1, waiting for transfers between devices, on_device(): lax.all_to_all(my_rows.reshape(part_rows, group_count, model_width // gro...  27.1 us
    all_to_all x1, blocking collectives, gathered_over(): lax.all_to_all(spread, axis, 0, 0, tiled=False)  24.1 us
    dot_general x2, matrix products, section_layer(): jnp.dot(normed_rows, joined_weight, preferred_element_type=jnp.float32)  13.1 us
    dot_general x2, matrix products, section_layer(): jnp.dot(gathered_over(attended_rows, 'dp'), out_weight, preferred_element...  11.2 us
  transfers between devices with their start and end apart: 9, of which 6 were waited for; matrix products, arithmetic and copies ran while one was open for 5% of the time, Pallas kernels for 0%

profile of v4, /device:TPU:2, one launch (start us, length us, event | category | flops | bytes accessed | tf_op | source)
XLA Modules:
  0.0 425.1 jit_solution(6153129352031992659)
XLA Ops:
  6.5 1.7 constant_dynamic-slice_fusion.1
  8.3 1.5 copy.55
  9.8 7.6 %all-to-all-start = ((bf16[64,16,1024]{2,0,1:T(8,128)(2,1)}), bf16[64,16,1024]{2,0,1:T(8,128)(2,1)S(1)}, u32[]{:S(2)}, u32[]{:S(2)}) async-start(bf16[64,16,1024]{2,0,1:T(8,128)(2,1)} %bitcast.100), calls=%async_computation | async-start | bytes 4194304 | tf_op jit(solution)/shard_map/all_to_all | solution.py:122
  17.4 27.1 %all-to-all-done = bf16[64,16,1024]{2,0,1:T(8,128)(2,1)S(1)} async-done(((bf16[64,16,1024]{2,0,1:T(8,128)(2,1)}), bf16[64,16,1024]{2,0,1:T(8,128)(2,1)S(1)}, u32[]{:S(2)}, u32[]{:S(2)}) %all-to-all-start) | async-done | bytes 2097184 | tf_op jit(solution)/shard_map/all_to_all | solution.py:122
  44.5 3.8 maximum_maximum_fusion
  48.3 0.5 collective-permute-start.2
  48.9 5.2 %collective-permute-done.1 = f32[1024]{0:T(1024)S(1)} collective-permute-done((f32[1024]{0:T(1024)S(1)}, f32[1024]{0:T(1024)S(1)}, u32[]{:S(2)}, u32[]{:S(2)}) %collective-permute-start.1) | collective-permute-done | bytes 4128 | tf_op jit(solution)/shard_map/ppermute | solution.py:118
  54.1 4.0 pad_maximum_fusion
  58.1 7.7 %gather_fusion = bf16[1024,1024]{1,0:T(8,128)(2,1)S(1)} fusion(bf16[2048,1024]{1,0:T(8,128)(2,1)} %pad_maximum_fusion, s32[1024]{0:T(1024)S(1)} %broadcast_clamp_fusion), kind=kCustom, calls=%fused_computation | custom fusion | bytes 4198400 | tf_op jit(solution)/shard_map/jit(_take)/gather | solution.py:137
  65.8 0.7 fusion
  66.6 7.0 %select_convert_fusion.1 = bf16[1024,1408]{1,0:T(8,128)(2,1)} fusion(bf16[1024,1408]{1,0:T(8,128)(2,1)} %collective-permute-done.2, bf16[1024]{0:T(1024)(128)(2,1)S(1)} %get-tuple-element.14, bf16[1024]{0:T(1024)(128)(2,1)S(1)} %get-tuple-element.13, pred[]{:T(512)S(6)} %eq.53, pred[1408]{0:T(1024)(128)(4,1)S(1)} %get-tuple-element.19, ...), kind=kOutput, calls=%fused_computation.10 | convolution fusion | flops 2969960448 | bytes 10500609 | tf_op jit(solution)/shard_map/dot_general | solution.py:67
  73.6 9.1 %all-to-all-start.1 = ((bf16[16,64,1408]{2,1,0:T(8,128)(2,1)}), bf16[16,64,1408]{2,1,0:T(8,128)(2,1)}, u32[]{:S(2)}, u32[]{:S(2)}) async-start(bf16[16,64,1408]{2,1,0:T(8,128)(2,1)} %bitcast.106), calls=%async_computation.1 | async-start | bytes 5767168 | tf_op jit(solution)/shard_map/all_to_all | solution.py:80
  82.7 1.0 collective-permute-start.3
  83.8 41.0 %all-to-all-done.1 = bf16[16,64,1408]{2,1,0:T(8,128)(2,1)} async-done(((bf16[16,64,1408]{2,1,0:T(8,128)(2,1)}), bf16[16,64,1408]{2,1,0:T(8,128)(2,1)}, u32[]{:S(2)}, u32[]{:S(2)}) %all-to-all-start.1) | async-done | bytes 2883616 | tf_op jit(solution)/shard_map/all_to_all | solution.py:80
  124.8 2.2 convert_reduce_fusion.1
  127.4 0.3 fusion.61
  127.8 0.2 fusion.32
  128.1 1.6 broadcast_in_dim.104
  129.7 9.0 %all-to-all-start.2 = ((bf16[16,64,1024]{2,1,0:T(8,128)(2,1)}), bf16[16,64,1024]{2,1,0:T(8,128)(2,1)}, u32[]{:S(2)}, u32[]{:S(2)}) async-start(bf16[16,64,1024]{2,1,0:T(8,128)(2,1)} %broadcast_in_dim.104), calls=%async_computation.2 | async-start | bytes 4194304 | tf_op jit(solution)/shard_map/all_to_all | solution.py:51
  138.9 28.4 %all-to-all-done.2 = bf16[16,64,1024]{2,1,0:T(8,128)(2,1)} async-done(((bf16[16,64,1024]{2,1,0:T(8,128)(2,1)}), bf16[16,64,1024]{2,1,0:T(8,128)(2,1)}, u32[]{:S(2)}, u32[]{:S(2)}) %all-to-all-start.2) | async-done | bytes 2097184 | tf_op jit(solution)/shard_map/all_to_all | solution.py:51
  167.3 5.9 %fusion.20 = bf16[1024,1024]{1,0:T(8,128)(2,1)} fusion(bf16[1024,1024]{1,0:T(8,128)(2,1)} %bitcast.21, bf16[1024,1024]{1,0:T(8,128)(2,1)} %collective-permute-done.3, pred[]{:T(512)S(6)} %eq.53, bf16[1,1024,1024]{2,1,0:T(8,128)(2,1)} %param.13), kind=kOutput, calls=%fused_computation.33 | convolution fusion | flops 2149580800 | bytes 8388609 | tf_op jit(solution)/shard_map/dot_general | solution.py:96
  173.2 86.5 %all-reduce.3.cloned.1.call-done = bf16[1024,1024]{1,0:T(8,128)(2,1)} async-done(((bf16[1024,1024]{1,0:T(8,128)(2,1)}), bf16[1024,1024]{1,0:T(8,128)(2,1)}) %all-reduce.3.cloned.1.call-update) | async-done | bytes 2097168 | tf_op jit(solution)/shard_map/psum | solution.py:99
  259.7 2.9 fusion.3
  262.7 6.1 %select_convert_fusion = bf16[1024,1408]{1,0:T(8,128)(2,1)S(1)} fusion(bf16[1024,1408]{1,0:T(8,128)(2,1)} %collective-permute-done.2, bf16[1024]{0:T(1024)(128)(2,1)S(1)} %get-tuple-element.12, bf16[1024]{0:T(1024)(128)(2,1)S(1)} %get-tuple-element.11, pred[]{:T(512)S(6)} %eq.57, pred[1408]{0:T(1024)(128)(4,1)S(1)} %get-tuple-element.19, ...), kind=kOutput, calls=%fused_computation.8 | convolution fusion | flops 2968911872 | bytes 10499585 | tf_op jit(solution)/shard_map/dot_general | solution.py:67
  268.8 36.4 %all_to_all.35 = bf16[16,64,1408]{2,1,0:T(8,128)(2,1)S(1)} all-to-all(bf16[16,64,1408]{2,1,0:T(8,128)(2,1)S(1)} %bitcast.107), channel_id=1, replica_groups=mesh['dp'=16,'section'=2,'tensor'=8] {'dp'}, dimensions={0} | all-to-all | bytes 5767168 | tf_op jit(solution)/shard_map/all_to_all | solution.py:80
  305.2 0.4 convert_reduce_fusion
  305.9 0.3 fusion.62
  306.6 0.3 broadcast_in_dim.108
  306.9 24.1 %all_to_all.36 = bf16[16,64,1024]{2,1,0:T(8,128)(2,1)S(1)} all-to-all(bf16[16,64,1024]{2,1,0:T(8,128)(2,1)S(1)} %broadcast_in_dim.108), channel_id=1, replica_groups=mesh['dp'=16,'section'=2,'tensor'=8] {'dp'}, dimensions={0} | all-to-all | bytes 4194304 | tf_op jit(solution)/shard_map/all_to_all | solution.py:51
  330.9 5.3 %fusion.23 = bf16[1024,1024]{1,0:T(8,128)(2,1)} fusion(bf16[1024,1024]{1,0:T(8,128)(2,1)S(1)} %bitcast.111, bf16[1024,1024]{1,0:T(8,128)(2,1)} %collective-permute-done.3, pred[]{:T(512)S(6)} %eq.57, bf16[1,1024,1024]{2,1,0:T(8,128)(2,1)S(1)} %copy-done.6), kind=kOutput, calls=%fused_computation.34 | convolution fusion | flops 2149580800 | bytes 8388609 | tf_op jit(solution)/shard_map/dot_general | solution.py:96
  336.3 78.1 %all-reduce.5.cloned.1.call-done = bf16[1024,1024]{1,0:T(8,128)(2,1)} async-done(((bf16[1024,1024]{1,0:T(8,128)(2,1)}), bf16[1024,1024]{1,0:T(8,128)(2,1)}) %all-reduce.5.cloned.1.call-update) | async-done | bytes 2097168 | tf_op jit(solution)/shard_map/psum | solution.py:99
  414.4 3.9 fusion.5
  (52 shorter events, 1.6 us)
Async XLA Ops:
  9.8 34.7 %copy-start.3 = (bf16[1,1024,1,256]{3,1,2,0:T(8,128)(2,1)S(1)}, bf16[1,1024,1,256]{3,1,2,0:T(8,128)(2,1)}, u32[]{:S(2)}) copy-start(bf16[1,1024,1,256]{3,1,2,0:T(8,128)(2,1)} %param.12) | copy-start | bytes 1572868
  9.8 34.7 %all-to-all-start = ((bf16[64,16,1024]{2,0,1:T(8,128)(2,1)}), bf16[64,16,1024]{2,0,1:T(8,128)(2,1)S(1)}, u32[]{:S(2)}, u32[]{:S(2)}) async-start(bf16[64,16,1024]{2,0,1:T(8,128)(2,1)} %bitcast.100), calls=%async_computation | async-start | bytes 4194304 | tf_op jit(solution)/shard_map/all_to_all | solution.py:122
  17.4 31.5 %copy-start.4 = (f32[1,1024]{1,0:T(1,128)S(1)}, f32[1,1024]{1,0:T(1,128)}, u32[]{:S(2)}) copy-start(f32[1,1024]{1,0:T(1,128)} %param.10) | copy-start | bytes 12292
  17.4 31.5 %copy-start.5 = (s32[2048]{0:T(1024)S(1)}, s32[2048]{0:T(1024)}, u32[]{:S(2)}) copy-start(s32[2048]{0:T(1024)} %param.8) | copy-start | bytes 24580
  44.5 9.6 %collective-permute-start = (bf16[1024,1024]{1,0:T(8,128)(2,1)S(1)}, bf16[1024,1024]{1,0:T(8,128)(2,1)}, u32[]{:S(2)}, u32[]{:S(2)}) collective-permute-start(bf16[1024,1024]{1,0:T(8,128)(2,1)S(1)} %bitcast.104), channel_id=1, source_target_pairs={{0,8},{8,0},{1,9},{9,1},{2,10},{10,2},{3,11},{11,3},{4,12},{12,4},... | collective-permute-start | bytes 6291464 | tf_op jit(solution)/shard_map/ppermute | solution.py:125
  48.3 18.2 %collective-permute-start.2 = (bf16[1024,1408]{1,0:T(8,128)(2,1)}, bf16[1024,1408]{1,0:T(8,128)(2,1)}, u32[]{:S(2)}, u32[]{:S(2)}) collective-permute-start(bf16[1024,1408]{1,0:T(8,128)(2,1)} %maximum_maximum_fusion), channel_id=1, source_target_pairs={{0,8},{8,0},{1,9},{9,1},{2,10},{10,2},{3,11},{11,3},{4,12},{12,4},... | collective-permute-start | bytes 8650760 | tf_op jit(solution)/shard_map/ppermute | solution.py:118
  48.9 5.3 %collective-permute-start.1 = (f32[1024]{0:T(1024)S(1)}, f32[1024]{0:T(1024)S(1)}, u32[]{:S(2)}, u32[]{:S(2)}) collective-permute-start(f32[1024]{0:T(1024)S(1)} %bitcast.125), channel_id=1, source_target_pairs={{0,8},{8,0},{1,9},{9,1},{2,10},{10,2},{3,11},{11,3},{4,12},{12,4},... | collective-permute-start | bytes 12296 | tf_op jit(solution)/shard_map/ppermute | solution.py:118
  73.6 10.1 %dynamic-slice-start = ((s32[2048]{0:T(1024)}, s32[]{:T(128)}), s32[1024]{0:T(1024)S(1)}, s32[]{:S(2)}) async-start(s32[2048]{0:T(1024)} %param.9, s32[]{:T(128)} %select_n.104), calls=%async_computation.7 | async-start | bytes 8704 | tf_op jit(solution)/shard_map/dynamic_slice | solution.py:138
  73.6 51.2 %all-to-all-start.1 = ((bf16[16,64,1408]{2,1,0:T(8,128)(2,1)}), bf16[16,64,1408]{2,1,0:T(8,128)(2,1)}, u32[]{:S(2)}, u32[]{:S(2)}) async-start(bf16[16,64,1408]{2,1,0:T(8,128)(2,1)} %bitcast.106), calls=%async_computation.1 | async-start | bytes 5767168 | tf_op jit(solution)/shard_map/all_to_all | solution.py:80
  82.7 56.2 %collective-permute-start.3 = (bf16[1024,1024]{1,0:T(8,128)(2,1)}, bf16[1024,1024]{1,0:T(8,128)(2,1)}, u32[]{:S(2)}, u32[]{:S(2)}) collective-permute-start(bf16[1024,1024]{1,0:T(8,128)(2,1)} %bitcast.127), channel_id=1, source_target_pairs={{0,8},{8,0},{1,9},{9,1},{2,10},{10,2},{3,11},{11,3},{4,12},{12,4},... | collective-permute-start | bytes 6291464 | tf_op jit(solution)/shard_map/ppermute | solution.py:118
  129.7 37.6 %all-to-all-start.2 = ((bf16[16,64,1024]{2,1,0:T(8,128)(2,1)}), bf16[16,64,1024]{2,1,0:T(8,128)(2,1)}, u32[]{:S(2)}, u32[]{:S(2)}) async-start(bf16[16,64,1024]{2,1,0:T(8,128)(2,1)} %broadcast_in_dim.104), calls=%async_computation.2 | async-start | bytes 4194304 | tf_op jit(solution)/shard_map/all_to_all | solution.py:51
  138.7 121.1 %all-reduce.3.cloned.1.call-start = ((), (), s32[]{:S(2)}) async-start(), calls=%async_computation.5 | async-start | bytes 4194304 | tf_op jit(solution)/shard_map/psum | solution.py:99
  173.2 241.2 %all-reduce.5.cloned.1.call-start = ((), (), s32[]{:S(2)}) async-start(), calls=%async_computation.6 | async-start | bytes 4194304 | tf_op jit(solution)/shard_map/psum | solution.py:99
  259.7 2.9 copy-start.2
  262.7 6.1 %copy-start = (bf16[1024,1024]{1,0:T(8,128)(2,1)}, bf16[1024,1024]{1,0:T(8,128)(2,1)S(1)}, u32[]{:S(2)}) copy-start(bf16[1024,1024]{1,0:T(8,128)(2,1)S(1)} %get-tuple-element.6) | copy-start | bytes 6291460
  306.6 24.4 %copy-start.6 = (bf16[1,1024,1024]{2,1,0:T(8,128)(2,1)S(1)}, bf16[1,1024,1024]{2,1,0:T(8,128)(2,1)}, u32[]{:S(2)}) copy-start(bf16[1,1024,1024]{2,1,0:T(8,128)(2,1)} %param.13) | copy-start | bytes 6291460
  336.2 78.2 %copy-start.1 = (bf16[1024,1024]{1,0:T(8,128)(2,1)S(1)}, bf16[1024,1024]{1,0:T(8,128)(2,1)}, u32[]{:S(2)}) copy-start(bf16[1024,1024]{1,0:T(8,128)(2,1)} %copy-done) | copy-start | bytes 6291460
Sparse Core Ops, SparseCore 0:
  173.3 86.4 all-reduce.2
  336.4 77.9 all-reduce.4

commit v5 on v4

--- a/solution.py
+++ b/solution.py
@@ -17,8 +17,8 @@
 norm_epsilon = 1e-05
 
 
-def causal_block_attend(query_rows, key_value_rows, sentence_segment_rows, query_group_width):
-    block_count, row_count = sentence_segment_rows.shape
+def causal_block_attend(query_rows, key_value_rows, allowed, query_group_width):
+    block_count, row_count = allowed.shape[:2]
     kv_heads = key_value_rows.shape[1]
     head_size = key_value_rows.shape[2] // 2
     query_head_rows = query_rows.reshape(
@@ -30,10 +30,6 @@
     scores = jnp.einsum(
         "bqkgd,bskd->bkgqs", query_head_rows, key_heads, preferred_element_type=jnp.float32
     ) / math.sqrt(head_size)
-    position = jnp.arange(row_count)
-    allowed = (sentence_segment_rows[:, :, None] == sentence_segment_rows[:, None, :]) & (
-        position[None, :] <= position[:, None]
-    )[None]
     raw_weights = jnp.where(allowed[:, None, None], jnp.exp(scores), 0.0)
     totals = jnp.sum(raw_weights, axis=-1, keepdims=True)
     probs = (raw_weights / totals).astype(jnp.bfloat16)
@@ -45,6 +41,14 @@
     )
 
 
+def block_mask(sentence_segment_rows):
+    row_count = sentence_segment_rows.shape[1]
+    position = jnp.arange(row_count)
+    return (sentence_segment_rows[:, :, None] == sentence_segment_rows[:, None, :]) & (
+        position[None, :] <= position[:, None]
+    )[None]
+
+
 def gathered_over(block, axis):
     count = lax.axis_size(axis)
     spread = jnp.broadcast_to(block[None], (count,) + block.shape)
@@ -53,15 +57,10 @@
     )
 
 
-def section_layer(hidden, sentence_segment_rows, gain_row, joined_weight, out_weight):
-    slice_width = hidden.shape[1]
+def section_layer(hidden, own_allowed, gain_row, joined_weight, out_weight):
     row_count = hidden.shape[0]
     group_count = lax.axis_size("dp")
     own_rows = row_count // group_count
-    own_blocks = own_rows // MICRO_TOKENS
-    own_segments = lax.dynamic_slice_in_dim(
-        sentence_segment_rows, lax.axis_index("dp") * own_blocks, own_blocks
-    )
     widened = hidden.astype(jnp.float32)
     normed_rows = (widened * gain_row[None, :]).astype(jnp.bfloat16)
     joined_terms = jnp.dot(normed_rows, joined_weight, preferred_element_type=jnp.float32)
@@ -91,7 +90,7 @@
         .reshape(own_rows, -1, 2 * HEAD_WIDTH)
     )
     attended_rows = causal_block_attend(
-        query_rows, key_value_rows, own_segments, QUERY_HEADS // KEYVALUE_HEADS
+        query_rows, key_value_rows, own_allowed, QUERY_HEADS // KEYVALUE_HEADS
     )
     head_terms = jnp.dot(
         gathered_over(attended_rows, "dp"), out_weight, preferred_element_type=jnp.float32
@@ -123,8 +122,17 @@
         my_rows.reshape(part_rows, group_count, model_width // group_count), "dp", 1, 0, tiled=True
     ).reshape(group_count * part_rows, -1)
     received = lax.ppermute(got, "section", swap)
+    rows_here = group_count * entry_rows // section_count
+    own_blocks = rows_here // (group_count * MICRO_TOKENS)
+    own_segments = lax.dynamic_slice_in_dim(
+        segments,
+        section_index * rows_here + lax.axis_index("dp") * own_blocks * MICRO_TOKENS,
+        own_blocks * MICRO_TOKENS,
+    ).reshape(own_blocks, MICRO_TOKENS)
+    other, received, own_allowed = lax.optimization_barrier(
+        (other, received, block_mask(own_segments))
+    )
     pool = jnp.concatenate([got, received], axis=0)
-    rows_here = group_count * entry_rows // section_count
     my_order = lax.dynamic_slice_in_dim(order, section_index * rows_here, rows_here)
     source_group = my_order // entry_rows
     within = my_order % entry_rows
@@ -135,14 +143,11 @@
         + within % part_rows
     )
     hidden = jnp.take(pool, pool_index, axis=0)
-    my_segments = lax.dynamic_slice_in_dim(
-        segments, section_index * rows_here, rows_here
-    ).reshape(-1, MICRO_TOKENS)
     for layer_index in range(section_count):
         params = jax.tree.map(
             lambda mine, theirs: jnp.where(section_index == layer_index, mine, theirs), own, other
         )
-        hidden = section_layer(hidden, my_segments, *params)
+        hidden = section_layer(hidden, own_allowed, *params)
     return hidden
 
 

time: 426 us -> 399 us (0.937)
  waiting for transfers between devices: 266 us -> 186 us
  blocking collectives: 60.4 us -> 137 us
  starting transfers between devices: 27.4 us -> 8.71 us
    all_to_all x2 -> x0, waiting for transfers between devices: 69.3 us -> none  [the longest x1 41 us: section_layer(): lax.all_to_all(payload.reshape(group_count, own_rows, payload.shape[1]),...]
    all_to_all x1 -> x2, blocking collectives: 36.4 us -> 81.9 us  [section_layer(): lax.all_to_all(payload.reshape(group_count, own_rows, payload.shape[1]),...]
    all_to_all x1 -> x2, blocking collectives: 24.1 us -> 54.9 us  [gathered_over(): lax.all_to_all(spread, axis, 0, 0, tiled=False)]
    all_to_all x2 -> x0, starting transfers between devices: 18.1 us -> none  [the longest x1 9.08 us: section_layer(): lax.all_to_all(payload.reshape(group_count, own_rows, payload.shape[1]),...]
    psum x2, waiting for transfers between devices: 165 us -> 160 us  [section_layer(): lax.psum(head_terms.astype(jnp.bfloat16), 'tensor').astype(jnp.float32)]
    all_to_all x1, waiting for transfers between devices: 27.1 us -> 22.7 us  [on_device(): lax.all_to_all(my_rows.reshape(part_rows, group_count, model_width // gro...]
  transfers between devices with their start and end apart: 9 -> 7, of which waited for: 6 -> 4; matrix products, arithmetic and copies ran while one was open for 5% -> 1% of each run, Pallas kernels for 0% -> 0%
where the time goes in v5:
time: 399 us; the launch traced here: 398 us
  waiting for transfers between devices  186 us (47%)
  blocking collectives  137 us (34%)
  matrix products  23.8 us (6%)
  other arithmetic  16.8 us (4%)
  between operations  13.7 us (3%)
  local copies, waits for them, and re-layouts  12.5 us (3%)
  starting transfers between devices  8.71 us (2%)
    psum x2, waiting for transfers between devices, section_layer(): lax.psum(head_terms.astype(jnp.bfloat16), 'tensor').astype(jnp.float32)  160 us
    all_to_all x2, blocking collectives, section_layer(): lax.all_to_all(payload.reshape(group_count, own_rows, payload.shape[1]),...  81.9 us
    all_to_all x2, blocking collectives, gathered_over(): lax.all_to_all(spread, axis, 0, 0, tiled=False)  54.9 us
    all_to_all x1, waiting for transfers between devices, on_device(): lax.all_to_all(my_rows.reshape(part_rows, group_count, model_width // gro...  22.7 us
    dot_general x2, matrix products, section_layer(): jnp.dot(normed_rows, joined_weight, preferred_element_type=jnp.float32)  11.5 us
    dot_general x2, matrix products, section_layer(): jnp.dot(gathered_over(attended_rows, 'dp'), out_weight, preferred_element...  11.2 us
  transfers between devices with their start and end apart: 7, of which 4 were waited for; matrix products, arithmetic and copies ran while one was open for 1% of the time, Pallas kernels for 0%

profile of v5, /device:TPU:2, one launch (start us, length us, event | category | flops | bytes accessed | tf_op | source)
XLA Modules:
  0.0 398.1 jit_solution(4492791983967993768)
XLA Ops:
  6.5 1.7 constant_dynamic-slice_fusion
  8.3 1.5 copy.55
  9.8 7.6 %all-to-all-start = ((bf16[64,16,1024]{2,0,1:T(8,128)(2,1)}), bf16[64,16,1024]{2,0,1:T(8,128)(2,1)S(1)}, u32[]{:S(2)}, u32[]{:S(2)}) async-start(bf16[64,16,1024]{2,0,1:T(8,128)(2,1)} %bitcast.100), calls=%async_computation | async-start | bytes 4194304 | tf_op jit(solution)/shard_map/all_to_all | solution.py:121
  17.5 3.8 maximum_maximum_fusion
  21.3 0.5 collective-permute-start.2
  21.8 22.7 %all-to-all-done = bf16[64,16,1024]{2,0,1:T(8,128)(2,1)S(1)} async-done(((bf16[64,16,1024]{2,0,1:T(8,128)(2,1)}), bf16[64,16,1024]{2,0,1:T(8,128)(2,1)S(1)}, u32[]{:S(2)}, u32[]{:S(2)}) %all-to-all-start) | async-done | bytes 2097184 | tf_op jit(solution)/shard_map/all_to_all | solution.py:121
  44.5 0.5 collective-permute-start
  45.0 0.8 dynamic_slice.11
  46.0 2.8 collective-permute-done
  48.8 4.0 pad_maximum_fusion
  52.8 7.7 %gather_fusion = bf16[1024,1024]{1,0:T(8,128)(2,1)S(1)} fusion(bf16[2048,1024]{1,0:T(8,128)(2,1)} %pad_maximum_fusion, s32[1024]{0:T(1024)S(1)} %broadcast_clamp_fusion), kind=kCustom, calls=%fused_computation | custom fusion | bytes 4198400 | tf_op jit(solution)/shard_map/jit(_take)/gather | solution.py:145
  60.5 0.7 fusion
  61.2 5.4 %select_convert_fusion.1 = bf16[1024,1408]{1,0:T(8,128)(2,1)S(1)} fusion(bf16[1024,1408]{1,0:T(8,128)(2,1)} %collective-permute-done.1, bf16[1024]{0:T(1024)(128)(2,1)S(1)} %get-tuple-element.24, bf16[1024]{0:T(1024)(128)(2,1)S(1)} %get-tuple-element.23, pred[]{:T(512)S(6)} %eq.48, pred[1408]{0:T(1024)(128)(4,1)S(1)} %get-tuple-element.29, ...), kind=kOutput, calls=%fused_computation.10 | convolution fusion | flops 2969960448 | bytes 10500609 | tf_op jit(solution)/shard_map/dot_general | solution.py:66
  66.6 45.6 %all_to_all.35 = bf16[16,64,1408]{2,1,0:T(8,128)(2,1)S(1)} all-to-all(bf16[16,64,1408]{2,1,0:T(8,128)(2,1)S(1)} %bitcast.107), channel_id=1, replica_groups=mesh['dp'=16,'section'=2,'tensor'=8] {'dp'}, dimensions={0} | all-to-all | bytes 5767168 | tf_op jit(solution)/shard_map/all_to_all | solution.py:79
  112.2 0.4 convert_reduce_fusion.1
  113.0 0.3 fusion.61
  113.3 0.2 fusion.32
  113.6 0.3 broadcast_in_dim.97
  113.9 30.9 %all_to_all.36 = bf16[16,64,1024]{2,1,0:T(8,128)(2,1)S(1)} all-to-all(bf16[16,64,1024]{2,1,0:T(8,128)(2,1)S(1)} %broadcast_in_dim.97), channel_id=1, replica_groups=mesh['dp'=16,'section'=2,'tensor'=8] {'dp'}, dimensions={0} | all-to-all | bytes 4194304 | tf_op jit(solution)/shard_map/all_to_all | solution.py:55
  144.8 5.3 %fusion.20 = bf16[1024,1024]{1,0:T(8,128)(2,1)} fusion(bf16[1024,1024]{1,0:T(8,128)(2,1)S(1)} %bitcast.112, bf16[1024,1024]{1,0:T(8,128)(2,1)} %collective-permute-done.2, pred[]{:T(512)S(6)} %eq.48, bf16[1,1024,1024]{2,1,0:T(8,128)(2,1)} %param.13), kind=kOutput, calls=%fused_computation.33 | convolution fusion | flops 2149580800 | bytes 8388609 | tf_op jit(solution)/shard_map/dot_general | solution.py:95
  150.2 82.2 %all-reduce.3.cloned.1.call-done = bf16[1024,1024]{1,0:T(8,128)(2,1)} async-done(((bf16[1024,1024]{1,0:T(8,128)(2,1)}), bf16[1024,1024]{1,0:T(8,128)(2,1)}) %all-reduce.3.cloned.1.call-update) | async-done | bytes 2097168 | tf_op jit(solution)/shard_map/psum | solution.py:98
  232.3 2.9 fusion.3
  235.3 6.1 %select_convert_fusion = bf16[1024,1408]{1,0:T(8,128)(2,1)S(1)} fusion(bf16[1024,1408]{1,0:T(8,128)(2,1)} %collective-permute-done.1, bf16[1024]{0:T(1024)(128)(2,1)S(1)} %get-tuple-element.22, bf16[1024]{0:T(1024)(128)(2,1)S(1)} %get-tuple-element.21, pred[]{:T(512)S(6)} %eq.49, pred[1408]{0:T(1024)(128)(4,1)S(1)} %get-tuple-element.29, ...), kind=kOutput, calls=%fused_computation.8 | convolution fusion | flops 2968911872 | bytes 10499585 | tf_op jit(solution)/shard_map/dot_general | solution.py:66
  241.4 36.4 %all_to_all.37 = bf16[16,64,1408]{2,1,0:T(8,128)(2,1)S(1)} all-to-all(bf16[16,64,1408]{2,1,0:T(8,128)(2,1)S(1)} %bitcast.106), channel_id=1, replica_groups=mesh['dp'=16,'section'=2,'tensor'=8] {'dp'}, dimensions={0} | all-to-all | bytes 5767168 | tf_op jit(solution)/shard_map/all_to_all | solution.py:79
  277.8 0.4 convert_reduce_fusion
  278.5 0.3 fusion.62
  278.8 0.2 fusion.33
  279.2 0.3 broadcast_in_dim.101
  279.4 23.9 %all_to_all.38 = bf16[16,64,1024]{2,1,0:T(8,128)(2,1)S(1)} all-to-all(bf16[16,64,1024]{2,1,0:T(8,128)(2,1)S(1)} %broadcast_in_dim.101), channel_id=1, replica_groups=mesh['dp'=16,'section'=2,'tensor'=8] {'dp'}, dimensions={0} | all-to-all | bytes 4194304 | tf_op jit(solution)/shard_map/all_to_all | solution.py:55
  303.4 5.9 %fusion.23 = bf16[1024,1024]{1,0:T(8,128)(2,1)} fusion(bf16[1024,1024]{1,0:T(8,128)(2,1)S(1)} %bitcast.111, bf16[1024,1024]{1,0:T(8,128)(2,1)} %collective-permute-done.2, pred[]{:T(512)S(6)} %eq.49, bf16[1,1024,1024]{2,1,0:T(8,128)(2,1)} %param.13), kind=kOutput, calls=%fused_computation.34 | convolution fusion | flops 2149580800 | bytes 8388609 | tf_op jit(solution)/shard_map/dot_general | solution.py:95
  309.3 78.1 %all-reduce.5.cloned.1.call-done = bf16[1024,1024]{1,0:T(8,128)(2,1)} async-done(((bf16[1024,1024]{1,0:T(8,128)(2,1)}), bf16[1024,1024]{1,0:T(8,128)(2,1)}) %all-reduce.5.cloned.1.call-update) | async-done | bytes 2097168 | tf_op jit(solution)/shard_map/psum | solution.py:98
  387.4 3.9 fusion.5
  (46 shorter events, 1.2 us)
Async XLA Ops:
  9.8 7.7 %copy-start.3 = (bf16[1,1024,1,256]{3,1,2,0:T(8,128)(2,1)S(1)}, bf16[1,1024,1,256]{3,1,2,0:T(8,128)(2,1)}, u32[]{:S(2)}) copy-start(bf16[1,1024,1,256]{3,1,2,0:T(8,128)(2,1)} %param.12) | copy-start | bytes 1572868
  9.8 34.7 %all-to-all-start = ((bf16[64,16,1024]{2,0,1:T(8,128)(2,1)}), bf16[64,16,1024]{2,0,1:T(8,128)(2,1)S(1)}, u32[]{:S(2)}, u32[]{:S(2)}) async-start(bf16[64,16,1024]{2,0,1:T(8,128)(2,1)} %bitcast.100), calls=%async_computation | async-start | bytes 4194304 | tf_op jit(solution)/shard_map/all_to_all | solution.py:121
  17.4 27.1 %copy-start.4 = (f32[1,1024]{1,0:T(1,128)S(1)}, f32[1,1024]{1,0:T(1,128)}, u32[]{:S(2)}) copy-start(f32[1,1024]{1,0:T(1,128)} %param.10) | copy-start | bytes 12292
  17.4 28.5 %copy-start.5 = (s32[2048]{0:T(1024)S(1)}, s32[2048]{0:T(1024)}, u32[]{:S(2)}) copy-start(s32[2048]{0:T(1024)} %param.8) | copy-start | bytes 24580
  17.4 214.9 %all-reduce.3.cloned.1.call-start = ((), (), s32[]{:S(2)}) async-start(), calls=%async_computation.5 | async-start | bytes 4194304 | tf_op jit(solution)/shard_map/psum | solution.py:98
  21.3 27.5 %collective-permute-start.1 = (bf16[1024,1408]{1,0:T(8,128)(2,1)}, bf16[1024,1408]{1,0:T(8,128)(2,1)}, u32[]{:S(2)}, u32[]{:S(2)}) collective-permute-start(bf16[1024,1408]{1,0:T(8,128)(2,1)} %maximum_maximum_fusion), channel_id=1, source_target_pairs={{0,8},{8,0},{1,9},{9,1},{2,10},{10,2},{3,11},{11,3},{4,12},{12,4},... | collective-permute-start | bytes 8650760 | tf_op jit(solution)/shard_map/ppermute | solution.py:117
  21.3 27.5 %collective-permute-start.2 = (bf16[1024,1024]{1,0:T(8,128)(2,1)}, bf16[1024,1024]{1,0:T(8,128)(2,1)}, u32[]{:S(2)}, u32[]{:S(2)}) collective-permute-start(bf16[1024,1024]{1,0:T(8,128)(2,1)} %bitcast.6), channel_id=1, source_target_pairs={{0,8},{8,0},{1,9},{9,1},{2,10},{10,2},{3,11},{11,3},{4,12},{12,4},... | collective-permute-start | bytes 6291464 | tf_op jit(solution)/shard_map/ppermute | solution.py:117
  44.5 4.3 %collective-permute-start.3 = (bf16[1024,1024]{1,0:T(8,128)(2,1)S(1)}, bf16[1024,1024]{1,0:T(8,128)(2,1)}, u32[]{:S(2)}, u32[]{:S(2)}) collective-permute-start(bf16[1024,1024]{1,0:T(8,128)(2,1)S(1)} %bitcast.104), channel_id=1, source_target_pairs={{0,8},{8,0},{1,9},{9,1},{2,10},{10,2},{3,11},{11,3},{4,12},{12,4},... | collective-permute-start | bytes 6291464 | tf_op jit(solution)/shard_map/ppermute | solution.py:124
  44.5 4.3 %collective-permute-start = (f32[1024]{0:T(1024)S(1)}, f32[1024]{0:T(1024)S(1)}, u32[]{:S(2)}, u32[]{:S(2)}) collective-permute-start(f32[1024]{0:T(1024)S(1)} %bitcast.126), channel_id=1, source_target_pairs={{0,8},{8,0},{1,9},{9,1},{2,10},{10,2},{3,11},{11,3},{4,12},{12,4},... | collective-permute-start | bytes 12296 | tf_op jit(solution)/shard_map/ppermute | solution.py:117
  150.1 237.3 %all-reduce.5.cloned.1.call-start = ((), (), s32[]{:S(2)}) async-start(), calls=%async_computation.6 | async-start | bytes 4194304 | tf_op jit(solution)/shard_map/psum | solution.py:98
  232.3 2.9 copy-start.2
  235.3 6.1 %copy-start = (bf16[1024,1024]{1,0:T(8,128)(2,1)}, bf16[1024,1024]{1,0:T(8,128)(2,1)S(1)}, u32[]{:S(2)}) copy-start(bf16[1024,1024]{1,0:T(8,128)(2,1)S(1)} %get-tuple-element.16) | copy-start | bytes 6291460
  309.3 78.1 %copy-start.1 = (bf16[1024,1024]{1,0:T(8,128)(2,1)S(1)}, bf16[1024,1024]{1,0:T(8,128)(2,1)}, u32[]{:S(2)}) copy-start(bf16[1024,1024]{1,0:T(8,128)(2,1)} %copy-done) | copy-start | bytes 6291460
Sparse Core Ops, SparseCore 0:
  150.2 82.0 all-reduce.2
  309.5 77.9 all-reduce.4

commit v6 on v5

--- a/solution.py
+++ b/solution.py
@@ -57,31 +57,39 @@
     )
 
 
-def section_layer(hidden, own_allowed, gain_row, joined_weight, out_weight):
+def section_layer(hidden, own_allowed, gain_row, joined_weight, out_weight, known_rms):
     row_count = hidden.shape[0]
     group_count = lax.axis_size("dp")
     own_rows = row_count // group_count
     widened = hidden.astype(jnp.float32)
     normed_rows = (widened * gain_row[None, :]).astype(jnp.bfloat16)
-    joined_terms = jnp.dot(normed_rows, joined_weight, preferred_element_type=jnp.float32)
     query_width = out_weight.shape[0]
-    keyval_width = joined_terms.shape[1] - query_width - SPARE_COLUMNS
-    square_terms = jnp.sum(widened * widened, axis=1, keepdims=True)
-    square_high = lax.reduce_precision(square_terms, exponent_bits=8, mantissa_bits=7)
-    square_low = square_terms - square_high
-    column = lax.broadcasted_iota(jnp.int32, joined_terms.shape, 1)
+    keyval_width = joined_weight.shape[1] - query_width - SPARE_COLUMNS
     square_column = query_width + keyval_width
-    payload = jnp.where(
-        column == square_column,
-        square_high,
-        jnp.where(column == square_column + 1, square_low, joined_terms),
-    ).astype(jnp.bfloat16)
+    if known_rms is None:
+        joined_terms = jnp.dot(normed_rows, joined_weight, preferred_element_type=jnp.float32)
+        square_terms = jnp.sum(widened * widened, axis=1, keepdims=True)
+        square_high = lax.reduce_precision(square_terms, exponent_bits=8, mantissa_bits=7)
+        square_low = square_terms - square_high
+        column = lax.broadcasted_iota(jnp.int32, joined_terms.shape, 1)
+        payload = jnp.where(
+            column == square_column,
+            square_high,
+            jnp.where(column == square_column + 1, square_low, joined_terms),
+        ).astype(jnp.bfloat16)
+    else:
+        payload = jnp.dot(
+            normed_rows, joined_weight[:, :square_column], preferred_element_type=jnp.float32
+        ).astype(jnp.bfloat16)
     arrived = lax.all_to_all(
         payload.reshape(group_count, own_rows, payload.shape[1]), "dp", 0, 0, tiled=False
     )
     summed = jnp.sum(arrived.astype(jnp.float32), axis=0)
-    own_squares = summed[:, query_width + keyval_width] + summed[:, query_width + keyval_width + 1]
-    root_mean_square = jnp.sqrt(own_squares / MODEL_WIDTH + norm_epsilon)
+    if known_rms is None:
+        own_squares = summed[:, square_column] + summed[:, square_column + 1]
+        root_mean_square = jnp.sqrt(own_squares / MODEL_WIDTH + norm_epsilon)
+    else:
+        root_mean_square = known_rms
     scaled_sums = summed[:, : query_width + keyval_width] / root_mean_square[:, None]
     query_rows = scaled_sums[:, :query_width].astype(jnp.bfloat16)
     key_value_rows = (
@@ -129,8 +137,21 @@
         section_index * rows_here + lax.axis_index("dp") * own_blocks * MICRO_TOKENS,
         own_blocks * MICRO_TOKENS,
     ).reshape(own_blocks, MICRO_TOKENS)
-    other, received, own_allowed = lax.optimization_barrier(
-        (other, received, block_mask(own_segments))
+    entry_squares = lax.all_gather(
+        jnp.sum(jnp.square(tokens.astype(jnp.float32)), axis=1), "dp", tiled=True
+    )
+    own_order = lax.dynamic_slice_in_dim(
+        order,
+        section_index * rows_here + lax.axis_index("dp") * own_blocks * MICRO_TOKENS,
+        own_blocks * MICRO_TOKENS,
+    )
+    other, received, own_allowed, first_rms = lax.optimization_barrier(
+        (
+            other,
+            received,
+            block_mask(own_segments),
+            jnp.sqrt(jnp.take(entry_squares, own_order) / MODEL_WIDTH + norm_epsilon),
+        )
     )
     pool = jnp.concatenate([got, received], axis=0)
     my_order = lax.dynamic_slice_in_dim(order, section_index * rows_here, rows_here)
@@ -143,11 +164,13 @@
         + within % part_rows
     )
     hidden = jnp.take(pool, pool_index, axis=0)
+    known_rms = first_rms
     for layer_index in range(section_count):
         params = jax.tree.map(
             lambda mine, theirs: jnp.where(section_index == layer_index, mine, theirs), own, other
         )
-        hidden = section_layer(hidden, own_allowed, *params)
+        hidden = section_layer(hidden, own_allowed, *params, known_rms)
+        known_rms = None
     return hidden
 
 

time: 399 us -> 407 us (1.020)
  blocking collectives: 137 us -> 144 us
    all_gather x0 -> x1, blocking collectives: none -> 22 us  [on_device(): lax.all_gather(jnp.sum(jnp.square(tokens.astype(jnp.float32)), axis=1), '...]
    all_to_all x2, blocking collectives: 81.9 us -> 71.4 us  [section_layer(): lax.all_to_all(payload.reshape(group_count, own_rows, payload.shape[1]),...]
    dot_general x0 -> x1, matrix products: none -> 6.24 us  [section_layer(): jnp.dot(normed_rows, joined_weight[:, :square_column], preferred_element_...]
    dot_general x2 -> x1, matrix products: 11.5 us -> 5.38 us  [section_layer(): jnp.dot(normed_rows, joined_weight, preferred_element_type=jnp.float32)]
    all_to_all x2, blocking collectives: 54.9 us -> 50.7 us  [gathered_over(): lax.all_to_all(spread, axis, 0, 0, tiled=False)]
  transfers between devices with their start and end apart: 7 -> 7, of which waited for: 4 -> 3; matrix products, arithmetic and copies ran while one was open for 1% -> 2% of each run, Pallas kernels for 0% -> 0%
where the time goes in v6:
time: 407 us; the launch traced here: 406 us
  waiting for transfers between devices  183 us (45%)
  blocking collectives  144 us (35%)
  matrix products  23.9 us (6%)
  other arithmetic  19.7 us (5%)
  between operations  13.7 us (3%)
  local copies, waits for them, and re-layouts  13.3 us (3%)
  starting transfers between devices  8.71 us (2%)
    psum x2, waiting for transfers between devices, section_layer(): lax.psum(head_terms.astype(jnp.bfloat16), 'tensor').astype(jnp.float32)  160 us
    all_to_all x2, blocking collectives, section_layer(): lax.all_to_all(payload.reshape(group_count, own_rows, payload.shape[1]),...  71.4 us
    all_to_all x2, blocking collectives, gathered_over(): lax.all_to_all(spread, axis, 0, 0, tiled=False)  50.7 us
    all_to_all x1, waiting for transfers between devices, on_device(): lax.all_to_all(my_rows.reshape(part_rows, group_count, model_width // gro...  22.7 us
    all_gather x1, blocking collectives, on_device(): lax.all_gather(jnp.sum(jnp.square(tokens.astype(jnp.float32)), axis=1), '...  22 us
    dot_general x2, matrix products, section_layer(): jnp.dot(gathered_over(attended_rows, 'dp'), out_weight, preferred_element...  11.2 us
  transfers between devices with their start and end apart: 7, of which 3 were waited for; matrix products, arithmetic and copies ran while one was open for 2% of the time, Pallas kernels for 0%

profile of v6, /device:TPU:2, one launch (start us, length us, event | category | flops | bytes accessed | tf_op | source)
XLA Modules:
  0.0 406.1 jit_solution(17568848213218785807)
XLA Ops:
  6.5 1.7 constant_dynamic-slice_fusion
  8.3 1.5 copy.54
  9.8 7.6 %all-to-all-start = ((bf16[64,16,1024]{2,0,1:T(8,128)(2,1)}), bf16[64,16,1024]{2,0,1:T(8,128)(2,1)S(1)}, u32[]{:S(2)}, u32[]{:S(2)}) async-start(bf16[64,16,1024]{2,0,1:T(8,128)(2,1)} %bitcast.102), calls=%async_computation | async-start | bytes 4194304 | tf_op jit(solution)/shard_map/all_to_all | solution.py:129
  17.5 3.8 maximum_maximum_fusion
  21.3 0.5 collective-permute-start.2
  21.8 22.7 %all-to-all-done = bf16[64,16,1024]{2,0,1:T(8,128)(2,1)S(1)} async-done(((bf16[64,16,1024]{2,0,1:T(8,128)(2,1)}), bf16[64,16,1024]{2,0,1:T(8,128)(2,1)S(1)}, u32[]{:S(2)}, u32[]{:S(2)}) %all-to-all-start) | async-done | bytes 2097184 | tf_op jit(solution)/shard_map/all_to_all | solution.py:129
  44.5 0.5 collective-permute-start
  45.0 0.8 dynamic_slice.14
  45.9 3.1 multiply_reduce_fusion
  48.9 22.0 %all-gather = f32[16,1,128]{2,1,0:T(1,128)S(1)} all-gather(f32[1,1,128]{2,1,0:T(1,128)S(1)} %bitcast.129), channel_id=1, replica_groups=mesh['dp'=16,'section'=2,'tensor'=8] {'dp'}, dimensions={0}, use_global_device_ids=true | all-gather | bytes 8704 | tf_op jit(solution)/shard_map/all_gather | solution.py:140
  71.1 0.8 gather_fusion
  72.1 4.0 pad_maximum_fusion
  76.1 7.7 %gather_fusion.1 = bf16[1024,1024]{1,0:T(8,128)(2,1)S(1)} fusion(bf16[2048,1024]{1,0:T(8,128)(2,1)} %pad_maximum_fusion, s32[1024]{0:T(1024)S(1)} %broadcast_clamp_fusion), kind=kCustom, calls=%fused_computation.1 | custom fusion | bytes 4198400 | tf_op jit(solution)/shard_map/jit(_take)/gather | solution.py:166
  83.8 6.2 %convolution_convert_fusion = bf16[1024,1280]{1,0:T(8,128)(2,1)S(1)} fusion(bf16[1024,1408]{1,0:T(8,128)(2,1)} %collective-permute-done.1, bf16[1024,1408]{1,0:T(8,128)(2,1)} %maximum_maximum_fusion, pred[]{:T(512)S(6)} %eq.46, f32[1024]{0:T(1024)S(1)} %get-tuple-element.22, bf16[1024,1024]{1,0:T(8,128)(2,1)S(1)} %gather_fusion.1, ...), kind=kOutput, calls=%fused_computation.17 | convolution fusion | flops 2691170304 | bytes 9966593 | tf_op jit(solution)/shard_map/dot_general | solution.py:81
  90.1 34.5 %all_to_all.35 = bf16[16,64,1280]{2,1,0:T(8,128)(2,1)S(1)} all-to-all(bf16[16,64,1280]{2,1,0:T(8,128)(2,1)S(1)} %bitcast.110), channel_id=1, replica_groups=mesh['dp'=16,'section'=2,'tensor'=8] {'dp'}, dimensions={0} | all-to-all | bytes 5242880 | tf_op jit(solution)/shard_map/all_to_all | solution.py:84
  124.5 0.4 convert_reduce_fusion.1
  125.0 0.3 fusion.55
  125.7 0.3 broadcast_in_dim.94
  126.0 25.2 %all_to_all.36 = bf16[16,64,1024]{2,1,0:T(8,128)(2,1)S(1)} all-to-all(bf16[16,64,1024]{2,1,0:T(8,128)(2,1)S(1)} %broadcast_in_dim.94), channel_id=1, replica_groups=mesh['dp'=16,'section'=2,'tensor'=8] {'dp'}, dimensions={0} | all-to-all | bytes 4194304 | tf_op jit(solution)/shard_map/all_to_all | solution.py:55
  151.1 5.3 %fusion.19 = bf16[1024,1024]{1,0:T(8,128)(2,1)} fusion(bf16[1024,1024]{1,0:T(8,128)(2,1)S(1)} %bitcast.114, bf16[1024,1024]{1,0:T(8,128)(2,1)} %collective-permute-done.2, pred[]{:T(512)S(6)} %eq.46, bf16[1,1024,1024]{2,1,0:T(8,128)(2,1)} %param.13), kind=kOutput, calls=%fused_computation.34 | convolution fusion | flops 2149580800 | bytes 8388609 | tf_op jit(solution)/shard_map/dot_general | solution.py:103
  156.5 82.0 %all-reduce.3.cloned.1.call-done = bf16[1024,1024]{1,0:T(8,128)(2,1)} async-done(((bf16[1024,1024]{1,0:T(8,128)(2,1)}), bf16[1024,1024]{1,0:T(8,128)(2,1)}) %all-reduce.3.cloned.1.call-update) | async-done | bytes 2097168 | tf_op jit(solution)/shard_map/psum | solution.py:106
  238.4 3.5 fusion.2
  242.0 5.4 %select_convert_fusion = bf16[1024,1408]{1,0:T(8,128)(2,1)S(1)} fusion(bf16[1024,1408]{1,0:T(8,128)(2,1)} %collective-permute-done.1, bf16[1024]{0:T(1024)(128)(2,1)S(1)} %get-tuple-element.24, bf16[1024]{0:T(1024)(128)(2,1)S(1)} %get-tuple-element.23, pred[]{:T(512)S(6)} %eq.51, pred[1408]{0:T(1024)(128)(4,1)S(1)} %get-tuple-element.29, ...), kind=kOutput, calls=%fused_computation.7 | convolution fusion | flops 2968911872 | bytes 10499585 | tf_op jit(solution)/shard_map/dot_general | solution.py:70
  247.4 37.0 %all_to_all.37 = bf16[16,64,1408]{2,1,0:T(8,128)(2,1)S(1)} all-to-all(bf16[16,64,1408]{2,1,0:T(8,128)(2,1)S(1)} %bitcast.109), channel_id=1, replica_groups=mesh['dp'=16,'section'=2,'tensor'=8] {'dp'}, dimensions={0} | all-to-all | bytes 5767168 | tf_op jit(solution)/shard_map/all_to_all | solution.py:84
  284.3 0.4 convert_reduce_fusion
  285.1 0.3 fusion.56
  285.4 0.2 fusion.32
  285.8 0.3 broadcast_in_dim.98
  286.0 25.5 %all_to_all.38 = bf16[16,64,1024]{2,1,0:T(8,128)(2,1)S(1)} all-to-all(bf16[16,64,1024]{2,1,0:T(8,128)(2,1)S(1)} %broadcast_in_dim.98), channel_id=1, replica_groups=mesh['dp'=16,'section'=2,'tensor'=8] {'dp'}, dimensions={0} | all-to-all | bytes 4194304 | tf_op jit(solution)/shard_map/all_to_all | solution.py:55
  311.5 5.9 %fusion.22 = bf16[1024,1024]{1,0:T(8,128)(2,1)} fusion(bf16[1024,1024]{1,0:T(8,128)(2,1)S(1)} %bitcast.113, bf16[1024,1024]{1,0:T(8,128)(2,1)} %collective-permute-done.2, pred[]{:T(512)S(6)} %eq.51, bf16[1,1024,1024]{2,1,0:T(8,128)(2,1)} %param.13), kind=kOutput, calls=%fused_computation.35 | convolution fusion | flops 2149580800 | bytes 8388609 | tf_op jit(solution)/shard_map/dot_general | solution.py:103
  317.5 77.9 %all-reduce.5.cloned.1.call-done = bf16[1024,1024]{1,0:T(8,128)(2,1)} async-done(((bf16[1024,1024]{1,0:T(8,128)(2,1)}), bf16[1024,1024]{1,0:T(8,128)(2,1)}) %all-reduce.5.cloned.1.call-update) | async-done | bytes 2097168 | tf_op jit(solution)/shard_map/psum | solution.py:106
  395.4 3.9 fusion.4
  (47 shorter events, 1.4 us)
Async XLA Ops:
  9.8 7.7 %copy-start.2 = (bf16[1,1024,1,256]{3,1,2,0:T(8,128)(2,1)S(1)}, bf16[1,1024,1,256]{3,1,2,0:T(8,128)(2,1)}, u32[]{:S(2)}) copy-start(bf16[1,1024,1,256]{3,1,2,0:T(8,128)(2,1)} %param.12) | copy-start | bytes 1572868
  9.8 34.7 %all-to-all-start = ((bf16[64,16,1024]{2,0,1:T(8,128)(2,1)}), bf16[64,16,1024]{2,0,1:T(8,128)(2,1)S(1)}, u32[]{:S(2)}, u32[]{:S(2)}) async-start(bf16[64,16,1024]{2,0,1:T(8,128)(2,1)} %bitcast.102), calls=%async_computation | async-start | bytes 4194304 | tf_op jit(solution)/shard_map/all_to_all | solution.py:129
  17.4 221.1 %all-reduce.3.cloned.1.call-start = ((), (), s32[]{:S(2)}) async-start(), calls=%async_computation.5 | async-start | bytes 4194304 | tf_op jit(solution)/shard_map/psum | solution.py:106
  17.5 27.1 %copy-start.3 = (f32[1,1024]{1,0:T(1,128)S(1)}, f32[1,1024]{1,0:T(1,128)}, u32[]{:S(2)}) copy-start(f32[1,1024]{1,0:T(1,128)} %param.10) | copy-start | bytes 12292
  21.3 49.7 %copy-start.4 = (s32[2048]{0:T(1024)S(1)}, s32[2048]{0:T(1024)}, u32[]{:S(2)}) copy-start(s32[2048]{0:T(1024)} %param.8) | copy-start | bytes 24580
  21.3 50.8 %collective-permute-start.1 = (bf16[1024,1408]{1,0:T(8,128)(2,1)}, bf16[1024,1408]{1,0:T(8,128)(2,1)}, u32[]{:S(2)}, u32[]{:S(2)}) collective-permute-start(bf16[1024,1408]{1,0:T(8,128)(2,1)} %maximum_maximum_fusion), channel_id=1, source_target_pairs={{0,8},{8,0},{1,9},{9,1},{2,10},{10,2},{3,11},{11,3},{4,12},{12,4},... | collective-permute-start | bytes 8650760 | tf_op jit(solution)/shard_map/ppermute | solution.py:125
  21.3 50.8 %collective-permute-start.2 = (bf16[1024,1024]{1,0:T(8,128)(2,1)}, bf16[1024,1024]{1,0:T(8,128)(2,1)}, u32[]{:S(2)}, u32[]{:S(2)}) collective-permute-start(bf16[1024,1024]{1,0:T(8,128)(2,1)} %bitcast.6), channel_id=1, source_target_pairs={{0,8},{8,0},{1,9},{9,1},{2,10},{10,2},{3,11},{11,3},{4,12},{12,4},... | collective-permute-start | bytes 6291464 | tf_op jit(solution)/shard_map/ppermute | solution.py:125
  44.5 27.6 %collective-permute-start.3 = (bf16[1024,1024]{1,0:T(8,128)(2,1)S(1)}, bf16[1024,1024]{1,0:T(8,128)(2,1)}, u32[]{:S(2)}, u32[]{:S(2)}) collective-permute-start(bf16[1024,1024]{1,0:T(8,128)(2,1)S(1)} %bitcast.107), channel_id=1, source_target_pairs={{0,8},{8,0},{1,9},{9,1},{2,10},{10,2},{3,11},{11,3},{4,12},{12,4},... | collective-permute-start | bytes 6291464 | tf_op jit(solution)/shard_map/ppermute | solution.py:132
  44.5 27.6 %collective-permute-start = (f32[1024]{0:T(1024)S(1)}, f32[1024]{0:T(1024)S(1)}, u32[]{:S(2)}, u32[]{:S(2)}) collective-permute-start(f32[1024]{0:T(1024)S(1)} %bitcast.127), channel_id=1, source_target_pairs={{0,8},{8,0},{1,9},{9,1},{2,10},{10,2},{3,11},{11,3},{4,12},{12,4},... | collective-permute-start | bytes 12296 | tf_op jit(solution)/shard_map/ppermute | solution.py:125
  83.8 6.3 %copy-start = (bf16[1024,1024]{1,0:T(8,128)(2,1)}, bf16[1024,1024]{1,0:T(8,128)(2,1)S(1)}, u32[]{:S(2)}) copy-start(bf16[1024,1024]{1,0:T(8,128)(2,1)S(1)} %gather_fusion.1) | copy-start | bytes 6291460
  156.4 239.0 %all-reduce.5.cloned.1.call-start = ((), (), s32[]{:S(2)}) async-start(), calls=%async_computation.6 | async-start | bytes 4194304 | tf_op jit(solution)/shard_map/psum | solution.py:106
  238.4 3.6 copy-start.1
Sparse Core Ops, SparseCore 0:
  156.5 81.8 all-reduce.2
  317.6 77.7 all-reduce.4

commit v7 on v5

--- a/solution.py
+++ b/solution.py
@@ -132,17 +132,18 @@
     other, received, own_allowed = lax.optimization_barrier(
         (other, received, block_mask(own_segments))
     )
-    pool = jnp.concatenate([got, received], axis=0)
     my_order = lax.dynamic_slice_in_dim(order, section_index * rows_here, rows_here)
     source_group = my_order // entry_rows
     within = my_order % entry_rows
     from_other = (within // part_rows) != section_index
-    pool_index = (
-        jnp.where(from_other, group_count * part_rows, 0)
-        + source_group * part_rows
-        + within % part_rows
-    )
-    hidden = jnp.take(pool, pool_index, axis=0)
+    block_index = source_group * part_rows + within % part_rows
+    hits = lax.broadcasted_iota(jnp.int32, (rows_here, got.shape[0]), 1) == block_index[:, None]
+    picked_here = (hits & ~from_other[:, None]).astype(got.dtype)
+    picked_there = (hits & from_other[:, None]).astype(got.dtype)
+    hidden = (
+        jnp.dot(picked_here, got, preferred_element_type=jnp.float32)
+        + jnp.dot(picked_there, received, preferred_element_type=jnp.float32)
+    ).astype(got.dtype)
     for layer_index in range(section_count):
         params = jax.tree.map(
             lambda mine, theirs: jnp.where(section_index == layer_index, mine, theirs), own, other

time: 399 us -> 398 us (level)
  matrix products: 23.8 us -> 31.7 us
  other arithmetic: 16.8 us -> 11.4 us
    dot_general x0 -> x2, matrix products: none -> 9.41 us  [the longest x1 5.09 us: on_device(): jnp.dot(picked_there, received, preferred_element_type=jnp.float32)]
    gather x1 -> x0, local copies, waits for them, and re-layouts: 7.7 us -> none  [on_device(): hidden = jnp.take(pool, pool_index, axis=0)]
  transfers between devices with their start and end apart: 7 -> 7, of which waited for: 4 -> 3; matrix products, arithmetic and copies ran while one was open for 1% -> 2% of each run, Pallas kernels for 0% -> 0%
where the time goes in v7:
time: 398 us
  waiting for transfers between devices  184 us (46%)
  blocking collectives  139 us (35%)
  matrix products  31.7 us (8%)
  between operations  13.8 us (3%)
  other arithmetic  11.4 us (3%)
  local copies, waits for them, and re-layouts  8.84 us (2%)
  starting transfers between devices  8.79 us (2%)
    psum x2, waiting for transfers between devices, section_layer(): lax.psum(head_terms.astype(jnp.bfloat16), 'tensor').astype(jnp.float32)  160 us
    all_to_all x2, blocking collectives, section_layer(): lax.all_to_all(payload.reshape(group_count, own_rows, payload.shape[1]),...  81.5 us
    all_to_all x2, blocking collectives, gathered_over(): lax.all_to_all(spread, axis, 0, 0, tiled=False)  57.5 us
    all_to_all x1, waiting for transfers between devices, on_device(): lax.all_to_all(my_rows.reshape(part_rows, group_count, model_width // gro...  24.3 us
    dot_general x2, matrix products, section_layer(): jnp.dot(gathered_over(attended_rows, 'dp'), out_weight, preferred_element...  11.4 us
    dot_general x2, matrix products, section_layer(): jnp.dot(normed_rows, joined_weight, preferred_element_type=jnp.float32)  9.69 us
  transfers between devices with their start and end apart: 7, of which 3 were waited for; matrix products, arithmetic and copies ran while one was open for 2% of the time, Pallas kernels for 0%

profile of v7, /device:TPU:2, one launch (start us, length us, event | category | flops | bytes accessed | tf_op | source)
XLA Modules:
  0.0 397.9 jit_solution(13542701200499469069)
XLA Ops:
  6.5 1.7 constant_dynamic-slice_fusion
  8.3 1.5 copy.68
  9.8 7.6 %all-to-all-start = ((bf16[64,16,1024]{2,0,1:T(8,128)(2,1)}), bf16[64,16,1024]{2,0,1:T(8,128)(2,1)}, u32[]{:S(2)}, u32[]{:S(2)}) async-start(bf16[64,16,1024]{2,0,1:T(8,128)(2,1)} %bitcast.102), calls=%async_computation | async-start | bytes 4194304 | tf_op jit(solution)/shard_map/all_to_all | solution.py:121
  17.5 2.2 maximum_maximum_fusion
  19.8 0.5 collective-permute-start.2
  20.3 24.3 %all-to-all-done = bf16[64,16,1024]{2,0,1:T(8,128)(2,1)} async-done(((bf16[64,16,1024]{2,0,1:T(8,128)(2,1)}), bf16[64,16,1024]{2,0,1:T(8,128)(2,1)}, u32[]{:S(2)}, u32[]{:S(2)}) %all-to-all-start) | async-done | bytes 2097184 | tf_op jit(solution)/shard_map/all_to_all | solution.py:121
  44.6 0.5 collective-permute-start
  45.1 0.8 dynamic_slice.11
  46.1 4.3 %fusion.8 = f32[1024,1024]{0,1:T(8,128)S(1)} fusion(bf16[1024,1024]{1,0:T(8,128)(2,1)} %bitcast.2, s32[1024]{0:T(1024)S(1)} %fusion.61, pred[1024]{0:T(1024)(128)(4,1)S(1)} %get-tuple-element.15), kind=kOutput, calls=%fused_computation.20 | convolution fusion | flops 2149580800 | bytes 6296576 | tf_op jit(solution)/shard_map/dot_general | solution.py:144
  50.5 5.1 %fusion = (f32[1024]{0:T(1024)S(1)}, bf16[1024,1024]{0,1:T(8,128)(2,1)S(1)}) fusion(f32[1024,1024]{0,1:T(8,128)S(1)} %fusion.8, bf16[1024,1024]{1,0:T(8,128)(2,1)} %collective-permute-done.3, s32[1024]{0:T(1024)S(1)} %fusion.61, pred[1024]{0:T(1024)(128)(4,1)S(1)} %get-tuple-element.16), kind=kOutput, calls=%fused_computation.10 | convolution fusion | flops 2154822656 | bytes 8397824 | tf_op jit(solution)/shard_map/dot_general | solution.py:145
  55.6 3.9 select_convert_fusion.1
  59.5 44.6 %all_to_all.35 = bf16[16,64,1408]{2,1,0:T(8,128)(2,1)S(1)} all-to-all(bf16[16,64,1408]{2,1,0:T(8,128)(2,1)S(1)} %bitcast.107), channel_id=1, replica_groups=mesh['dp'=16,'section'=2,'tensor'=8] {'dp'}, dimensions={0} | all-to-all | bytes 5767168 | tf_op jit(solution)/shard_map/all_to_all | solution.py:79
  104.1 0.4 convert_reduce_fusion.1
  104.5 0.2 fusion.59
  104.9 0.3 fusion.73
  105.2 0.2 fusion.44
  105.5 0.3 broadcast_in_dim.78
  105.8 32.0 %all_to_all.36 = bf16[16,64,1024]{2,1,0:T(8,128)(2,1)S(1)} all-to-all(bf16[16,64,1024]{2,1,0:T(8,128)(2,1)S(1)} %broadcast_in_dim.78), channel_id=1, replica_groups=mesh['dp'=16,'section'=2,'tensor'=8] {'dp'}, dimensions={0} | all-to-all | bytes 4194304 | tf_op jit(solution)/shard_map/all_to_all | solution.py:55
  137.8 5.4 %fusion.30 = bf16[1024,1024]{0,1:T(8,128)(2,1)} fusion(bf16[1024,1024]{1,0:T(8,128)(2,1)S(1)} %bitcast.112, bf16[1024,1024]{1,0:T(8,128)(2,1)} %collective-permute-done.2, pred[]{:T(512)S(6)} %eq.58, bf16[1,1024,1024]{2,1,0:T(8,128)(2,1)} %param.13), kind=kOutput, calls=%fused_computation.40 | convolution fusion | flops 2149580800 | bytes 8388609 | tf_op jit(solution)/shard_map/dot_general | solution.py:95
  143.3 82.0 %all-reduce.3.cloned.1.call-done = bf16[1024,1024]{0,1:T(8,128)(2,1)} async-done(((bf16[1024,1024]{0,1:T(8,128)(2,1)}), bf16[1024,1024]{0,1:T(8,128)(2,1)}) %all-reduce.3.cloned.1.call-update) | async-done | bytes 2097168 | tf_op jit(solution)/shard_map/psum | solution.py:98
  225.3 2.7 fusion.3
  228.2 5.8 %select_convert_fusion = bf16[1024,1408]{1,0:T(8,128)(2,1)S(1)} fusion(bf16[1024,1408]{1,0:T(8,128)(2,1)} %collective-permute-done.1, bf16[1024]{0:T(1024)(128)(2,1)S(1)} %get-tuple-element.20, bf16[1024]{0:T(1024)(128)(2,1)S(1)} %get-tuple-element.19, pred[]{:T(512)S(6)} %eq.59, pred[1408]{0:T(1024)(128)(4,1)S(1)} %get-tuple-element.29, ...), kind=kOutput, calls=%fused_computation.7 | convolution fusion | flops 2973106176 | bytes 12596737 | tf_op jit(solution)/shard_map/dot_general | solution.py:66
  234.0 37.0 %all_to_all.37 = bf16[16,64,1408]{2,1,0:T(8,128)(2,1)S(1)} all-to-all(bf16[16,64,1408]{2,1,0:T(8,128)(2,1)S(1)} %bitcast.106), channel_id=1, replica_groups=mesh['dp'=16,'section'=2,'tensor'=8] {'dp'}, dimensions={0} | all-to-all | bytes 5767168 | tf_op jit(solution)/shard_map/all_to_all | solution.py:79
  270.9 0.4 convert_reduce_fusion
  271.7 0.3 fusion.74
  272.0 0.2 fusion.45
  272.4 0.3 broadcast_in_dim.82
  272.6 25.5 %all_to_all.38 = bf16[16,64,1024]{2,1,0:T(8,128)(2,1)S(1)} all-to-all(bf16[16,64,1024]{2,1,0:T(8,128)(2,1)S(1)} %broadcast_in_dim.82), channel_id=1, replica_groups=mesh['dp'=16,'section'=2,'tensor'=8] {'dp'}, dimensions={0} | all-to-all | bytes 4194304 | tf_op jit(solution)/shard_map/all_to_all | solution.py:55
  298.1 6.0 %fusion.33 = bf16[1024,1024]{0,1:T(8,128)(2,1)} fusion(bf16[1024,1024]{1,0:T(8,128)(2,1)S(1)} %bitcast.111, bf16[1024,1024]{1,0:T(8,128)(2,1)} %collective-permute-done.2, pred[]{:T(512)S(6)} %eq.59, bf16[1,1024,1024]{2,1,0:T(8,128)(2,1)} %param.13), kind=kOutput, calls=%fused_computation.41 | convolution fusion | flops 2149580800 | bytes 8388609 | tf_op jit(solution)/shard_map/dot_general | solution.py:95
  304.2 78.0 %all-reduce.5.cloned.1.call-done = bf16[1024,1024]{0,1:T(8,128)(2,1)} async-done(((bf16[1024,1024]{0,1:T(8,128)(2,1)}), bf16[1024,1024]{0,1:T(8,128)(2,1)}) %all-reduce.5.cloned.1.call-update) | async-done | bytes 2097168 | tf_op jit(solution)/shard_map/psum | solution.py:98
  382.2 5.0 %fusion.5 = bf16[1024,1024]{0,1:T(8,128)(2,1)} fusion(bf16[1024,1024]{0,1:T(8,128)(2,1)} %all-reduce.5.cloned.1.call-done, bf16[1024,1024]{0,1:T(8,128)(2,1)} %all-reduce.3.cloned.1.call-done, bf16[1024,1024]{0,1:T(8,128)(2,1)S(1)} %get-tuple-element.24), kind=kLoop, calls=%fused_computation.15 | loop fusion | flops 8388608 | bytes 8388608 | tf_op jit(solution)/shard_map/convert_element_type | solution.py:99
  387.2 3.9 copy.43
  (46 shorter events, 1.2 us)
Async XLA Ops:
  9.8 7.7 %copy-start.3 = (bf16[1,1024,1,256]{3,1,2,0:T(8,128)(2,1)S(1)}, bf16[1,1024,1,256]{3,1,2,0:T(8,128)(2,1)}, u32[]{:S(2)}) copy-start(bf16[1,1024,1,256]{3,1,2,0:T(8,128)(2,1)} %param.12) | copy-start | bytes 1572868
  9.8 34.8 %all-to-all-start = ((bf16[64,16,1024]{2,0,1:T(8,128)(2,1)}), bf16[64,16,1024]{2,0,1:T(8,128)(2,1)}, u32[]{:S(2)}, u32[]{:S(2)}) async-start(bf16[64,16,1024]{2,0,1:T(8,128)(2,1)} %bitcast.102), calls=%async_computation | async-start | bytes 4194304 | tf_op jit(solution)/shard_map/all_to_all | solution.py:121
  17.4 27.2 %copy-start.5 = (f32[1,1024]{1,0:T(1,128)S(1)}, f32[1,1024]{1,0:T(1,128)}, u32[]{:S(2)}) copy-start(f32[1,1024]{1,0:T(1,128)} %param.10) | copy-start | bytes 12292
  17.4 28.6 %copy-start.4 = (s32[2048]{0:T(1024)S(1)}, s32[2048]{0:T(1024)}, u32[]{:S(2)}) copy-start(s32[2048]{0:T(1024)} %param.8) | copy-start | bytes 24580
  17.4 207.9 %all-reduce.3.cloned.1.call-start = ((), (), s32[]{:S(2)}) async-start(), calls=%async_computation.5 | async-start | bytes 4194304 | tf_op jit(solution)/shard_map/psum | solution.py:98
  19.7 30.8 %collective-permute-start.1 = (bf16[1024,1408]{1,0:T(8,128)(2,1)S(1)}, bf16[1024,1408]{1,0:T(8,128)(2,1)}, u32[]{:S(2)}, u32[]{:S(2)}) collective-permute-start(bf16[1024,1408]{1,0:T(8,128)(2,1)S(1)} %maximum_maximum_fusion), channel_id=1, source_target_pairs={{0,8},{8,0},{1,9},{9,1},{2,10},{10,2},{3,11},{11,3},{4,12},{12,4},... | collective-permute-start | bytes 8650760 | tf_op jit(solution)/shard_map/ppermute | solution.py:117
  19.8 30.7 %collective-permute-start.2 = (bf16[1024,1024]{1,0:T(8,128)(2,1)}, bf16[1024,1024]{1,0:T(8,128)(2,1)}, u32[]{:S(2)}, u32[]{:S(2)}) collective-permute-start(bf16[1024,1024]{1,0:T(8,128)(2,1)} %bitcast.6), channel_id=1, source_target_pairs={{0,8},{8,0},{1,9},{9,1},{2,10},{10,2},{3,11},{11,3},{4,12},{12,4},... | collective-permute-start | bytes 6291464 | tf_op jit(solution)/shard_map/ppermute | solution.py:117
  44.6 5.9 %collective-permute-start.3 = (bf16[1024,1024]{1,0:T(8,128)(2,1)}, bf16[1024,1024]{1,0:T(8,128)(2,1)}, u32[]{:S(2)}, u32[]{:S(2)}) collective-permute-start(bf16[1024,1024]{1,0:T(8,128)(2,1)} %bitcast.2), channel_id=1, source_target_pairs={{0,8},{8,0},{1,9},{9,1},{2,10},{10,2},{3,11},{11,3},{4,12},{12,4},... | collective-permute-start | bytes 6291464 | tf_op jit(solution)/shard_map/ppermute | solution.py:124
  44.6 5.8 %collective-permute-start = (f32[1024]{0:T(1024)S(1)}, f32[1024]{0:T(1024)S(1)}, u32[]{:S(2)}, u32[]{:S(2)}) collective-permute-start(f32[1024]{0:T(1024)S(1)} %bitcast.126), channel_id=1, source_target_pairs={{0,8},{8,0},{1,9},{9,1},{2,10},{10,2},{3,11},{11,3},{4,12},{12,4},... | collective-permute-start | bytes 12296 | tf_op jit(solution)/shard_map/ppermute | solution.py:117
  50.5 5.1 %copy-start.1 = (bf16[1,1024,1024]{2,1,0:T(8,128)(2,1)S(1)}, bf16[1,1024,1024]{2,1,0:T(8,128)(2,1)}, u32[]{:S(2)}) copy-start(bf16[1,1024,1024]{2,1,0:T(8,128)(2,1)} %param.11) | copy-start | bytes 6291460
  143.2 238.9 %all-reduce.5.cloned.1.call-start = ((), (), s32[]{:S(2)}) async-start(), calls=%async_computation.6 | async-start | bytes 4194304 | tf_op jit(solution)/shard_map/psum | solution.py:98
  225.3 2.8 copy-start
  225.3 2.9 copy-start.2
Sparse Core Ops, SparseCore 0:
  143.3 81.9 all-reduce.2
  304.3 77.8 all-reduce.4

commit v8 on v7

--- a/solution.py
+++ b/solution.py
@@ -3,6 +3,7 @@
 import jax
 import jax.numpy as jnp
 from jax import lax
+from jax.experimental.layout import Layout, with_layout_constraint
 from jax.sharding import PartitionSpec as P
 
 MODEL_WIDTH = 16384
@@ -144,6 +145,7 @@
         jnp.dot(picked_here, got, preferred_element_type=jnp.float32)
         + jnp.dot(picked_there, received, preferred_element_type=jnp.float32)
     ).astype(got.dtype)
+    hidden = with_layout_constraint(hidden, Layout(major_to_minor=(0, 1)))
     for layer_index in range(section_count):
         params = jax.tree.map(
             lambda mine, theirs: jnp.where(section_index == layer_index, mine, theirs), own, other

time: 398 us -> 393 us (0.987)
  no operation moved by 1% of the time
where the time goes in v8:
time: 393 us
  waiting for transfers between devices  185 us (47%)
  blocking collectives  139 us (35%)
  matrix products  30.1 us (8%)
  between operations  13.7 us (3%)
  other arithmetic  11.2 us (3%)
  starting transfers between devices  8.84 us (2%)
  local copies, waits for them, and re-layouts  5.23 us (1%)
    psum x2, waiting for transfers between devices, section_layer(): lax.psum(head_terms.astype(jnp.bfloat16), 'tensor').astype(jnp.float32)  160 us
    all_to_all x2, blocking collectives, section_layer(): lax.all_to_all(payload.reshape(group_count, own_rows, payload.shape[1]),...  81.4 us
    all_to_all x2, blocking collectives, gathered_over(): lax.all_to_all(spread, axis, 0, 0, tiled=False)  57.7 us
    all_to_all x1, waiting for transfers between devices, on_device(): lax.all_to_all(my_rows.reshape(part_rows, group_count, model_width // gro...  24.4 us
    dot_general x2, matrix products, section_layer(): jnp.dot(gathered_over(attended_rows, 'dp'), out_weight, preferred_element...  11.2 us
    dot_general x2, matrix products, section_layer(): jnp.dot(normed_rows, joined_weight, preferred_element_type=jnp.float32)  8.97 us
  transfers between devices with their start and end apart: 7, of which 3 were waited for; matrix products, arithmetic and copies ran while one was open for 2% of the time, Pallas kernels for 0%

profile of v8, /device:TPU:2, one launch (start us, length us, event | category | flops | bytes accessed | tf_op | source)
XLA Modules:
  0.0 392.8 jit_solution(6139880613853147727)
XLA Ops:
  6.5 1.7 constant_dynamic-slice_fusion
  8.3 1.6 copy.54
  9.8 7.7 %all-to-all-start = ((bf16[64,16,1024]{2,0,1:T(8,128)(2,1)}), bf16[64,16,1024]{2,0,1:T(8,128)(2,1)}, u32[]{:S(2)}, u32[]{:S(2)}) async-start(bf16[64,16,1024]{2,0,1:T(8,128)(2,1)} %bitcast.102), calls=%async_computation | async-start | bytes 4194304 | tf_op jit(solution)/shard_map/all_to_all | solution.py:122
  17.7 2.2 maximum_maximum_fusion
  19.9 0.5 collective-permute-start.2
  20.4 24.4 %all-to-all-done = bf16[64,16,1024]{2,0,1:T(8,128)(2,1)} async-done(((bf16[64,16,1024]{2,0,1:T(8,128)(2,1)}), bf16[64,16,1024]{2,0,1:T(8,128)(2,1)}, u32[]{:S(2)}, u32[]{:S(2)}) %all-to-all-start) | async-done | bytes 2097184 | tf_op jit(solution)/shard_map/all_to_all | solution.py:122
  44.8 0.5 collective-permute-start
  45.3 0.8 dynamic_slice.11
  46.3 4.0 %fusion.8 = f32[1024,1024]{1,0:T(8,128)S(1)} fusion(bf16[1024,1024]{1,0:T(8,128)(2,1)} %bitcast.2, s32[1024]{0:T(1024)S(1)} %fusion.61, pred[1024]{0:T(1024)(128)(4,1)S(1)} %get-tuple-element.15), kind=kOutput, calls=%fused_computation.20 | convolution fusion | flops 2149580800 | bytes 6296576 | tf_op jit(solution)/shard_map/dot_general | solution.py:145
  50.4 4.9 %fusion = (f32[1024]{0:T(1024)S(1)}, bf16[1024,1024]{1,0:T(8,128)(2,1)S(1)}) fusion(f32[1024,1024]{1,0:T(8,128)S(1)} %fusion.8, bf16[1024,1024]{1,0:T(8,128)(2,1)} %collective-permute-done.3, s32[1024]{0:T(1024)S(1)} %fusion.61, pred[1024]{0:T(1024)(128)(4,1)S(1)} %get-tuple-element.16), kind=kOutput, calls=%fused_computation.10 | convolution fusion | flops 2154822656 | bytes 8397824 | tf_op jit(solution)/shard_map/dot_general | solution.py:146
  55.3 3.6 select_convert_fusion.1
  58.9 44.4 %all_to_all.35 = bf16[16,64,1408]{2,1,0:T(8,128)(2,1)S(1)} all-to-all(bf16[16,64,1408]{2,1,0:T(8,128)(2,1)S(1)} %bitcast.107), channel_id=1, replica_groups=mesh['dp'=16,'section'=2,'tensor'=8] {'dp'}, dimensions={0} | all-to-all | bytes 5767168 | tf_op jit(solution)/shard_map/all_to_all | solution.py:80
  103.3 0.4 convert_reduce_fusion.1
  103.6 0.2 fusion.59
  104.0 0.3 fusion.73
  104.3 0.2 fusion.44
  104.7 0.3 broadcast_in_dim.78
  104.9 32.2 %all_to_all.36 = bf16[16,64,1024]{2,1,0:T(8,128)(2,1)S(1)} all-to-all(bf16[16,64,1024]{2,1,0:T(8,128)(2,1)S(1)} %broadcast_in_dim.78), channel_id=1, replica_groups=mesh['dp'=16,'section'=2,'tensor'=8] {'dp'}, dimensions={0} | all-to-all | bytes 4194304 | tf_op jit(solution)/shard_map/all_to_all | solution.py:56
  137.1 5.3 %fusion.30 = bf16[1024,1024]{1,0:T(8,128)(2,1)} fusion(bf16[1024,1024]{1,0:T(8,128)(2,1)S(1)} %bitcast.112, bf16[1024,1024]{1,0:T(8,128)(2,1)} %collective-permute-done.2, pred[]{:T(512)S(6)} %eq.58, bf16[1,1024,1024]{2,1,0:T(8,128)(2,1)} %param.13), kind=kOutput, calls=%fused_computation.40 | convolution fusion | flops 2149580800 | bytes 8388609 | tf_op jit(solution)/shard_map/dot_general | solution.py:96
  142.4 82.2 %all-reduce.3.cloned.1.call-done = bf16[1024,1024]{1,0:T(8,128)(2,1)} async-done(((bf16[1024,1024]{1,0:T(8,128)(2,1)}), bf16[1024,1024]{1,0:T(8,128)(2,1)}) %all-reduce.3.cloned.1.call-update) | async-done | bytes 2097168 | tf_op jit(solution)/shard_map/psum | solution.py:99
  224.6 2.5 fusion.3
  227.1 0.3 copy-done.3
  227.5 5.4 %select_convert_fusion = bf16[1024,1408]{1,0:T(8,128)(2,1)S(1)} fusion(bf16[1024,1408]{1,0:T(8,128)(2,1)} %collective-permute-done.1, bf16[1024]{0:T(1024)(128)(2,1)S(1)} %get-tuple-element.20, bf16[1024]{0:T(1024)(128)(2,1)S(1)} %get-tuple-element.19, pred[]{:T(512)S(6)} %eq.59, pred[1408]{0:T(1024)(128)(4,1)S(1)} %get-tuple-element.29, ...), kind=kOutput, calls=%fused_computation.7 | convolution fusion | flops 2973106176 | bytes 12596737 | tf_op jit(solution)/shard_map/dot_general | solution.py:67
  232.9 37.0 %all_to_all.37 = bf16[16,64,1408]{2,1,0:T(8,128)(2,1)S(1)} all-to-all(bf16[16,64,1408]{2,1,0:T(8,128)(2,1)S(1)} %bitcast.106), channel_id=1, replica_groups=mesh['dp'=16,'section'=2,'tensor'=8] {'dp'}, dimensions={0} | all-to-all | bytes 5767168 | tf_op jit(solution)/shard_map/all_to_all | solution.py:80
  269.8 0.4 convert_reduce_fusion
  270.6 0.3 fusion.74
  270.9 0.2 fusion.45
  271.2 0.3 broadcast_in_dim.82
  271.5 25.5 %all_to_all.38 = bf16[16,64,1024]{2,1,0:T(8,128)(2,1)S(1)} all-to-all(bf16[16,64,1024]{2,1,0:T(8,128)(2,1)S(1)} %broadcast_in_dim.82), channel_id=1, replica_groups=mesh['dp'=16,'section'=2,'tensor'=8] {'dp'}, dimensions={0} | all-to-all | bytes 4194304 | tf_op jit(solution)/shard_map/all_to_all | solution.py:56
  297.0 5.9 %fusion.33 = bf16[1024,1024]{1,0:T(8,128)(2,1)} fusion(bf16[1024,1024]{1,0:T(8,128)(2,1)S(1)} %bitcast.111, bf16[1024,1024]{1,0:T(8,128)(2,1)} %collective-permute-done.2, pred[]{:T(512)S(6)} %eq.59, bf16[1,1024,1024]{2,1,0:T(8,128)(2,1)} %param.13), kind=kOutput, calls=%fused_computation.41 | convolution fusion | flops 2149580800 | bytes 8388609 | tf_op jit(solution)/shard_map/dot_general | solution.py:96
  302.9 78.0 %all-reduce.5.cloned.1.call-done = bf16[1024,1024]{1,0:T(8,128)(2,1)} async-done(((bf16[1024,1024]{1,0:T(8,128)(2,1)}), bf16[1024,1024]{1,0:T(8,128)(2,1)}) %all-reduce.5.cloned.1.call-update) | async-done | bytes 2097168 | tf_op jit(solution)/shard_map/psum | solution.py:99
  380.9 5.0 %fusion.5 = bf16[1024,1024]{1,0:T(8,128)(2,1)} fusion(bf16[1024,1024]{1,0:T(8,128)(2,1)} %all-reduce.5.cloned.1.call-done, bf16[1024,1024]{1,0:T(8,128)(2,1)} %all-reduce.3.cloned.1.call-done, bf16[1024,1024]{1,0:T(8,128)(2,1)S(1)} %get-tuple-element.24), kind=kLoop, calls=%fused_computation.15 | loop fusion | flops 8388608 | bytes 8388608 | tf_op jit(solution)/shard_map/convert_element_type | solution.py:100
  (47 shorter events, 1.0 us)
Async XLA Ops:
  9.8 7.8 %copy-start.1 = (bf16[1,1024,1024]{2,1,0:T(8,128)(2,1)S(1)}, bf16[1,1024,1024]{2,1,0:T(8,128)(2,1)}, u32[]{:S(2)}) copy-start(bf16[1,1024,1024]{2,1,0:T(8,128)(2,1)} %param.11) | copy-start | bytes 6291460
  9.8 7.8 %copy-start.4 = (bf16[1,1024,1,256]{3,1,2,0:T(8,128)(2,1)S(1)}, bf16[1,1024,1,256]{3,1,2,0:T(8,128)(2,1)}, u32[]{:S(2)}) copy-start(bf16[1,1024,1,256]{3,1,2,0:T(8,128)(2,1)} %param.12) | copy-start | bytes 1572868
  9.8 35.0 %all-to-all-start = ((bf16[64,16,1024]{2,0,1:T(8,128)(2,1)}), bf16[64,16,1024]{2,0,1:T(8,128)(2,1)}, u32[]{:S(2)}, u32[]{:S(2)}) async-start(bf16[64,16,1024]{2,0,1:T(8,128)(2,1)} %bitcast.102), calls=%async_computation | async-start | bytes 4194304 | tf_op jit(solution)/shard_map/all_to_all | solution.py:122
  17.6 27.2 %copy-start.6 = (f32[1,1024]{1,0:T(1,128)S(1)}, f32[1,1024]{1,0:T(1,128)}, u32[]{:S(2)}) copy-start(f32[1,1024]{1,0:T(1,128)} %param.10) | copy-start | bytes 12292
  17.6 28.6 %copy-start.5 = (s32[2048]{0:T(1024)S(1)}, s32[2048]{0:T(1024)}, u32[]{:S(2)}) copy-start(s32[2048]{0:T(1024)} %param.8) | copy-start | bytes 24580
  17.6 207.0 %all-reduce.3.cloned.1.call-start = ((), (), s32[]{:S(2)}) async-start(), calls=%async_computation.5 | async-start | bytes 4194304 | tf_op jit(solution)/shard_map/psum | solution.py:99
  19.9 30.4 %collective-permute-start.1 = (bf16[1024,1408]{1,0:T(8,128)(2,1)}, bf16[1024,1408]{1,0:T(8,128)(2,1)}, u32[]{:S(2)}, u32[]{:S(2)}) collective-permute-start(bf16[1024,1408]{1,0:T(8,128)(2,1)} %maximum_maximum_fusion), channel_id=1, source_target_pairs={{0,8},{8,0},{1,9},{9,1},{2,10},{10,2},{3,11},{11,3},{4,12},{12,4},... | collective-permute-start | bytes 8650760 | tf_op jit(solution)/shard_map/ppermute | solution.py:118
  19.9 30.4 %collective-permute-start.2 = (bf16[1024,1024]{1,0:T(8,128)(2,1)}, bf16[1024,1024]{1,0:T(8,128)(2,1)}, u32[]{:S(2)}, u32[]{:S(2)}) collective-permute-start(bf16[1024,1024]{1,0:T(8,128)(2,1)} %bitcast.6), channel_id=1, source_target_pairs={{0,8},{8,0},{1,9},{9,1},{2,10},{10,2},{3,11},{11,3},{4,12},{12,4},... | collective-permute-start | bytes 6291464 | tf_op jit(solution)/shard_map/ppermute | solution.py:118
  44.8 5.5 %collective-permute-start.3 = (bf16[1024,1024]{1,0:T(8,128)(2,1)}, bf16[1024,1024]{1,0:T(8,128)(2,1)}, u32[]{:S(2)}, u32[]{:S(2)}) collective-permute-start(bf16[1024,1024]{1,0:T(8,128)(2,1)} %bitcast.2), channel_id=1, source_target_pairs={{0,8},{8,0},{1,9},{9,1},{2,10},{10,2},{3,11},{11,3},{4,12},{12,4},... | collective-permute-start | bytes 6291464 | tf_op jit(solution)/shard_map/ppermute | solution.py:125
  44.8 5.5 %collective-permute-start = (f32[1024]{0:T(1024)S(1)}, f32[1024]{0:T(1024)S(1)}, u32[]{:S(2)}, u32[]{:S(2)}) collective-permute-start(f32[1024]{0:T(1024)S(1)} %bitcast.126), channel_id=1, source_target_pairs={{0,8},{8,0},{1,9},{9,1},{2,10},{10,2},{3,11},{11,3},{4,12},{12,4},... | collective-permute-start | bytes 12296 | tf_op jit(solution)/shard_map/ppermute | solution.py:118
  50.3 4.9 %copy-start.2 = (bf16[1,1024,1024]{2,1,0:T(8,128)(2,1)S(1)}, bf16[1,1024,1024]{2,1,0:T(8,128)(2,1)}, u32[]{:S(2)}) copy-start(bf16[1,1024,1024]{2,1,0:T(8,128)(2,1)} %param.11) | copy-start | bytes 6291460
  142.4 238.5 %all-reduce.5.cloned.1.call-start = ((), (), s32[]{:S(2)}) async-start(), calls=%async_computation.6 | async-start | bytes 4194304 | tf_op jit(solution)/shard_map/psum | solution.py:99
  224.6 2.5 copy-start
  224.6 2.9 copy-start.3
Sparse Core Ops, SparseCore 0:
  142.5 82.0 all-reduce.2
  303.1 77.8 all-reduce.4

commit v9 on v8

--- a/solution.py
+++ b/solution.py
@@ -150,7 +150,7 @@
         params = jax.tree.map(
             lambda mine, theirs: jnp.where(section_index == layer_index, mine, theirs), own, other
         )
-        hidden = section_layer(hidden, own_allowed, *params)
+        hidden = lax.optimization_barrier(section_layer(hidden, own_allowed, *params))
     return hidden
 
 

time: 393 us -> 394 us (level)
  no operation moved by 1% of the time
where the time goes in v9:
time: 394 us
  waiting for transfers between devices  184 us (47%)
  blocking collectives  140 us (36%)
  matrix products  30.7 us (8%)
  between operations  13.8 us (4%)
  other arithmetic  11.2 us (3%)
  starting transfers between devices  8.79 us (2%)
  local copies, waits for them, and re-layouts  4.82 us (1%)
    psum x2, waiting for transfers between devices, section_layer(): lax.psum(head_terms.astype(jnp.bfloat16), 'tensor').astype(jnp.float32)  160 us
    all_to_all x2, blocking collectives, section_layer(): lax.all_to_all(payload.reshape(group_count, own_rows, payload.shape[1]),...  81.5 us
    all_to_all x2, blocking collectives, gathered_over(): lax.all_to_all(spread, axis, 0, 0, tiled=False)  58.6 us
    all_to_all x1, waiting for transfers between devices, on_device(): lax.all_to_all(my_rows.reshape(part_rows, group_count, model_width // gro...  24.3 us
    dot_general x2, matrix products, section_layer(): jnp.dot(gathered_over(attended_rows, 'dp'), out_weight, preferred_element...  11.2 us
    dot_general x2, matrix products, section_layer(): jnp.dot(normed_rows, joined_weight, preferred_element_type=jnp.float32)  9.53 us
  transfers between devices with their start and end apart: 7, of which 3 were waited for; matrix products, arithmetic and copies ran while one was open for 2% of the time, Pallas kernels for 0%

profile of v9, /device:TPU:2, one launch (start us, length us, event | category | flops | bytes accessed | tf_op | source)
XLA Modules:
  0.0 393.9 jit_solution(1007037926768024324)
XLA Ops:
  6.5 1.7 constant_dynamic-slice_fusion
  8.3 1.5 copy.54
  9.8 7.6 %all-to-all-start = ((bf16[64,16,1024]{2,0,1:T(8,128)(2,1)}), bf16[64,16,1024]{2,0,1:T(8,128)(2,1)}, u32[]{:S(2)}, u32[]{:S(2)}) async-start(bf16[64,16,1024]{2,0,1:T(8,128)(2,1)} %bitcast.102), calls=%async_computation | async-start | bytes 4194304 | tf_op jit(solution)/shard_map/all_to_all | solution.py:122
  17.5 2.2 maximum_maximum_fusion
  19.8 0.5 collective-permute-start.2
  20.3 24.3 %all-to-all-done = bf16[64,16,1024]{2,0,1:T(8,128)(2,1)} async-done(((bf16[64,16,1024]{2,0,1:T(8,128)(2,1)}), bf16[64,16,1024]{2,0,1:T(8,128)(2,1)}, u32[]{:S(2)}, u32[]{:S(2)}) %all-to-all-start) | async-done | bytes 2097184 | tf_op jit(solution)/shard_map/all_to_all | solution.py:122
  44.6 0.5 collective-permute-start
  45.1 0.8 dynamic_slice.11
  46.1 4.0 %fusion.8 = f32[1024,1024]{1,0:T(8,128)S(1)} fusion(bf16[1024,1024]{1,0:T(8,128)(2,1)} %bitcast.2, s32[1024]{0:T(1024)S(1)} %fusion.61, pred[1024]{0:T(1024)(128)(4,1)S(1)} %get-tuple-element.15), kind=kOutput, calls=%fused_computation.20 | convolution fusion | flops 2149580800 | bytes 6296576 | tf_op jit(solution)/shard_map/dot_general | solution.py:145
  50.2 4.9 %fusion = (f32[1024]{0:T(1024)S(1)}, bf16[1024,1024]{1,0:T(8,128)(2,1)S(1)}) fusion(f32[1024,1024]{1,0:T(8,128)S(1)} %fusion.8, bf16[1024,1024]{1,0:T(8,128)(2,1)} %collective-permute-done.3, s32[1024]{0:T(1024)S(1)} %fusion.61, pred[1024]{0:T(1024)(128)(4,1)S(1)} %get-tuple-element.16), kind=kOutput, calls=%fused_computation.10 | convolution fusion | flops 2154822656 | bytes 8397824 | tf_op jit(solution)/shard_map/dot_general | solution.py:146
  55.1 3.5 select_convert_fusion.1
  58.6 43.6 %all_to_all.35 = bf16[16,64,1408]{2,1,0:T(8,128)(2,1)S(1)} all-to-all(bf16[16,64,1408]{2,1,0:T(8,128)(2,1)S(1)} %bitcast.107), channel_id=1, replica_groups=mesh['dp'=16,'section'=2,'tensor'=8] {'dp'}, dimensions={0} | all-to-all | bytes 5767168 | tf_op jit(solution)/shard_map/all_to_all | solution.py:80
  102.2 0.4 convert_reduce_fusion.1
  102.6 0.2 fusion.59
  103.0 0.3 fusion.72
  103.3 0.2 fusion.44
  103.7 0.3 broadcast_in_dim.78
  103.9 32.8 %all_to_all.36 = bf16[16,64,1024]{2,1,0:T(8,128)(2,1)S(1)} all-to-all(bf16[16,64,1024]{2,1,0:T(8,128)(2,1)S(1)} %broadcast_in_dim.78), channel_id=1, replica_groups=mesh['dp'=16,'section'=2,'tensor'=8] {'dp'}, dimensions={0} | all-to-all | bytes 4194304 | tf_op jit(solution)/shard_map/all_to_all | solution.py:56
  136.7 5.4 %fusion.30 = bf16[1024,1024]{1,0:T(8,128)(2,1)} fusion(bf16[1024,1024]{1,0:T(8,128)(2,1)S(1)} %bitcast.112, bf16[1024,1024]{1,0:T(8,128)(2,1)} %collective-permute-done.2, pred[]{:T(512)S(6)} %eq.58, bf16[1,1024,1024]{2,1,0:T(8,128)(2,1)} %param.13), kind=kOutput, calls=%fused_computation.40 | convolution fusion | flops 2149580800 | bytes 8388609 | tf_op jit(solution)/shard_map/dot_general | solution.py:96
  142.1 82.2 %all-reduce.3.cloned.1.call-done = bf16[1024,1024]{1,0:T(8,128)(2,1)} async-done(((bf16[1024,1024]{1,0:T(8,128)(2,1)}), bf16[1024,1024]{1,0:T(8,128)(2,1)}) %all-reduce.3.cloned.1.call-update) | async-done | bytes 2097168 | tf_op jit(solution)/shard_map/psum | solution.py:99
  224.3 3.2 fusion.2
  227.5 0.5 fusion.3
  228.0 6.0 %select_convert_fusion = bf16[1024,1408]{1,0:T(8,128)(2,1)S(1)} fusion(bf16[1024,1408]{1,0:T(8,128)(2,1)} %collective-permute-done.1, bf16[1024]{0:T(1024)(128)(2,1)S(1)} %get-tuple-element.20, bf16[1024]{0:T(1024)(128)(2,1)S(1)} %get-tuple-element.19, pred[]{:T(512)S(6)} %eq.59, pred[1408]{0:T(1024)(128)(4,1)S(1)} %get-tuple-element.29, ...), kind=kOutput, calls=%fused_computation.7 | convolution fusion | flops 2968911872 | bytes 10499585 | tf_op jit(solution)/shard_map/dot_general | solution.py:67
  234.0 37.9 %all_to_all.37 = bf16[16,64,1408]{2,1,0:T(8,128)(2,1)S(1)} all-to-all(bf16[16,64,1408]{2,1,0:T(8,128)(2,1)S(1)} %bitcast.106), channel_id=1, replica_groups=mesh['dp'=16,'section'=2,'tensor'=8] {'dp'}, dimensions={0} | all-to-all | bytes 5767168 | tf_op jit(solution)/shard_map/all_to_all | solution.py:80
  271.9 0.4 convert_reduce_fusion
  272.7 0.3 fusion.73
  273.0 0.2 fusion.45
  273.3 0.3 broadcast_in_dim.82
  273.6 25.8 %all_to_all.38 = bf16[16,64,1024]{2,1,0:T(8,128)(2,1)S(1)} all-to-all(bf16[16,64,1024]{2,1,0:T(8,128)(2,1)S(1)} %broadcast_in_dim.82), channel_id=1, replica_groups=mesh['dp'=16,'section'=2,'tensor'=8] {'dp'}, dimensions={0} | all-to-all | bytes 4194304 | tf_op jit(solution)/shard_map/all_to_all | solution.py:56
  299.4 5.9 %fusion.33 = bf16[1024,1024]{1,0:T(8,128)(2,1)} fusion(bf16[1024,1024]{1,0:T(8,128)(2,1)S(1)} %bitcast.111, bf16[1024,1024]{1,0:T(8,128)(2,1)} %collective-permute-done.2, pred[]{:T(512)S(6)} %eq.59, bf16[1,1024,1024]{2,1,0:T(8,128)(2,1)} %param.13), kind=kOutput, calls=%fused_computation.41 | convolution fusion | flops 2149580800 | bytes 8388609 | tf_op jit(solution)/shard_map/dot_general | solution.py:96
  305.3 77.8 %all-reduce.5.cloned.1.call-done = bf16[1024,1024]{1,0:T(8,128)(2,1)} async-done(((bf16[1024,1024]{1,0:T(8,128)(2,1)}), bf16[1024,1024]{1,0:T(8,128)(2,1)}) %all-reduce.5.cloned.1.call-update) | async-done | bytes 2097168 | tf_op jit(solution)/shard_map/psum | solution.py:99
  383.2 3.9 fusion.5
  (44 shorter events, 1.1 us)
Async XLA Ops:
  9.8 7.7 %copy-start.2 = (bf16[1,1024,1,256]{3,1,2,0:T(8,128)(2,1)S(1)}, bf16[1,1024,1,256]{3,1,2,0:T(8,128)(2,1)}, u32[]{:S(2)}) copy-start(bf16[1,1024,1,256]{3,1,2,0:T(8,128)(2,1)} %param.12) | copy-start | bytes 1572868
  9.8 34.8 %all-to-all-start = ((bf16[64,16,1024]{2,0,1:T(8,128)(2,1)}), bf16[64,16,1024]{2,0,1:T(8,128)(2,1)}, u32[]{:S(2)}, u32[]{:S(2)}) async-start(bf16[64,16,1024]{2,0,1:T(8,128)(2,1)} %bitcast.102), calls=%async_computation | async-start | bytes 4194304 | tf_op jit(solution)/shard_map/all_to_all | solution.py:122
  17.4 27.2 %copy-start.4 = (f32[1,1024]{1,0:T(1,128)S(1)}, f32[1,1024]{1,0:T(1,128)}, u32[]{:S(2)}) copy-start(f32[1,1024]{1,0:T(1,128)} %param.10) | copy-start | bytes 12292
  17.4 28.6 %copy-start.3 = (s32[2048]{0:T(1024)S(1)}, s32[2048]{0:T(1024)}, u32[]{:S(2)}) copy-start(s32[2048]{0:T(1024)} %param.8) | copy-start | bytes 24580
  17.4 206.9 %all-reduce.3.cloned.1.call-start = ((), (), s32[]{:S(2)}) async-start(), calls=%async_computation.5 | async-start | bytes 4194304 | tf_op jit(solution)/shard_map/psum | solution.py:99
  19.7 30.4 %collective-permute-start.1 = (bf16[1024,1408]{1,0:T(8,128)(2,1)S(1)}, bf16[1024,1408]{1,0:T(8,128)(2,1)}, u32[]{:S(2)}, u32[]{:S(2)}) collective-permute-start(bf16[1024,1408]{1,0:T(8,128)(2,1)S(1)} %maximum_maximum_fusion), channel_id=1, source_target_pairs={{0,8},{8,0},{1,9},{9,1},{2,10},{10,2},{3,11},{11,3},{4,12},{12,4},... | collective-permute-start | bytes 8650760 | tf_op jit(solution)/shard_map/ppermute | solution.py:118
  19.8 30.3 %collective-permute-start.2 = (bf16[1024,1024]{1,0:T(8,128)(2,1)}, bf16[1024,1024]{1,0:T(8,128)(2,1)}, u32[]{:S(2)}, u32[]{:S(2)}) collective-permute-start(bf16[1024,1024]{1,0:T(8,128)(2,1)} %bitcast.6), channel_id=1, source_target_pairs={{0,8},{8,0},{1,9},{9,1},{2,10},{10,2},{3,11},{11,3},{4,12},{12,4},... | collective-permute-start | bytes 6291464 | tf_op jit(solution)/shard_map/ppermute | solution.py:118
  44.6 5.5 %collective-permute-start.3 = (bf16[1024,1024]{1,0:T(8,128)(2,1)}, bf16[1024,1024]{1,0:T(8,128)(2,1)}, u32[]{:S(2)}, u32[]{:S(2)}) collective-permute-start(bf16[1024,1024]{1,0:T(8,128)(2,1)} %bitcast.2), channel_id=1, source_target_pairs={{0,8},{8,0},{1,9},{9,1},{2,10},{10,2},{3,11},{11,3},{4,12},{12,4},... | collective-permute-start | bytes 6291464 | tf_op jit(solution)/shard_map/ppermute | solution.py:125
  44.6 5.5 %collective-permute-start = (f32[1024]{0:T(1024)S(1)}, f32[1024]{0:T(1024)S(1)}, u32[]{:S(2)}, u32[]{:S(2)}) collective-permute-start(f32[1024]{0:T(1024)S(1)} %bitcast.126), channel_id=1, source_target_pairs={{0,8},{8,0},{1,9},{9,1},{2,10},{10,2},{3,11},{11,3},{4,12},{12,4},... | collective-permute-start | bytes 12296 | tf_op jit(solution)/shard_map/ppermute | solution.py:118
  50.1 4.9 %copy-start.1 = (bf16[1,1024,1024]{2,1,0:T(8,128)(2,1)S(1)}, bf16[1,1024,1024]{2,1,0:T(8,128)(2,1)}, u32[]{:S(2)}) copy-start(bf16[1,1024,1024]{2,1,0:T(8,128)(2,1)} %param.11) | copy-start | bytes 6291460
  55.0 3.6 copy-start
  142.1 241.1 %all-reduce.5.cloned.1.call-start = ((), (), s32[]{:S(2)}) async-start(), calls=%async_computation.6 | async-start | bytes 4194304 | tf_op jit(solution)/shard_map/psum | solution.py:99
Sparse Core Ops, SparseCore 0:
  142.2 82.0 all-reduce.2
  305.5 77.6 all-reduce.4

commit v10 on v8

--- a/solution.py
+++ b/solution.py
@@ -130,17 +130,21 @@
         section_index * rows_here + lax.axis_index("dp") * own_blocks * MICRO_TOKENS,
         own_blocks * MICRO_TOKENS,
     ).reshape(own_blocks, MICRO_TOKENS)
-    other, received, own_allowed = lax.optimization_barrier(
-        (other, received, block_mask(own_segments))
-    )
     my_order = lax.dynamic_slice_in_dim(order, section_index * rows_here, rows_here)
     source_group = my_order // entry_rows
     within = my_order % entry_rows
     from_other = (within // part_rows) != section_index
     block_index = source_group * part_rows + within % part_rows
     hits = lax.broadcasted_iota(jnp.int32, (rows_here, got.shape[0]), 1) == block_index[:, None]
-    picked_here = (hits & ~from_other[:, None]).astype(got.dtype)
-    picked_there = (hits & from_other[:, None]).astype(got.dtype)
+    other, received, own_allowed, picked_here, picked_there = lax.optimization_barrier(
+        (
+            other,
+            received,
+            block_mask(own_segments),
+            (hits & ~from_other[:, None]).astype(got.dtype),
+            (hits & from_other[:, None]).astype(got.dtype),
+        )
+    )
     hidden = (
         jnp.dot(picked_here, got, preferred_element_type=jnp.float32)
         + jnp.dot(picked_there, received, preferred_element_type=jnp.float32)

time: 393 us -> 395 us (level)
  transfers between devices with their start and end apart: 7 -> 7, of which waited for: 3 -> 4; matrix products, arithmetic and copies ran while one was open for 2% -> 1% of each run, Pallas kernels for 0% -> 0%
where the time goes in v10:
time: 395 us
  waiting for transfers between devices  185 us (47%)
  blocking collectives  139 us (35%)
  matrix products  29.5 us (7%)
  between operations  13.7 us (3%)
  other arithmetic  13.6 us (3%)
  starting transfers between devices  8.84 us (2%)
  local copies, waits for them, and re-layouts  5.24 us (1%)
    psum x2, waiting for transfers between devices, section_layer(): lax.psum(head_terms.astype(jnp.bfloat16), 'tensor').astype(jnp.float32)  160 us
    all_to_all x2, blocking collectives, section_layer(): lax.all_to_all(payload.reshape(group_count, own_rows, payload.shape[1]),...  81.2 us
    all_to_all x2, blocking collectives, gathered_over(): lax.all_to_all(spread, axis, 0, 0, tiled=False)  57.6 us
    all_to_all x1, waiting for transfers between devices, on_device(): lax.all_to_all(my_rows.reshape(part_rows, group_count, model_width // gro...  24.4 us
    dot_general x2, matrix products, section_layer(): jnp.dot(gathered_over(attended_rows, 'dp'), out_weight, preferred_element...  11.2 us
    dot_general x2, matrix products, section_layer(): jnp.dot(normed_rows, joined_weight, preferred_element_type=jnp.float32)  8.97 us
  transfers between devices with their start and end apart: 7, of which 4 were waited for; matrix products, arithmetic and copies ran while one was open for 1% of the time, Pallas kernels for 0%

profile of v10, /device:TPU:2, one launch (start us, length us, event | category | flops | bytes accessed | tf_op | source)
XLA Modules:
  0.0 394.9 jit_solution(2802923108917124698)
XLA Ops:
  6.5 1.7 constant_dynamic-slice_fusion
  8.3 1.6 copy.54
  9.8 7.7 %all-to-all-start = ((bf16[64,16,1024]{2,0,1:T(8,128)(2,1)}), bf16[64,16,1024]{2,0,1:T(8,128)(2,1)}, u32[]{:S(2)}, u32[]{:S(2)}) async-start(bf16[64,16,1024]{2,0,1:T(8,128)(2,1)} %bitcast.104), calls=%async_computation | async-start | bytes 4194304 | tf_op jit(solution)/shard_map/all_to_all | solution.py:122
  17.7 2.2 maximum_maximum_fusion
  19.9 0.5 collective-permute-start.2
  20.4 24.4 %all-to-all-done = bf16[64,16,1024]{2,0,1:T(8,128)(2,1)} async-done(((bf16[64,16,1024]{2,0,1:T(8,128)(2,1)}), bf16[64,16,1024]{2,0,1:T(8,128)(2,1)}, u32[]{:S(2)}, u32[]{:S(2)}) %all-to-all-start) | async-done | bytes 2097184 | tf_op jit(solution)/shard_map/all_to_all | solution.py:122
  44.8 0.5 collective-permute-start
  45.3 0.8 dynamic_slice.10
  46.3 2.4 fusion.9
  48.7 0.6 collective-permute-done
  49.3 4.1 %fusion.67 = f32[1024,1024]{1,0:T(8,128)S(1)} fusion(bf16[1024,1024]{1,0:T(8,128)(2,1)S(1)} %get-tuple-element.13, bf16[1024,1024]{1,0:T(8,128)(2,1)} %collective-permute-done.3), kind=kOutput, calls=%fused_computation.112 | convolution fusion | flops 2147483648 | bytes 8388608 | tf_op jit(solution)/shard_map/dot_general | solution.py:150
  53.4 4.2 %fusion = (f32[1024]{0:T(1024)S(1)}, bf16[1024,1024]{1,0:T(8,128)(2,1)S(1)}) fusion(f32[1024,1024]{1,0:T(8,128)S(1)} %fusion.67, bf16[1024,1024]{1,0:T(8,128)(2,1)S(1)} %copy-done.4, bf16[1024,1024]{1,0:T(8,128)(2,1)} %bitcast.6), kind=kOutput, calls=%fused_computation.10 | convolution fusion | flops 2152725504 | bytes 10489856 | tf_op jit(solution)/shard_map/dot_general | solution.py:149
  57.6 3.6 select_convert_fusion.1
  61.2 44.3 %all_to_all.35 = bf16[16,64,1408]{2,1,0:T(8,128)(2,1)S(1)} all-to-all(bf16[16,64,1408]{2,1,0:T(8,128)(2,1)S(1)} %bitcast.109), channel_id=1, replica_groups=mesh['dp'=16,'section'=2,'tensor'=8] {'dp'}, dimensions={0} | all-to-all | bytes 5767168 | tf_op jit(solution)/shard_map/all_to_all | solution.py:80
  105.5 0.4 convert_reduce_fusion.1
  106.2 0.3 fusion.65
  106.6 0.2 fusion.36
  106.9 0.3 broadcast_in_dim.78
  107.2 32.1 %all_to_all.36 = bf16[16,64,1024]{2,1,0:T(8,128)(2,1)S(1)} all-to-all(bf16[16,64,1024]{2,1,0:T(8,128)(2,1)S(1)} %broadcast_in_dim.78), channel_id=1, replica_groups=mesh['dp'=16,'section'=2,'tensor'=8] {'dp'}, dimensions={0} | all-to-all | bytes 4194304 | tf_op jit(solution)/shard_map/all_to_all | solution.py:56
  139.3 5.3 %fusion.24 = bf16[1024,1024]{1,0:T(8,128)(2,1)} fusion(bf16[1024,1024]{1,0:T(8,128)(2,1)S(1)} %bitcast.114, bf16[1024,1024]{1,0:T(8,128)(2,1)} %collective-permute-done.2, pred[]{:T(512)S(6)} %eq.58, bf16[1,1024,1024]{2,1,0:T(8,128)(2,1)} %param.13), kind=kOutput, calls=%fused_computation.36 | convolution fusion | flops 2149580800 | bytes 8388609 | tf_op jit(solution)/shard_map/dot_general | solution.py:96
  144.6 82.1 %all-reduce.3.cloned.1.call-done = bf16[1024,1024]{1,0:T(8,128)(2,1)} async-done(((bf16[1024,1024]{1,0:T(8,128)(2,1)}), bf16[1024,1024]{1,0:T(8,128)(2,1)}) %all-reduce.3.cloned.1.call-update) | async-done | bytes 2097168 | tf_op jit(solution)/shard_map/psum | solution.py:99
  226.8 2.5 fusion.3
  229.3 0.3 copy-done.3
  229.6 5.4 %select_convert_fusion = bf16[1024,1408]{1,0:T(8,128)(2,1)S(1)} fusion(bf16[1024,1408]{1,0:T(8,128)(2,1)} %collective-permute-done.1, bf16[1024]{0:T(1024)(128)(2,1)S(1)} %get-tuple-element.24, bf16[1024]{0:T(1024)(128)(2,1)S(1)} %get-tuple-element.23, pred[]{:T(512)S(6)} %eq.59, pred[1408]{0:T(1024)(128)(4,1)S(1)} %get-tuple-element.35, ...), kind=kOutput, calls=%fused_computation.7 | convolution fusion | flops 2973106176 | bytes 12596737 | tf_op jit(solution)/shard_map/dot_general | solution.py:67
  235.0 37.0 %all_to_all.37 = bf16[16,64,1408]{2,1,0:T(8,128)(2,1)S(1)} all-to-all(bf16[16,64,1408]{2,1,0:T(8,128)(2,1)S(1)} %bitcast.108), channel_id=1, replica_groups=mesh['dp'=16,'section'=2,'tensor'=8] {'dp'}, dimensions={0} | all-to-all | bytes 5767168 | tf_op jit(solution)/shard_map/all_to_all | solution.py:80
  272.0 0.4 convert_reduce_fusion
  272.7 0.3 fusion.66
  273.4 0.3 broadcast_in_dim.82
  273.7 25.5 %all_to_all.38 = bf16[16,64,1024]{2,1,0:T(8,128)(2,1)S(1)} all-to-all(bf16[16,64,1024]{2,1,0:T(8,128)(2,1)S(1)} %broadcast_in_dim.82), channel_id=1, replica_groups=mesh['dp'=16,'section'=2,'tensor'=8] {'dp'}, dimensions={0} | all-to-all | bytes 4194304 | tf_op jit(solution)/shard_map/all_to_all | solution.py:56
  299.2 5.9 %fusion.27 = bf16[1024,1024]{1,0:T(8,128)(2,1)} fusion(bf16[1024,1024]{1,0:T(8,128)(2,1)S(1)} %bitcast.113, bf16[1024,1024]{1,0:T(8,128)(2,1)} %collective-permute-done.2, pred[]{:T(512)S(6)} %eq.59, bf16[1,1024,1024]{2,1,0:T(8,128)(2,1)} %param.13), kind=kOutput, calls=%fused_computation.37 | convolution fusion | flops 2149580800 | bytes 8388609 | tf_op jit(solution)/shard_map/dot_general | solution.py:96
  305.1 77.9 %all-reduce.5.cloned.1.call-done = bf16[1024,1024]{1,0:T(8,128)(2,1)} async-done(((bf16[1024,1024]{1,0:T(8,128)(2,1)}), bf16[1024,1024]{1,0:T(8,128)(2,1)}) %all-reduce.5.cloned.1.call-update) | async-done | bytes 2097168 | tf_op jit(solution)/shard_map/psum | solution.py:99
  383.0 5.0 %fusion.5 = bf16[1024,1024]{1,0:T(8,128)(2,1)} fusion(bf16[1024,1024]{1,0:T(8,128)(2,1)} %all-reduce.5.cloned.1.call-done, bf16[1024,1024]{1,0:T(8,128)(2,1)} %all-reduce.3.cloned.1.call-done, bf16[1024,1024]{1,0:T(8,128)(2,1)S(1)} %get-tuple-element.30), kind=kLoop, calls=%fused_computation.15 | loop fusion | flops 8388608 | bytes 8388608 | tf_op jit(solution)/shard_map/convert_element_type | solution.py:100
  (50 shorter events, 1.4 us)
Async XLA Ops:
  9.8 7.8 %copy-start.1 = (bf16[1,1024,1024]{2,1,0:T(8,128)(2,1)S(1)}, bf16[1,1024,1024]{2,1,0:T(8,128)(2,1)}, u32[]{:S(2)}) copy-start(bf16[1,1024,1024]{2,1,0:T(8,128)(2,1)} %param.11) | copy-start | bytes 6291460
  9.8 7.8 %copy-start.5 = (bf16[1,1024,1,256]{3,1,2,0:T(8,128)(2,1)S(1)}, bf16[1,1024,1,256]{3,1,2,0:T(8,128)(2,1)}, u32[]{:S(2)}) copy-start(bf16[1,1024,1,256]{3,1,2,0:T(8,128)(2,1)} %param.12) | copy-start | bytes 1572868
  9.8 35.0 %all-to-all-start = ((bf16[64,16,1024]{2,0,1:T(8,128)(2,1)}), bf16[64,16,1024]{2,0,1:T(8,128)(2,1)}, u32[]{:S(2)}, u32[]{:S(2)}) async-start(bf16[64,16,1024]{2,0,1:T(8,128)(2,1)} %bitcast.104), calls=%async_computation | async-start | bytes 4194304 | tf_op jit(solution)/shard_map/all_to_all | solution.py:122
  17.6 27.2 %copy-start.7 = (f32[1,1024]{1,0:T(1,128)S(1)}, f32[1,1024]{1,0:T(1,128)}, u32[]{:S(2)}) copy-start(f32[1,1024]{1,0:T(1,128)} %param.10) | copy-start | bytes 12292
  17.6 28.6 %copy-start.6 = (s32[2048]{0:T(1024)S(1)}, s32[2048]{0:T(1024)}, u32[]{:S(2)}) copy-start(s32[2048]{0:T(1024)} %param.8) | copy-start | bytes 24580
  17.6 209.2 %all-reduce.3.cloned.1.call-start = ((), (), s32[]{:S(2)}) async-start(), calls=%async_computation.5 | async-start | bytes 4194304 | tf_op jit(solution)/shard_map/psum | solution.py:99
  19.9 29.4 %collective-permute-start.1 = (bf16[1024,1408]{1,0:T(8,128)(2,1)}, bf16[1024,1408]{1,0:T(8,128)(2,1)}, u32[]{:S(2)}, u32[]{:S(2)}) collective-permute-start(bf16[1024,1408]{1,0:T(8,128)(2,1)} %maximum_maximum_fusion), channel_id=1, source_target_pairs={{0,8},{8,0},{1,9},{9,1},{2,10},{10,2},{3,11},{11,3},{4,12},{12,4},... | collective-permute-start | bytes 8650760 | tf_op jit(solution)/shard_map/ppermute | solution.py:118
  19.9 29.4 %collective-permute-start.2 = (bf16[1024,1024]{1,0:T(8,128)(2,1)}, bf16[1024,1024]{1,0:T(8,128)(2,1)}, u32[]{:S(2)}, u32[]{:S(2)}) collective-permute-start(bf16[1024,1024]{1,0:T(8,128)(2,1)} %bitcast.3), channel_id=1, source_target_pairs={{0,8},{8,0},{1,9},{9,1},{2,10},{10,2},{3,11},{11,3},{4,12},{12,4},... | collective-permute-start | bytes 6291464 | tf_op jit(solution)/shard_map/ppermute | solution.py:118
  44.8 4.5 %collective-permute-start.3 = (bf16[1024,1024]{1,0:T(8,128)(2,1)}, bf16[1024,1024]{1,0:T(8,128)(2,1)}, u32[]{:S(2)}, u32[]{:S(2)}) collective-permute-start(bf16[1024,1024]{1,0:T(8,128)(2,1)} %bitcast.6), channel_id=1, source_target_pairs={{0,8},{8,0},{1,9},{9,1},{2,10},{10,2},{3,11},{11,3},{4,12},{12,4},... | collective-permute-start | bytes 6291464 | tf_op jit(solution)/shard_map/ppermute | solution.py:125
  44.8 4.5 %collective-permute-start = (f32[1024]{0:T(1024)S(1)}, f32[1024]{0:T(1024)S(1)}, u32[]{:S(2)}, u32[]{:S(2)}) collective-permute-start(f32[1024]{0:T(1024)S(1)} %bitcast.128), channel_id=1, source_target_pairs={{0,8},{8,0},{1,9},{9,1},{2,10},{10,2},{3,11},{11,3},{4,12},{12,4},... | collective-permute-start | bytes 12296 | tf_op jit(solution)/shard_map/ppermute | solution.py:118
  49.3 4.1 %copy-start.4 = (bf16[1024,1024]{1,0:T(8,128)(2,1)S(1)}, bf16[1024,1024]{1,0:T(8,128)(2,1)}, u32[]{:S(2)}) copy-start(bf16[1024,1024]{1,0:T(8,128)(2,1)} %get-tuple-element.12) | copy-start | bytes 6291460
  53.4 4.2 %copy-start.2 = (bf16[1,1024,1024]{2,1,0:T(8,128)(2,1)S(1)}, bf16[1,1024,1024]{2,1,0:T(8,128)(2,1)}, u32[]{:S(2)}) copy-start(bf16[1,1024,1024]{2,1,0:T(8,128)(2,1)} %param.11) | copy-start | bytes 6291460
  144.6 238.4 %all-reduce.5.cloned.1.call-start = ((), (), s32[]{:S(2)}) async-start(), calls=%async_computation.6 | async-start | bytes 4194304 | tf_op jit(solution)/shard_map/psum | solution.py:99
  226.8 2.5 copy-start
  226.8 2.9 copy-start.3
Sparse Core Ops, SparseCore 0:
  144.7 82.0 all-reduce.2
  305.2 77.7 all-reduce.4

commit v11 on v8

--- a/solution.py
+++ b/solution.py
@@ -130,9 +130,7 @@
         section_index * rows_here + lax.axis_index("dp") * own_blocks * MICRO_TOKENS,
         own_blocks * MICRO_TOKENS,
     ).reshape(own_blocks, MICRO_TOKENS)
-    other, received, own_allowed = lax.optimization_barrier(
-        (other, received, block_mask(own_segments))
-    )
+    other, own_allowed = lax.optimization_barrier((other, block_mask(own_segments)))
     my_order = lax.dynamic_slice_in_dim(order, section_index * rows_here, rows_here)
     source_group = my_order // entry_rows
     within = my_order % entry_rows

time: 393 us -> 393 us (level)
  no operation moved by 1% of the time
where the time goes in v11:
time: 393 us
  waiting for transfers between devices  185 us (47%)
  blocking collectives  139 us (35%)
  matrix products  30.1 us (8%)
  between operations  13.7 us (3%)
  other arithmetic  11.2 us (3%)
  starting transfers between devices  8.84 us (2%)
  local copies, waits for them, and re-layouts  5.23 us (1%)
    psum x2, waiting for transfers between devices, section_layer(): lax.psum(head_terms.astype(jnp.bfloat16), 'tensor').astype(jnp.float32)  160 us
    all_to_all x2, blocking collectives, section_layer(): lax.all_to_all(payload.reshape(group_count, own_rows, payload.shape[1]),...  81.3 us
    all_to_all x2, blocking collectives, gathered_over(): lax.all_to_all(spread, axis, 0, 0, tiled=False)  57.7 us
    all_to_all x1, waiting for transfers between devices, on_device(): lax.all_to_all(my_rows.reshape(part_rows, group_count, model_width // gro...  24.4 us
    dot_general x2, matrix products, section_layer(): jnp.dot(gathered_over(attended_rows, 'dp'), out_weight, preferred_element...  11.2 us
    dot_general x2, matrix products, section_layer(): jnp.dot(normed_rows, joined_weight, preferred_element_type=jnp.float32)  8.97 us
  transfers between devices with their start and end apart: 7, of which 3 were waited for; matrix products, arithmetic and copies ran while one was open for 2% of the time, Pallas kernels for 0%

profile of v11, /device:TPU:2, one launch (start us, length us, event | category | flops | bytes accessed | tf_op | source)
XLA Modules:
  0.0 392.8 jit_solution(10873524358296757689)
XLA Ops:
  6.5 1.7 constant_dynamic-slice_fusion
  8.3 1.6 copy.54
  9.8 7.7 %all-to-all-start = ((bf16[64,16,1024]{2,0,1:T(8,128)(2,1)}), bf16[64,16,1024]{2,0,1:T(8,128)(2,1)}, u32[]{:S(2)}, u32[]{:S(2)}) async-start(bf16[64,16,1024]{2,0,1:T(8,128)(2,1)} %bitcast.102), calls=%async_computation | async-start | bytes 4194304 | tf_op jit(solution)/shard_map/all_to_all | solution.py:122
  17.7 2.2 maximum_maximum_fusion
  19.9 0.5 collective-permute-start.3
  20.4 24.4 %all-to-all-done = bf16[64,16,1024]{2,0,1:T(8,128)(2,1)} async-done(((bf16[64,16,1024]{2,0,1:T(8,128)(2,1)}), bf16[64,16,1024]{2,0,1:T(8,128)(2,1)}, u32[]{:S(2)}, u32[]{:S(2)}) %all-to-all-start) | async-done | bytes 2097184 | tf_op jit(solution)/shard_map/all_to_all | solution.py:122
  44.8 0.5 collective-permute-start.1
  45.3 0.8 dynamic_slice.11
  46.3 4.0 %fusion.8 = f32[1024,1024]{1,0:T(8,128)S(1)} fusion(bf16[1024,1024]{1,0:T(8,128)(2,1)} %bitcast.2, s32[1024]{0:T(1024)S(1)} %fusion.61, pred[1024]{0:T(1024)(128)(4,1)S(1)} %get-tuple-element.13), kind=kOutput, calls=%fused_computation.20 | convolution fusion | flops 2149580800 | bytes 6296576 | tf_op jit(solution)/shard_map/dot_general | solution.py:143
  50.4 4.9 %fusion = (f32[1024]{0:T(1024)S(1)}, bf16[1024,1024]{1,0:T(8,128)(2,1)S(1)}) fusion(f32[1024,1024]{1,0:T(8,128)S(1)} %fusion.8, bf16[1024,1024]{1,0:T(8,128)(2,1)} %collective-permute-done, s32[1024]{0:T(1024)S(1)} %fusion.61, pred[1024]{0:T(1024)(128)(4,1)S(1)} %get-tuple-element.14), kind=kOutput, calls=%fused_computation.10 | convolution fusion | flops 2154822656 | bytes 8397824 | tf_op jit(solution)/shard_map/dot_general | solution.py:144
  55.3 3.6 select_convert_fusion.1
  58.8 44.4 %all_to_all.35 = bf16[16,64,1408]{2,1,0:T(8,128)(2,1)S(1)} all-to-all(bf16[16,64,1408]{2,1,0:T(8,128)(2,1)S(1)} %bitcast.107), channel_id=1, replica_groups=mesh['dp'=16,'section'=2,'tensor'=8] {'dp'}, dimensions={0} | all-to-all | bytes 5767168 | tf_op jit(solution)/shard_map/all_to_all | solution.py:80
  103.2 0.4 convert_reduce_fusion.1
  104.0 0.3 fusion.73
  104.3 0.2 fusion.44
  104.7 0.3 broadcast_in_dim.78
  104.9 32.2 %all_to_all.36 = bf16[16,64,1024]{2,1,0:T(8,128)(2,1)S(1)} all-to-all(bf16[16,64,1024]{2,1,0:T(8,128)(2,1)S(1)} %broadcast_in_dim.78), channel_id=1, replica_groups=mesh['dp'=16,'section'=2,'tensor'=8] {'dp'}, dimensions={0} | all-to-all | bytes 4194304 | tf_op jit(solution)/shard_map/all_to_all | solution.py:56
  137.1 5.3 %fusion.30 = bf16[1024,1024]{1,0:T(8,128)(2,1)} fusion(bf16[1024,1024]{1,0:T(8,128)(2,1)S(1)} %bitcast.112, bf16[1024,1024]{1,0:T(8,128)(2,1)} %collective-permute-done.3, pred[]{:T(512)S(6)} %eq.54, bf16[1,1024,1024]{2,1,0:T(8,128)(2,1)} %param.13), kind=kOutput, calls=%fused_computation.40 | convolution fusion | flops 2149580800 | bytes 8388609 | tf_op jit(solution)/shard_map/dot_general | solution.py:96
  142.4 82.2 %all-reduce.3.cloned.1.call-done = bf16[1024,1024]{1,0:T(8,128)(2,1)} async-done(((bf16[1024,1024]{1,0:T(8,128)(2,1)}), bf16[1024,1024]{1,0:T(8,128)(2,1)}) %all-reduce.3.cloned.1.call-update) | async-done | bytes 2097168 | tf_op jit(solution)/shard_map/psum | solution.py:99
  224.6 2.5 fusion.3
  227.1 0.3 copy-done.3
  227.5 5.4 %select_convert_fusion = bf16[1024,1408]{1,0:T(8,128)(2,1)S(1)} fusion(bf16[1024,1408]{1,0:T(8,128)(2,1)} %collective-permute-done.2, bf16[1024]{0:T(1024)(128)(2,1)S(1)} %get-tuple-element.18, bf16[1024]{0:T(1024)(128)(2,1)S(1)} %get-tuple-element.17, pred[]{:T(512)S(6)} %eq.59, pred[1408]{0:T(1024)(128)(4,1)S(1)} %get-tuple-element.27, ...), kind=kOutput, calls=%fused_computation.7 | convolution fusion | flops 2973106176 | bytes 12596737 | tf_op jit(solution)/shard_map/dot_general | solution.py:67
  232.9 37.0 %all_to_all.37 = bf16[16,64,1408]{2,1,0:T(8,128)(2,1)S(1)} all-to-all(bf16[16,64,1408]{2,1,0:T(8,128)(2,1)S(1)} %bitcast.106), channel_id=1, replica_groups=mesh['dp'=16,'section'=2,'tensor'=8] {'dp'}, dimensions={0} | all-to-all | bytes 5767168 | tf_op jit(solution)/shard_map/all_to_all | solution.py:80
  269.9 0.4 convert_reduce_fusion
  270.3 0.2 fusion.55
  270.6 0.3 fusion.74
  270.9 0.2 fusion.45
  271.3 0.3 broadcast_in_dim.82
  271.5 25.5 %all_to_all.38 = bf16[16,64,1024]{2,1,0:T(8,128)(2,1)S(1)} all-to-all(bf16[16,64,1024]{2,1,0:T(8,128)(2,1)S(1)} %broadcast_in_dim.82), channel_id=1, replica_groups=mesh['dp'=16,'section'=2,'tensor'=8] {'dp'}, dimensions={0} | all-to-all | bytes 4194304 | tf_op jit(solution)/shard_map/all_to_all | solution.py:56
  297.1 5.9 %fusion.33 = bf16[1024,1024]{1,0:T(8,128)(2,1)} fusion(bf16[1024,1024]{1,0:T(8,128)(2,1)S(1)} %bitcast.111, bf16[1024,1024]{1,0:T(8,128)(2,1)} %collective-permute-done.3, pred[]{:T(512)S(6)} %eq.59, bf16[1,1024,1024]{2,1,0:T(8,128)(2,1)} %param.13), kind=kOutput, calls=%fused_computation.41 | convolution fusion | flops 2149580800 | bytes 8388609 | tf_op jit(solution)/shard_map/dot_general | solution.py:96
  303.0 78.0 %all-reduce.5.cloned.1.call-done = bf16[1024,1024]{1,0:T(8,128)(2,1)} async-done(((bf16[1024,1024]{1,0:T(8,128)(2,1)}), bf16[1024,1024]{1,0:T(8,128)(2,1)}) %all-reduce.5.cloned.1.call-update) | async-done | bytes 2097168 | tf_op jit(solution)/shard_map/psum | solution.py:99
  381.0 5.0 %fusion.5 = bf16[1024,1024]{1,0:T(8,128)(2,1)} fusion(bf16[1024,1024]{1,0:T(8,128)(2,1)} %all-reduce.5.cloned.1.call-done, bf16[1024,1024]{1,0:T(8,128)(2,1)} %all-reduce.3.cloned.1.call-done, bf16[1024,1024]{1,0:T(8,128)(2,1)S(1)} %get-tuple-element.22), kind=kLoop, calls=%fused_computation.15 | loop fusion | flops 8388608 | bytes 8388608 | tf_op jit(solution)/shard_map/convert_element_type | solution.py:100
  (47 shorter events, 1.0 us)
Async XLA Ops:
  9.8 7.8 %copy-start.1 = (bf16[1,1024,1024]{2,1,0:T(8,128)(2,1)S(1)}, bf16[1,1024,1024]{2,1,0:T(8,128)(2,1)}, u32[]{:S(2)}) copy-start(bf16[1,1024,1024]{2,1,0:T(8,128)(2,1)} %param.11) | copy-start | bytes 6291460
  9.8 7.8 %copy-start.4 = (bf16[1,1024,1,256]{3,1,2,0:T(8,128)(2,1)S(1)}, bf16[1,1024,1,256]{3,1,2,0:T(8,128)(2,1)}, u32[]{:S(2)}) copy-start(bf16[1,1024,1,256]{3,1,2,0:T(8,128)(2,1)} %param.12) | copy-start | bytes 1572868
  9.8 35.0 %all-to-all-start = ((bf16[64,16,1024]{2,0,1:T(8,128)(2,1)}), bf16[64,16,1024]{2,0,1:T(8,128)(2,1)}, u32[]{:S(2)}, u32[]{:S(2)}) async-start(bf16[64,16,1024]{2,0,1:T(8,128)(2,1)} %bitcast.102), calls=%async_computation | async-start | bytes 4194304 | tf_op jit(solution)/shard_map/all_to_all | solution.py:122
  17.6 27.2 %copy-start.6 = (f32[1,1024]{1,0:T(1,128)S(1)}, f32[1,1024]{1,0:T(1,128)}, u32[]{:S(2)}) copy-start(f32[1,1024]{1,0:T(1,128)} %param.10) | copy-start | bytes 12292
  17.6 28.6 %copy-start.5 = (s32[2048]{0:T(1024)S(1)}, s32[2048]{0:T(1024)}, u32[]{:S(2)}) copy-start(s32[2048]{0:T(1024)} %param.8) | copy-start | bytes 24580
  17.6 207.0 %all-reduce.3.cloned.1.call-start = ((), (), s32[]{:S(2)}) async-start(), calls=%async_computation.5 | async-start | bytes 4194304 | tf_op jit(solution)/shard_map/psum | solution.py:99
  19.9 30.4 %collective-permute-start.2 = (bf16[1024,1408]{1,0:T(8,128)(2,1)}, bf16[1024,1408]{1,0:T(8,128)(2,1)}, u32[]{:S(2)}, u32[]{:S(2)}) collective-permute-start(bf16[1024,1408]{1,0:T(8,128)(2,1)} %maximum_maximum_fusion), channel_id=1, source_target_pairs={{0,8},{8,0},{1,9},{9,1},{2,10},{10,2},{3,11},{11,3},{4,12},{12,4},... | collective-permute-start | bytes 8650760 | tf_op jit(solution)/shard_map/ppermute | solution.py:118
  19.9 30.4 %collective-permute-start.3 = (bf16[1024,1024]{1,0:T(8,128)(2,1)}, bf16[1024,1024]{1,0:T(8,128)(2,1)}, u32[]{:S(2)}, u32[]{:S(2)}) collective-permute-start(bf16[1024,1024]{1,0:T(8,128)(2,1)} %bitcast.8), channel_id=1, source_target_pairs={{0,8},{8,0},{1,9},{9,1},{2,10},{10,2},{3,11},{11,3},{4,12},{12,4},... | collective-permute-start | bytes 6291464 | tf_op jit(solution)/shard_map/ppermute | solution.py:118
  44.8 5.5 %collective-permute-start = (bf16[1024,1024]{1,0:T(8,128)(2,1)}, bf16[1024,1024]{1,0:T(8,128)(2,1)}, u32[]{:S(2)}, u32[]{:S(2)}) collective-permute-start(bf16[1024,1024]{1,0:T(8,128)(2,1)} %bitcast.2), channel_id=1, source_target_pairs={{0,8},{8,0},{1,9},{9,1},{2,10},{10,2},{3,11},{11,3},{4,12},{12,4},... | collective-permute-start | bytes 6291464 | tf_op jit(solution)/shard_map/ppermute | solution.py:125
  44.8 5.5 %collective-permute-start.1 = (f32[1024]{0:T(1024)S(1)}, f32[1024]{0:T(1024)S(1)}, u32[]{:S(2)}, u32[]{:S(2)}) collective-permute-start(f32[1024]{0:T(1024)S(1)} %bitcast.126), channel_id=1, source_target_pairs={{0,8},{8,0},{1,9},{9,1},{2,10},{10,2},{3,11},{11,3},{4,12},{12,4},... | collective-permute-start | bytes 12296 | tf_op jit(solution)/shard_map/ppermute | solution.py:118
  50.4 4.9 %copy-start.2 = (bf16[1,1024,1024]{2,1,0:T(8,128)(2,1)S(1)}, bf16[1,1024,1024]{2,1,0:T(8,128)(2,1)}, u32[]{:S(2)}) copy-start(bf16[1,1024,1024]{2,1,0:T(8,128)(2,1)} %param.11) | copy-start | bytes 6291460
  142.4 238.6 %all-reduce.5.cloned.1.call-start = ((), (), s32[]{:S(2)}) async-start(), calls=%async_computation.6 | async-start | bytes 4194304 | tf_op jit(solution)/shard_map/psum | solution.py:99
  224.6 2.5 copy-start
  224.6 2.9 copy-start.3
Sparse Core Ops, SparseCore 0:
  142.5 82.0 all-reduce.2
  303.1 77.8 all-reduce.4
